TPU v7x, 128 devices: a whole 4x4x4 slice. The times are simulated.
128 devices in a mesh: dp: 16 (over z, y_lo, core), land: 8 (over x, y_hi).
Axes of the slice: x: 4, y: 4 (y_hi: 2, y_lo: 2; y = y_hi * 2 + y_lo), z: 4, core: 2. Of those that a mesh axis runs over, the one named last changes fastest.
Arguments:
- doc_values: bfloat16 [24576, 1024], P('dp'), may hold values from 0 to 100
- doc_blocks: int32 [192, 8], P('dp'), may hold values from 0 to 511, as said below
- land_values: bfloat16 [16384, 1024], P(('dp', 'land')), may hold values from 0 to 100
- land_blocks: int32 [128, 8], replicated, may hold values from 0 to 511, as said below
- coefficients: bfloat16 [16384, 64], P(('dp', 'land')), may hold values from -12 to 12
Outputs:
- normal_product: float32 [16384, 64], P(('dp', 'land'))
Inputs may be any that keep to these rules, and one draw needn't show every extreme that they name: `doc_blocks`: each row lists 8 different vocabulary block numbers. `land_blocks`: each row lists 8 different vocabulary block numbers.
All inputs are finite; a program needn't handle non-finite values.
Results may differ from a plain program's by a relative error of at most 0.0003.
Values may be sent and summed in bfloat16 or wider, within the bound.
No kernel may reach another device: no remote copies, remote signals or barrier semaphores. Data moves between devices by JAX's collectives and lax.ppermute only.
A program may use at most 64 MiB of HBM per device.

v0:
```python
import jax
import jax.numpy as jnp
from jax import lax
from jax.sharding import PartitionSpec as P

TERM_BLOCK = 128
ACTIVE = 8
LAND_ACTIVE = 8
DOC_BLOCK = 128
LM_BLOCK = 128


sharpness = 2.0


def split_pair(values):
    high = lax.optimization_barrier(values.astype(jnp.bfloat16))
    low = (values - high.astype(jnp.float32)).astype(jnp.bfloat16)
    return (high, low)


def kernel_tiles(doc_grid, doc_blocks, doc_norm, land_rows, land_ids):
    block_count = land_ids.shape[0]
    land_norm = lax.rsqrt(jnp.sum(jnp.square(land_rows.astype(jnp.float32)), axis=1) + 1e-06)
    land_grid = land_rows.reshape(block_count, LM_BLOCK, LAND_ACTIVE, TERM_BLOCK)
    norm_grid = land_norm.reshape(block_count, LM_BLOCK)

    def one_block(packed):
        tile_grid, tile_ids, tile_norms = packed
        matches = (doc_blocks[:, :, None] == tile_ids[None, None, :]).astype(jnp.bfloat16)
        aligned = jnp.einsum(
            "dab,lbt->dlat", matches, tile_grid, preferred_element_type=jnp.float32
        ).astype(jnp.bfloat16)
        aligned = aligned.reshape(matches.shape[0], LM_BLOCK, ACTIVE * TERM_BLOCK)
        inner_terms = jnp.einsum(
            "drw,dlw->drl", doc_grid, aligned, preferred_element_type=jnp.float32
        )
        inner_terms = inner_terms.reshape(-1, LM_BLOCK)
        cosine = inner_terms * doc_norm[:, None] * tile_norms[None, :]
        return split_pair(jnp.exp(2.0 * sharpness * (cosine - 1.0)))

    return lax.map(one_block, (land_grid, land_ids, norm_grid))


def on_device(doc_values, doc_blocks, land_values, land_blocks, coefficients):
    dp_count = lax.axis_size("dp")
    land_count = lax.axis_size("land")
    doc_rows = doc_values.shape[0]
    targets = coefficients.shape[1]
    total_docs = doc_rows * dp_count
    own_blocks = land_values.shape[0] // LM_BLOCK
    doc_norm = lax.rsqrt(jnp.sum(jnp.square(doc_values.astype(jnp.float32)), axis=1) + 1e-06)
    doc_grid = doc_values.reshape(doc_rows // DOC_BLOCK, DOC_BLOCK, ACTIVE * TERM_BLOCK)
    table = land_blocks.reshape(dp_count, land_count, own_blocks, LAND_ACTIVE)
    own_table = lax.dynamic_index_in_dim(table, lax.axis_index("land"), axis=1, keepdims=False)
    own_table = own_table.reshape(dp_count * own_blocks, LAND_ACTIVE)
    land_rows = lax.all_gather(land_values, "dp", axis=0, tiled=True)
    coef_rows = lax.all_gather(coefficients, "dp", axis=0, tiled=True)
    tile_high, tile_low = kernel_tiles(doc_grid, doc_blocks, doc_norm, land_rows, own_table)
    coef_grid = coef_rows.reshape(tile_high.shape[0], LM_BLOCK, -1)
    part_one = jnp.einsum("qnl,qlt->nt", tile_high, coef_grid, preferred_element_type=jnp.float32)
    fitted = part_one + jnp.einsum(
        "qnl,qlt->nt", tile_low, coef_grid, preferred_element_type=jnp.float32
    )
    absorb_high_all = tile_high
    absorb_low_all = tile_low
    folded = (fitted, absorb_high_all, absorb_low_all)
    fitted = folded[0]
    fitted = lax.psum(fitted, "land")
    fitted_high, fitted_low = split_pair(fitted)
    fitted_pair = jnp.concatenate([fitted_high, fitted_low], axis=1)
    high_all = folded[1]
    low_all = folded[2]
    tile_high = high_all
    tile_low = low_all
    summed = jnp.einsum("qnl,nt->qlt", tile_high, fitted_pair, preferred_element_type=jnp.float32)
    summed = summed + jnp.einsum(
        "qnl,nt->qlt", tile_low, fitted_pair, preferred_element_type=jnp.float32
    )
    summed = summed[:, :, :targets] + summed[:, :, targets:]
    result = lax.psum_scatter(summed.reshape(-1, targets), "dp", scatter_dimension=0, tiled=True)
    return result / total_docs


def solution(mesh):
    placed = (P("dp", None), P("dp", None), P(("dp", "land"), None), P(), P(("dp", "land"), None))
    return jax.shard_map(
        on_device, mesh=mesh, in_specs=placed, out_specs=P(("dp", "land"), None), check_vma=False
    )
```

profile of v0, /device:TPU:1, one launch (start us, length us, event | category | flops | bytes accessed | tf_op | source)
XLA Modules:
  0.0 483.8 jit_solution(7076118365409632704)
XLA Ops:
  8.4 24.4 %all_gather.7 = bf16[2048,64]{0,1:T(8,128)(2,1)S(1)} all-gather(bf16[128,64]{0,1:T(8,128)(2,1)} %param.11), channel_id=1, replica_groups=mesh['dp'=16,'land'=8] {'dp'}, dimensions={0}, use_global_device_ids=true | all-gather | bytes 278528 | tf_op jit(solution)/shard_map/all_gather | solution.py:58
  35.4 14.6 %all-gather.2.cloned.1.call-done = bf16[2048,1024]{1,0:T(8,128)(2,1)} async-done(((bf16[128,1024]{1,0:T(8,128)(2,1)}), bf16[2048,1024]{1,0:T(8,128)(2,1)}) %all-gather.2.cloned.1.call-update) | async-done | bytes 4194320 | tf_op jit(solution)/shard_map/all_gather | solution.py:57
  50.0 5.4 %copy.24 = bf16[256,8,8,128]{3,2,1,0:T(8,128)(2,1)} copy(bf16[256,8,8,128]{3,1,2,0:T(8,128)(2,1)} %bitcast.102) | data formatting | bytes 8388608
  56.3 262.2 %while.14 = (s32[]{:T(128)}, bf16[16,1536,128]{2,1,0:T(8,128)(2,1)}, bf16[16,1536,128]{2,1,0:T(8,128)(2,1)}, bf16[16,128,8,128]{3,2,1,0:T(8,128)(2,1)}, s32[12,8...) while((s32[]{:T(128)}, ...), condition=%wide.region_3.4_spmd, body=%wide.region_2.3_spmd.sunk | while | flops 431751936 | bytes 19938892 | solution.py:42
  56.4 4.3 convert_bitcast_fusion.2
  60.6 7.8 %copy.35 = bf16[12,128,8,128]{1,3,2,0:T(8,128)(2,1)S(1)} copy(bf16[12,128,8,128]{3,0,2,1:T(8,128)(2,1)} %convert_bitcast_fusion.2) | data formatting | bytes 6291456 | tf_op jit(solution)/shard_map/while/body/eval_jaxpr/convert_element_type | solution.py:33
  77.0 7.8 %copy.35 = bf16[12,128,8,128]{1,3,2,0:T(8,128)(2,1)S(1)} copy(bf16[12,128,8,128]{3,0,2,1:T(8,128)(2,1)} %convert_bitcast_fusion.2) | data formatting | bytes 6291456 | tf_op jit(solution)/shard_map/while/body/eval_jaxpr/convert_element_type | solution.py:33
  89.1 4.2 convert_bitcast_fusion.2
  93.4 7.8 %copy.35 = bf16[12,128,8,128]{1,3,2,0:T(8,128)(2,1)S(1)} copy(bf16[12,128,8,128]{3,0,2,1:T(8,128)(2,1)} %convert_bitcast_fusion.2) | data formatting | bytes 6291456 | tf_op jit(solution)/shard_map/while/body/eval_jaxpr/convert_element_type | solution.py:33
  105.5 4.2 convert_bitcast_fusion.2
  109.8 7.8 %copy.35 = bf16[12,128,8,128]{1,3,2,0:T(8,128)(2,1)S(1)} copy(bf16[12,128,8,128]{3,0,2,1:T(8,128)(2,1)} %convert_bitcast_fusion.2) | data formatting | bytes 6291456 | tf_op jit(solution)/shard_map/while/body/eval_jaxpr/convert_element_type | solution.py:33
  121.9 4.2 convert_bitcast_fusion.2
  126.1 7.8 %copy.35 = bf16[12,128,8,128]{1,3,2,0:T(8,128)(2,1)S(1)} copy(bf16[12,128,8,128]{3,0,2,1:T(8,128)(2,1)} %convert_bitcast_fusion.2) | data formatting | bytes 6291456 | tf_op jit(solution)/shard_map/while/body/eval_jaxpr/convert_element_type | solution.py:33
  142.5 7.8 %copy.35 = bf16[12,128,8,128]{1,3,2,0:T(8,128)(2,1)S(1)} copy(bf16[12,128,8,128]{3,0,2,1:T(8,128)(2,1)} %convert_bitcast_fusion.2) | data formatting | bytes 6291456 | tf_op jit(solution)/shard_map/while/body/eval_jaxpr/convert_element_type | solution.py:33
  158.9 7.8 %copy.35 = bf16[12,128,8,128]{1,3,2,0:T(8,128)(2,1)S(1)} copy(bf16[12,128,8,128]{3,0,2,1:T(8,128)(2,1)} %convert_bitcast_fusion.2) | data formatting | bytes 6291456 | tf_op jit(solution)/shard_map/while/body/eval_jaxpr/convert_element_type | solution.py:33
  175.3 7.8 %copy.35 = bf16[12,128,8,128]{1,3,2,0:T(8,128)(2,1)S(1)} copy(bf16[12,128,8,128]{3,0,2,1:T(8,128)(2,1)} %convert_bitcast_fusion.2) | data formatting | bytes 6291456 | tf_op jit(solution)/shard_map/while/body/eval_jaxpr/convert_element_type | solution.py:33
  191.7 7.8 %copy.35 = bf16[12,128,8,128]{1,3,2,0:T(8,128)(2,1)S(1)} copy(bf16[12,128,8,128]{3,0,2,1:T(8,128)(2,1)} %convert_bitcast_fusion.2) | data formatting | bytes 6291456 | tf_op jit(solution)/shard_map/while/body/eval_jaxpr/convert_element_type | solution.py:33
  203.8 4.2 convert_bitcast_fusion.2
  208.0 7.8 %copy.35 = bf16[12,128,8,128]{1,3,2,0:T(8,128)(2,1)S(1)} copy(bf16[12,128,8,128]{3,0,2,1:T(8,128)(2,1)} %convert_bitcast_fusion.2) | data formatting | bytes 6291456 | tf_op jit(solution)/shard_map/while/body/eval_jaxpr/convert_element_type | solution.py:33
  220.2 4.2 convert_bitcast_fusion.2
  224.4 7.8 %copy.35 = bf16[12,128,8,128]{1,3,2,0:T(8,128)(2,1)S(1)} copy(bf16[12,128,8,128]{3,0,2,1:T(8,128)(2,1)} %convert_bitcast_fusion.2) | data formatting | bytes 6291456 | tf_op jit(solution)/shard_map/while/body/eval_jaxpr/convert_element_type | solution.py:33
  236.5 4.2 convert_bitcast_fusion.2
  240.8 7.8 %copy.35 = bf16[12,128,8,128]{1,3,2,0:T(8,128)(2,1)S(1)} copy(bf16[12,128,8,128]{3,0,2,1:T(8,128)(2,1)} %convert_bitcast_fusion.2) | data formatting | bytes 6291456 | tf_op jit(solution)/shard_map/while/body/eval_jaxpr/convert_element_type | solution.py:33
  252.9 4.2 convert_bitcast_fusion.2
  257.2 7.8 %copy.35 = bf16[12,128,8,128]{1,3,2,0:T(8,128)(2,1)S(1)} copy(bf16[12,128,8,128]{3,0,2,1:T(8,128)(2,1)} %convert_bitcast_fusion.2) | data formatting | bytes 6291456 | tf_op jit(solution)/shard_map/while/body/eval_jaxpr/convert_element_type | solution.py:33
  273.6 7.8 %copy.35 = bf16[12,128,8,128]{1,3,2,0:T(8,128)(2,1)S(1)} copy(bf16[12,128,8,128]{3,0,2,1:T(8,128)(2,1)} %convert_bitcast_fusion.2) | data formatting | bytes 6291456 | tf_op jit(solution)/shard_map/while/body/eval_jaxpr/convert_element_type | solution.py:33
  285.7 4.2 convert_bitcast_fusion.2
  290.0 7.8 %copy.35 = bf16[12,128,8,128]{1,3,2,0:T(8,128)(2,1)S(1)} copy(bf16[12,128,8,128]{3,0,2,1:T(8,128)(2,1)} %convert_bitcast_fusion.2) | data formatting | bytes 6291456 | tf_op jit(solution)/shard_map/while/body/eval_jaxpr/convert_element_type | solution.py:33
  306.4 7.8 %copy.35 = bf16[12,128,8,128]{1,3,2,0:T(8,128)(2,1)S(1)} copy(bf16[12,128,8,128]{3,0,2,1:T(8,128)(2,1)} %convert_bitcast_fusion.2) | data formatting | bytes 6291456 | tf_op jit(solution)/shard_map/while/body/eval_jaxpr/convert_element_type | solution.py:33
  318.5 4.9 %convolution_bitcast_fusion.1 = f32[1536,64]{0,1:T(8,128)S(1)} fusion(bf16[16,1536,128]{2,1,0:T(8,128)(2,1)} %get-tuple-element.119, bf16[2048,64]{0,1:T(8,128)(2,1)S(1)} %all_gather.7), kind=kOutput, calls=%fused_computation.25 | convolution fusion | flops 402653184 | bytes 6946816 | tf_op jit(solution)/shard_map/qnl,qlt->nt/dot_general | solution.py:61
  326.4 80.3 %all-reduce.2.cloned.1.call-done = f32[1536,64]{0,1:T(8,128)} async-done(((f32[1536,64]{0,1:T(8,128)}), f32[1536,64]{0,1:T(8,128)}) %all-reduce.2.cloned.1.call-update) | async-done | bytes 393232 | tf_op jit(solution)/shard_map/psum | solution.py:69
  414.7 61.2 %reduce-scatter.2.cloned.1.call-done = f32[128,64]{0,1:T(8,128)} async-done(((f32[2048,64]{0,1:T(8,128)}), f32[128,64]{0,1:T(8,128)}) %reduce-scatter.2.cloned.1.call-update) | async-done | bytes 32784 | tf_op jit(solution)/shard_map/reduce_scatter | solution.py:81
  (120 shorter events, 116.9 us)
Async XLA Ops:
  6.5 43.5 %all-gather.2.cloned.1.call-start = ((), (), s32[]{:S(2)}) async-start(), calls=%async_computation.1 | async-start | bytes 4456448 | tf_op jit(solution)/shard_map/all_gather | solution.py:57
  7.3 399.4 %all-reduce.2.cloned.1.call-start = ((), (), s32[]{:S(2)}) async-start(), calls=%async_computation.2 | async-start | bytes 786432 | tf_op jit(solution)/shard_map/psum | solution.py:69
  50.0 5.4 %copy-start.1 = (bf16[2048,1024]{1,0:T(8,128)(2,1)S(1)}, bf16[2048,1024]{1,0:T(8,128)(2,1)}, u32[]{:S(2)}) copy-start(bf16[2048,1024]{1,0:T(8,128)(2,1)} %all-gather.2.cloned.1.call-done) | copy-start | bytes 12582916
  50.0 6.3 %copy-start.2 = (s32[12,8]{0,1:T(8,128)S(1)}, s32[12,8]{0,1:T(8,128)}, u32[]{:S(2)}) copy-start(s32[12,8]{0,1:T(8,128)} %param.8) | copy-start | bytes 1156
  318.5 4.9 %copy-start = (bf16[16,1536,128]{2,1,0:T(8,128)(2,1)S(1)}, bf16[16,1536,128]{2,1,0:T(8,128)(2,1)}, u32[]{:S(2)}) copy-start(bf16[16,1536,128]{2,1,0:T(8,128)(2,1)} %get-tuple-element.120) | copy-start | bytes 18874372
  323.5 89.4 %slice-start = ((s8[6291456]{0:T(1024)(128)(4,1)}), s8[2097152]{0:T(1024)(128)(4,1)S(1)}, s32[]{:S(2)}) async-start(s8[6291456]{0:T(1024)(128)(4,1)} %bitcast.100), calls=%async_computation.4 | async-start | bytes 4194304
  326.3 149.6 %reduce-scatter.2.cloned.1.call-start = ((), (), s32[]{:S(2)}) async-start(), calls=%async_computation.3 | async-start | bytes 557056 | tf_op jit(solution)/shard_map/reduce_scatter | solution.py:81
  407.7 5.2 %slice-start.1 = ((s8[6291456]{0:T(1024)(128)(4,1)}), s8[4194304]{0:T(1024)(128)(4,1)S(1)}, s32[]{:S(2)}) async-start(s8[6291456]{0:T(1024)(128)(4,1)} %bitcast.100), calls=%async_computation.5 | async-start | bytes 8388608
Sparse Core Ops, SparseCore 0:
  9.0 40.9 all-gather.1
  326.4 80.1 all-reduce.1
  414.8 60.9 reduce-scatter.1
where the time goes:
time: 489 us; the launch traced here: 484 us
  waiting for transfers between devices  157 us (32%)
  local copies, waits for them, and re-layouts  131 us (27%)
  matrix products  126 us (26%)
  other arithmetic  31.5 us (6%)
  blocking collectives  24.4 us (5%)
  between operations  13.2 us (3%)
    convert_element_type x16, local copies, waits for them, and re-layouts, one_block(): aligned = jnp.einsum('dab,lbt->dlat', matches, tile_grid, preferred_eleme...  124 us
    psum x1, waiting for transfers between devices, on_device(): fitted = lax.psum(fitted, 'land')  80.3 us
    dot_general x16, matrix products, one_block(): jnp.einsum('dab,lbt->dlat', matches, tile_grid, preferred_element_type=jn...  68 us
    reduce_scatter x1, waiting for transfers between devices, on_device(): lax.psum_scatter(summed.reshape(-1, targets), 'dp', scatter_dimension=0,...  61.2 us
    dot_general x16, matrix products, one_block(): jnp.einsum('drw,dlw->drl', doc_grid, aligned, preferred_element_type=jnp....  45.7 us
    all_gather x1, blocking collectives, on_device(): coef_rows = lax.all_gather(coefficients, 'dp', axis=0, tiled=True)  24.4 us
    dynamic_update_slice x16, other arithmetic, kernel_tiles(): return lax.map(one_block, (land_grid, land_ids, norm_grid))  19 us
    all_gather x1, waiting for transfers between devices, on_device(): land_rows = lax.all_gather(land_values, 'dp', axis=0, tiled=True)  14.6 us
  transfers between devices with their start and end apart: 3, of which 3 were waited for; matrix products, arithmetic and copies ran while one was open for 1% of the time, Pallas kernels for 0%

commit v1 on v0

v1 whole, which is shorter than its diff:
```python
import jax
import jax.numpy as jnp
from jax import lax
from jax.experimental import pallas as pl
from jax.experimental.pallas import tpu as pltpu
from jax.sharding import PartitionSpec as P

TERM_BLOCK = 128
ACTIVE = 8
LAND_ACTIVE = 8
DOC_BLOCK = 128
LM_BLOCK = 128


sharpness = 2.0


def split_pair(values):
    high = lax.optimization_barrier(values.astype(jnp.bfloat16))
    low = (values - high.astype(jnp.float32)).astype(jnp.bfloat16)
    return (high, low)


def match_table(doc_blocks, land_ids):
    eq = doc_blocks[None, :, :, None] == land_ids[:, None, None, :]
    has = jnp.any(eq, axis=2)
    first = jnp.argmax(eq, axis=2).astype(jnp.int32)
    return jnp.where(has, first, ACTIVE).astype(jnp.int32).reshape(-1)


def forward_kernel(slot_ref, doc_ref, dn_ref, land_ref, ln_ref, coef_ref,
                   high_ref, low_ref, fit_ref, aligned_ref):
    step = pl.program_id(0)
    doc_count = dn_ref.shape[0] // DOC_BLOCK

    @pl.when(step == 0)
    def _():
        fit_ref[...] = jnp.zeros_like(fit_ref)

    for d in range(doc_count):
        for b in range(LAND_ACTIVE):
            a = slot_ref[(step * doc_count + d) * LAND_ACTIVE + b]
            aligned_ref[d * DOC_BLOCK:(d + 1) * DOC_BLOCK, b * TERM_BLOCK:(b + 1) * TERM_BLOCK] = (
                doc_ref[d * (ACTIVE + 1) + a])
    inner = lax.dot_general(
        aligned_ref[...], land_ref[...], (((1,), (1,)), ((), ())),
        preferred_element_type=jnp.float32)
    cosine = inner * dn_ref[...] * ln_ref[0]
    kern = jnp.exp(2.0 * sharpness * (cosine - 1.0))
    high = kern.astype(jnp.bfloat16)
    low = (kern - high.astype(jnp.float32)).astype(jnp.bfloat16)
    high_ref[...] = high
    low_ref[...] = low
    coef = coef_ref[...]
    part = jnp.dot(high, coef, preferred_element_type=jnp.float32)
    part = part + jnp.dot(low, coef, preferred_element_type=jnp.float32)
    fit_ref[...] += part


def forward(slots, doc_tiles, doc_norm, land_rows, land_norm, coef_rows):
    doc_rows = doc_norm.shape[0]
    land_count = land_rows.shape[0]
    block_count = land_count // LM_BLOCK
    width = land_rows.shape[1]
    targets = coef_rows.shape[1]
    grid_spec = pltpu.PrefetchScalarGridSpec(
        num_scalar_prefetch=1,
        grid=(block_count,),
        in_specs=[
            pl.BlockSpec(doc_tiles.shape, lambda l, s: (0, 0, 0)),
            pl.BlockSpec((doc_rows, 1), lambda l, s: (0, 0)),
            pl.BlockSpec((LM_BLOCK, width), lambda l, s: (l, 0)),
            pl.BlockSpec((1, 1, LM_BLOCK), lambda l, s: (l, 0, 0)),
            pl.BlockSpec((LM_BLOCK, targets), lambda l, s: (l, 0)),
        ],
        out_specs=[
            pl.BlockSpec((doc_rows, LM_BLOCK), lambda l, s: (0, l)),
            pl.BlockSpec((doc_rows, LM_BLOCK), lambda l, s: (0, l)),
            pl.BlockSpec((doc_rows, targets), lambda l, s: (0, 0)),
        ],
        scratch_shapes=[pltpu.VMEM((doc_rows, width), jnp.bfloat16)],
    )
    return pl.pallas_call(
        forward_kernel,
        grid_spec=grid_spec,
        out_shape=[
            jax.ShapeDtypeStruct((doc_rows, land_count), jnp.bfloat16),
            jax.ShapeDtypeStruct((doc_rows, land_count), jnp.bfloat16),
            jax.ShapeDtypeStruct((doc_rows, targets), jnp.float32),
        ],
        compiler_params=pltpu.CompilerParams(
            dimension_semantics=("arbitrary",), vmem_limit_bytes=48 * 1024 * 1024),
    )(slots, doc_tiles, doc_norm, land_rows, land_norm.reshape(block_count, 1, LM_BLOCK), coef_rows)


def on_device(doc_values, doc_blocks, land_values, land_blocks, coefficients):
    dp_count = lax.axis_size("dp")
    land_count = lax.axis_size("land")
    doc_rows = doc_values.shape[0]
    targets = coefficients.shape[1]
    total_docs = doc_rows * dp_count
    own_blocks = land_values.shape[0] // LM_BLOCK
    doc_count = doc_rows // DOC_BLOCK
    doc_norm = lax.rsqrt(jnp.sum(jnp.square(doc_values.astype(jnp.float32)), axis=1) + 1e-06)
    land_norm = lax.rsqrt(jnp.sum(jnp.square(land_values.astype(jnp.float32)), axis=1) + 1e-06)
    table = land_blocks.reshape(dp_count, land_count, own_blocks, LAND_ACTIVE)
    own_table = lax.dynamic_index_in_dim(table, lax.axis_index("land"), axis=1, keepdims=False)
    own_table = own_table.reshape(dp_count * own_blocks, LAND_ACTIVE)
    land_rows = lax.all_gather(land_values, "dp", axis=0, tiled=True)
    coef_rows = lax.all_gather(coefficients, "dp", axis=0, tiled=True)
    norm_rows = lax.all_gather(land_norm, "dp", axis=0, tiled=True)
    doc_tiles = doc_values.reshape(doc_count, DOC_BLOCK, ACTIVE, TERM_BLOCK).transpose(0, 2, 1, 3)
    doc_tiles = jnp.pad(doc_tiles, ((0, 0), (0, 1), (0, 0), (0, 0)))
    doc_tiles = doc_tiles.reshape(doc_count * (ACTIVE + 1), DOC_BLOCK, TERM_BLOCK)
    slots = match_table(doc_blocks, own_table)
    tile_high, tile_low, fitted = forward(
        slots, doc_tiles, doc_norm.reshape(doc_rows, 1), land_rows, norm_rows, coef_rows)
    fitted = lax.psum(fitted, "land")
    fitted_high, fitted_low = split_pair(fitted)
    fitted_pair = jnp.concatenate([fitted_high, fitted_low], axis=1)
    summed = jnp.dot(tile_high.T, fitted_pair, preferred_element_type=jnp.float32)
    summed = summed + jnp.dot(tile_low.T, fitted_pair, preferred_element_type=jnp.float32)
    summed = summed[:, :targets] + summed[:, targets:]
    result = lax.psum_scatter(summed, "dp", scatter_dimension=0, tiled=True)
    return result / total_docs


def solution(mesh):
    placed = (P("dp", None), P("dp", None), P(("dp", "land"), None), P(), P(("dp", "land"), None))
    return jax.shard_map(
        on_device, mesh=mesh, in_specs=placed, out_specs=P(("dp", "land"), None), check_vma=False
    )
```

time: 489 us -> 254 us (0.52)
  local copies, waits for them, and re-layouts: 131 us -> 10.1 us
  matrix products: 126 us -> 5.23 us
  Pallas kernels: 0 us -> 28.4 us
  other arithmetic: 31.5 us -> 8.36 us
  blocking collectives: 24.4 us -> 43.4 us
  waiting for transfers between devices: 157 us -> 142 us
    convert_element_type x16 -> x0, local copies, waits for them, and re-layouts: 124 us -> none  [one_block(): aligned = jnp.einsum('dab,lbt->dlat', matches, tile_grid, preferred_eleme...]
    dot_general x36 -> x2, matrix products: 126 us -> 5.23 us  [the longest x1 4.08 us: on_device(): jnp.dot(tile_high.T, fitted_pair, preferred_element_type=jnp.float32)]
    pallas_call x0 -> x1, Pallas kernels: none -> 28.4 us  [forward(): pl.pallas_call(forward_kernel, grid_spec=grid_spec, out_shape=[jax.ShapeD...]
    all_gather x0 -> x1, blocking collectives: none -> 22.3 us  [on_device(): norm_rows = lax.all_gather(land_norm, 'dp', axis=0, tiled=True)]
    dynamic_update_slice x16 -> x0, other arithmetic: 19 us -> none  [kernel_tiles(): return lax.map(one_block, (land_grid, land_ids, norm_grid))]
    all_gather x1, waiting for transfers between devices: 14.6 us -> 0.01 us  [on_device(): land_rows = lax.all_gather(land_values, 'dp', axis=0, tiled=True)]
  transfers between devices with their start and end apart: 3 -> 3, of which waited for: 3 -> 2; matrix products, arithmetic and copies ran while one was open for 1% -> 4% of each run, Pallas kernels for 0% -> 0%
where the time goes in v1:
time: 254 us; the launch traced here: 251 us
  waiting for transfers between devices  142 us (56%)
  blocking collectives  43.4 us (17%)
  Pallas kernels  28.4 us (11%)
  between operations  13.3 us (5%)
  local copies, waits for them, and re-layouts  10.1 us (4%)
  other arithmetic  8.36 us (3%)
  matrix products  5.23 us (2%)
    psum x1, waiting for transfers between devices, on_device(): fitted = lax.psum(fitted, 'land')  80.1 us
    reduce_scatter x1, waiting for transfers between devices, on_device(): result = lax.psum_scatter(summed, 'dp', scatter_dimension=0, tiled=True)  61.2 us
    pallas_call x1, Pallas kernels, forward(): pl.pallas_call(forward_kernel, grid_spec=grid_spec, out_shape=[jax.ShapeD...  28.4 us
    all_gather x1, blocking collectives, on_device(): norm_rows = lax.all_gather(land_norm, 'dp', axis=0, tiled=True)  22.3 us
    all_gather x1, blocking collectives, on_device(): coef_rows = lax.all_gather(coefficients, 'dp', axis=0, tiled=True)  21.1 us
    unnamed x19, local copies, waits for them, and re-layouts  6.27 us
  transfers between devices with their start and end apart: 3, of which 2 were waited for; matrix products, arithmetic and copies ran while one was open for 4% of the time, Pallas kernels for 0%

profile of v1, /device:TPU:1, one launch (start us, length us, event | category | flops | bytes accessed | tf_op | source)
XLA Modules:
  0.0 250.9 jit_solution(5967299636942272839)
XLA Ops:
  6.5 0.7 all-gather.3.cloned.1.call-update
  7.3 0.0 all-reduce.3.cloned.1.call-start
  7.3 0.9 copy.25
  8.2 1.4 copy.28
  9.7 0.8 reshape.30
  10.5 0.3 dynamic-slice_reduce_fusion
  10.7 0.2 compare_reduce_fusion.1
  10.9 0.8 compare_reduce_fusion
  11.8 0.1 copy.26
  11.9 0.1 reshape.31.slot_ref
  12.0 2.6 %multiply_reduce_fusion = f32[1536]{0:T(1024)S(1)} fusion(bf16[1536,1024]{1,0:T(8,128)(2,1)} %param.5), kind=kLoop, calls=%fused_computation | loop fusion | flops 4717056 | bytes 3151872 | tf_op jit(solution)/shard_map/reduce_sum | solution.py:104
  14.6 1.1 rsqrt.19.dn_ref
  15.7 0.8 copy.30
  16.6 0.9 copy.32
  17.5 0.5 pad.4
  18.0 0.1 multiply_reduce_fusion.1
  18.2 22.3 %all-gather.ln_ref = f32[16,1,128]{2,1,0:T(1,128)S(1)} all-gather(f32[1,1,128]{2,1,0:T(1,128)S(1)} %rsqrt_bitcast_fusion), channel_id=1, replica_groups=mesh['dp'=16,'land'=8] {'dp'}, dimensions={0}, use_global_device_ids=true | all-gather | bytes 8704 | tf_op jit(solution)/shard_map/all_gather | solution.py:111
  40.5 21.1 %all_gather.11.coef_ref = bf16[2048,64]{1,0:T(8,128)(2,1)} all-gather(bf16[128,64]{1,0:T(8,128)(2,1)S(1)} %copy-done.5), channel_id=1, replica_groups=mesh['dp'=16,'land'=8] {'dp'}, dimensions={0}, use_global_device_ids=true | all-gather | bytes 278528 | tf_op jit(solution)/shard_map/all_gather | solution.py:110
  61.6 1.1 copy-done
  62.7 1.0 copy-done.1
  63.7 28.4 %shard_map.55 = (bf16[1536,2048]{1,0:T(8,128)(2,1)}, bf16[1536,2048]{1,0:T(8,128)(2,1)}, f32[1536,64]{1,0:T(8,128)S(1)}) custom-call(s32[1536]{0:T(1024)S(1)} %reshape.31.slot_ref, bf16[108,128,128]{2,1,0:T(8,128)(2,1)S(1)} %bitcast.13, f32[1536,1]{1,0:T(8,128)S(1)} %copy-done, bf16[2048,1024]{1,0:T(8,128)(2,1)} %all-gather.3.cloned.1.call-done.land_ref, ...), custom_call_target="tpu_custom_call" | custom-call | tf_op jit(solution)/shard_map/pallas_call | solution.py:83
  92.2 0.9 copy-done.2
  93.0 0.0 all-reduce.3.cloned.1.call-update
  93.1 0.0 reduce-scatter.2.cloned.1.call-start
  93.1 80.1 %all-reduce.3.cloned.1.call-done = f32[1536,64]{1,0:T(8,128)} async-done(((f32[1536,64]{1,0:T(8,128)}), f32[1536,64]{1,0:T(8,128)}) %all-reduce.3.cloned.1.call-update) | async-done | bytes 393232 | tf_op jit(solution)/shard_map/psum | solution.py:118
  173.3 1.2 convert_element_type.19
  174.4 1.2 subtract_convert_fusion
  175.7 4.1 %fusion = f32[2048,128]{0,1:T(8,128)S(1)} fusion(bf16[1536,2048]{1,0:T(8,128)(2,1)} %get-tuple-element.10, bf16[1536,64]{1,0:T(8,128)(2,1)S(1)} %subtract_convert_fusion, bf16[1536,64]{1,0:T(8,128)(2,1)S(1)} %convert_element_type.19), kind=kOutput, calls=%fused_computation.10 | convolution fusion | flops 806092800 | bytes 7733248 | tf_op jit(solution)/shard_map/dot_general | solution.py:121
  179.8 1.1 convolution_add_fusion
  180.9 0.8 slice_add_fusion
  181.8 61.2 %reduce-scatter.2.cloned.1.call-done = f32[128,64]{0,1:T(8,128)} async-done(((f32[2048,64]{0,1:T(8,128)}), f32[128,64]{0,1:T(8,128)}) %reduce-scatter.2.cloned.1.call-update) | async-done | bytes 32784 | tf_op jit(solution)/shard_map/reduce_scatter | solution.py:124
  243.0 1.4 broadcast_multiply_fusion
  (20 shorter events, 0.1 us)
Async XLA Ops:
  6.5 9.2 %copy-start.3 = (bf16[1536,1024]{1,0:T(8,128)(2,1)S(1)}, bf16[1536,1024]{1,0:T(8,128)(2,1)}, u32[]{:S(2)}) copy-start(bf16[1536,1024]{1,0:T(8,128)(2,1)} %param.5) | copy-start | bytes 9437188
  6.5 55.0 %all-gather.3.cloned.1.call-start = ((), (), s32[]{:S(2)}) async-start(), calls=%async_computation.1 | async-start | bytes 4456448 | tf_op jit(solution)/shard_map/all_gather | solution.py:109
  7.3 166.0 %all-reduce.3.cloned.1.call-start = ((), (), s32[]{:S(2)}) async-start(), calls=%async_computation.2 | async-start | bytes 1572864 | tf_op jit(solution)/shard_map/psum | solution.py:118
  16.6 1.5 copy-start.4
  16.6 23.9 %copy-start.5 = (bf16[128,64]{1,0:T(8,128)(2,1)S(1)}, bf16[128,64]{1,0:T(8,128)(2,1)}, u32[]{:S(2)}) copy-start(bf16[128,64]{1,0:T(8,128)(2,1)} %copy.28) | copy-start | bytes 49156
  61.6 1.1 copy-start
  62.7 1.0 copy-start.1
  92.2 0.9 copy-start.2
  93.0 86.7 %slice-start = ((s8[6291456]{0:T(1024)(128)(4,1)}), s8[2097152]{0:T(1024)(128)(4,1)S(1)}, s32[]{:S(2)}) async-start(s8[6291456]{0:T(1024)(128)(4,1)} %bitcast.17), calls=%async_computation.4 | async-start | bytes 4194304
  93.1 149.9 %reduce-scatter.2.cloned.1.call-start = ((), (), s32[]{:S(2)}) async-start(), calls=%async_computation.3 | async-start | bytes 557056 | tf_op jit(solution)/shard_map/reduce_scatter | solution.py:124
  175.7 4.1 %slice-start.1 = ((s8[6291456]{0:T(1024)(128)(4,1)}), s8[4194304]{0:T(1024)(128)(4,1)S(1)}, s32[]{:S(2)}) async-start(s8[6291456]{0:T(1024)(128)(4,1)} %bitcast.17), calls=%async_computation.5 | async-start | bytes 8388608
Sparse Core Ops, SparseCore 0:
  9.0 42.2 all-gather.2
  93.2 80.0 all-reduce.2
  181.9 61.0 reduce-scatter.1

commit v2 on v1

--- a/solution.py
+++ b/solution.py
@@ -28,7 +28,7 @@
     return jnp.where(has, first, ACTIVE).astype(jnp.int32).reshape(-1)
 
 
-def forward_kernel(slot_ref, doc_ref, dn_ref, land_ref, ln_ref, coef_ref,
+def forward_kernel(slot_ref, doc_ref, dn_ref, land_ref,
                    high_ref, low_ref, fit_ref, aligned_ref):
     step = pl.program_id(0)
     doc_count = dn_ref.shape[0] // DOC_BLOCK
@@ -42,36 +42,40 @@
             a = slot_ref[(step * doc_count + d) * LAND_ACTIVE + b]
             aligned_ref[d * DOC_BLOCK:(d + 1) * DOC_BLOCK, b * TERM_BLOCK:(b + 1) * TERM_BLOCK] = (
                 doc_ref[d * (ACTIVE + 1) + a])
+    width = ACTIVE * TERM_BLOCK
+    tile = land_ref[:, :width]
+    squares = jnp.zeros((LM_BLOCK, TERM_BLOCK), jnp.float32)
+    for b in range(LAND_ACTIVE):
+        part = tile[:, b * TERM_BLOCK:(b + 1) * TERM_BLOCK].astype(jnp.float32)
+        squares = squares + part * part
+    land_norm = lax.rsqrt(jnp.sum(squares.T, axis=0, keepdims=True) + 1e-06)
     inner = lax.dot_general(
-        aligned_ref[...], land_ref[...], (((1,), (1,)), ((), ())),
+        aligned_ref[...], tile, (((1,), (1,)), ((), ())),
         preferred_element_type=jnp.float32)
-    cosine = inner * dn_ref[...] * ln_ref[0]
+    cosine = inner * dn_ref[...] * land_norm
     kern = jnp.exp(2.0 * sharpness * (cosine - 1.0))
     high = kern.astype(jnp.bfloat16)
     low = (kern - high.astype(jnp.float32)).astype(jnp.bfloat16)
     high_ref[...] = high
     low_ref[...] = low
-    coef = coef_ref[...]
+    coef = land_ref[:, width:]
     part = jnp.dot(high, coef, preferred_element_type=jnp.float32)
     part = part + jnp.dot(low, coef, preferred_element_type=jnp.float32)
     fit_ref[...] += part
 
 
-def forward(slots, doc_tiles, doc_norm, land_rows, land_norm, coef_rows):
+def forward(slots, doc_tiles, doc_norm, land_rows, targets):
     doc_rows = doc_norm.shape[0]
     land_count = land_rows.shape[0]
     block_count = land_count // LM_BLOCK
-    width = land_rows.shape[1]
-    targets = coef_rows.shape[1]
+    width = ACTIVE * TERM_BLOCK
     grid_spec = pltpu.PrefetchScalarGridSpec(
         num_scalar_prefetch=1,
         grid=(block_count,),
         in_specs=[
             pl.BlockSpec(doc_tiles.shape, lambda l, s: (0, 0, 0)),
             pl.BlockSpec((doc_rows, 1), lambda l, s: (0, 0)),
-            pl.BlockSpec((LM_BLOCK, width), lambda l, s: (l, 0)),
-            pl.BlockSpec((1, 1, LM_BLOCK), lambda l, s: (l, 0, 0)),
-            pl.BlockSpec((LM_BLOCK, targets), lambda l, s: (l, 0)),
+            pl.BlockSpec((LM_BLOCK, land_rows.shape[1]), lambda l, s: (l, 0)),
         ],
         out_specs=[
             pl.BlockSpec((doc_rows, LM_BLOCK), lambda l, s: (0, l)),
@@ -90,7 +94,33 @@
         ],
         compiler_params=pltpu.CompilerParams(
             dimension_semantics=("arbitrary",), vmem_limit_bytes=48 * 1024 * 1024),
-    )(slots, doc_tiles, doc_norm, land_rows, land_norm.reshape(block_count, 1, LM_BLOCK), coef_rows)
+    )(slots, doc_tiles, doc_norm, land_rows)
+
+
+def gather_rows(rows, dp_count):
+    own = lax.axis_index("dp")
+    parts = [rows]
+    sources = [own]
+    for k in range(1, dp_count // 2):
+        shift = [(i, (i + 2 * k) % dp_count) for i in range(dp_count)]
+        parts.append(lax.ppermute(rows, "dp", shift))
+        sources.append((own - 2 * k) % dp_count)
+    mine = jnp.concatenate(parts, axis=0)
+    other = lax.ppermute(mine, "dp", [(i, i ^ 1) for i in range(dp_count)])
+    sources = sources + [s ^ 1 for s in sources]
+    return jnp.concatenate([mine, other], axis=0), jnp.stack(sources).astype(jnp.int32)
+
+
+def sum_over(values, axis, count):
+    pieces = values.reshape((count, values.shape[0] // count) + values.shape[1:])
+    pieces = lax.all_to_all(pieces, axis, 0, 0, tiled=False)
+    return jnp.sum(pieces, axis=0)
+
+
+def all_sum(values, axis, count):
+    mine = sum_over(values, axis, count)
+    spread = jnp.broadcast_to(mine[None], (count,) + mine.shape)
+    return lax.all_to_all(spread, axis, 0, 0, tiled=False).reshape(values.shape)
 
 
 def on_device(doc_values, doc_blocks, land_values, land_blocks, coefficients):
@@ -102,26 +132,26 @@
     own_blocks = land_values.shape[0] // LM_BLOCK
     doc_count = doc_rows // DOC_BLOCK
     doc_norm = lax.rsqrt(jnp.sum(jnp.square(doc_values.astype(jnp.float32)), axis=1) + 1e-06)
-    land_norm = lax.rsqrt(jnp.sum(jnp.square(land_values.astype(jnp.float32)), axis=1) + 1e-06)
     table = land_blocks.reshape(dp_count, land_count, own_blocks, LAND_ACTIVE)
     own_table = lax.dynamic_index_in_dim(table, lax.axis_index("land"), axis=1, keepdims=False)
     own_table = own_table.reshape(dp_count * own_blocks, LAND_ACTIVE)
-    land_rows = lax.all_gather(land_values, "dp", axis=0, tiled=True)
-    coef_rows = lax.all_gather(coefficients, "dp", axis=0, tiled=True)
-    norm_rows = lax.all_gather(land_norm, "dp", axis=0, tiled=True)
+    land_rows, sources = gather_rows(jnp.concatenate([land_values, coefficients], axis=1), dp_count)
+    own_table = own_table[sources]
     doc_tiles = doc_values.reshape(doc_count, DOC_BLOCK, ACTIVE, TERM_BLOCK).transpose(0, 2, 1, 3)
     doc_tiles = jnp.pad(doc_tiles, ((0, 0), (0, 1), (0, 0), (0, 0)))
     doc_tiles = doc_tiles.reshape(doc_count * (ACTIVE + 1), DOC_BLOCK, TERM_BLOCK)
     slots = match_table(doc_blocks, own_table)
     tile_high, tile_low, fitted = forward(
-        slots, doc_tiles, doc_norm.reshape(doc_rows, 1), land_rows, norm_rows, coef_rows)
-    fitted = lax.psum(fitted, "land")
+        slots, doc_tiles, doc_norm.reshape(doc_rows, 1), land_rows, targets)
+    fitted = all_sum(fitted, "land", land_count)
     fitted_high, fitted_low = split_pair(fitted)
     fitted_pair = jnp.concatenate([fitted_high, fitted_low], axis=1)
     summed = jnp.dot(tile_high.T, fitted_pair, preferred_element_type=jnp.float32)
     summed = summed + jnp.dot(tile_low.T, fitted_pair, preferred_element_type=jnp.float32)
     summed = summed[:, :targets] + summed[:, targets:]
-    result = lax.psum_scatter(summed, "dp", scatter_dimension=0, tiled=True)
+    order = jnp.argsort(sources)
+    summed = summed.reshape(dp_count, own_blocks * LM_BLOCK, targets)[order]
+    result = sum_over(summed.reshape(-1, targets), "dp", dp_count)
     return result / total_docs
 
 

time: 254 us -> 148 us (0.58)
  waiting for transfers between devices: 142 us -> 21.4 us
  local copies, waits for them, and re-layouts: 10.1 us -> 27.3 us
  between operations: 13.3 us -> 0.23 us
  starting transfers between devices: 0.08 us -> 9.5 us
  blocking collectives: 43.4 us -> 49.9 us
  other arithmetic: 8.36 us -> 5.71 us
    psum x1 -> x0, waiting for transfers between devices: 80.1 us -> none  [on_device(): fitted = lax.psum(fitted, 'land')]
    reduce_scatter x1 -> x0, waiting for transfers between devices: 61.2 us -> none  [on_device(): result = lax.psum_scatter(summed, 'dp', scatter_dimension=0, tiled=True)]
    all_to_all x0 -> x3, blocking collectives: none -> 49.9 us  [the longest x2 37.3 us: sum_over(): pieces = lax.all_to_all(pieces, axis, 0, 0, tiled=False)]
    all_gather x2 -> x0, blocking collectives: 43.4 us -> none  [the longest x1 22.3 us: on_device(): norm_rows = lax.all_gather(land_norm, 'dp', axis=0, tiled=True)]
    ppermute x0 -> x8, waiting for transfers between devices: none -> 21.4 us  [the longest x7 21.4 us: gather_rows(): parts.append(lax.ppermute(rows, 'dp', shift))]
    ppermute x0 -> x8, starting transfers between devices: none -> 9.5 us  [the longest x7 9.01 us: gather_rows(): parts.append(lax.ppermute(rows, 'dp', shift))]
    concatenate x0 -> x3, local copies, waits for them, and re-layouts: none -> 8.46 us  [the longest x2 5.14 us: gather_rows(): mine = jnp.concatenate(parts, axis=0)]
    ppermute x0 -> x1, local copies, waits for them, and re-layouts: none -> 4.21 us  [gather_rows(): other = lax.ppermute(mine, 'dp', [(i, i ^ 1) for i in range(dp_count)])]
  transfers between devices with their start and end apart: 3 -> 8, of which waited for: 2 -> 4; matrix products, arithmetic and copies ran while one was open for 4% -> 9% of each run, Pallas kernels for 0% -> 0%
where the time goes in v2:
time: 148 us; the launch traced here: 147 us
  blocking collectives  49.9 us (34%)
  Pallas kernels  28.5 us (19%)
  local copies, waits for them, and re-layouts  27.3 us (18%)
  waiting for transfers between devices  21.4 us (14%)
  starting transfers between devices  9.5 us (6%)
  other arithmetic  5.71 us (4%)
  matrix products  4.95 us (3%)
    all_to_all x2, blocking collectives, sum_over(): pieces = lax.all_to_all(pieces, axis, 0, 0, tiled=False)  37.3 us
    pallas_call x1, Pallas kernels, forward(): pl.pallas_call(forward_kernel, grid_spec=grid_spec, out_shape=[jax.ShapeD...  28.5 us
    ppermute x7, waiting for transfers between devices, gather_rows(): parts.append(lax.ppermute(rows, 'dp', shift))  21.4 us
    all_to_all x1, blocking collectives, all_sum(): return lax.all_to_all(spread, axis, 0, 0, tiled=False).reshape(values.shape)  12.5 us
    ppermute x7, starting transfers between devices, gather_rows(): parts.append(lax.ppermute(rows, 'dp', shift))  9.01 us
    unnamed x23, local copies, waits for them, and re-layouts  8.07 us
    concatenate x2, local copies, waits for them, and re-layouts, gather_rows(): mine = jnp.concatenate(parts, axis=0)  5.14 us
    ppermute x1, local copies, waits for them, and re-layouts, gather_rows(): other = lax.ppermute(mine, 'dp', [(i, i ^ 1) for i in range(dp_count)])  4.21 us
  transfers between devices with their start and end apart: 8, of which 4 were waited for; matrix products, arithmetic and copies ran while one was open for 9% of the time, Pallas kernels for 0%

profile of v2, /device:TPU:1, one launch (start us, length us, event | category | flops | bytes accessed | tf_op | source)
XLA Modules:
  0.0 147.4 jit_solution(14956900067203985676)
XLA Ops:
  0.8 1.9 %constant_dynamic-update-slice_fusion.7 = (bf16[1024,1088]{1,0:T(8,128)(2,1)}, bf16[2048,1088]{1,0:T(8,128)(2,1)}, bf16[128,1088]{1,0:T(8,128)(2,1)S(1)}) fusion(bf16[128,64]{1,0:T(8,128)(2,1)S(1)} %copy.46, bf16[128,1024]{1,0:T(8,128)(2,1)} %param.7), kind=kLoop, calls=%fused_computation.21 | loop fusion | flops 557054 | bytes 1146880
  2.7 2.1 %collective-permute-start = (bf16[128,1088]{1,0:T(8,128)(2,1)S(1)}, bf16[128,1088]{1,0:T(8,128)(2,1)S(1)}, u32[]{:S(2)}, u32[]{:S(2)}) collective-permute-start(bf16[128,1088]{1,0:T(8,128)(2,1)S(1)} %get-tuple-element.31), channel_id=1, source_target_pairs={{0,16},{8,24},{16,32},{24,40},{32,48},{40,56},{48,64},{56,72},{64,... | collective-permute-start | bytes 835592 | tf_op jit(solution)/shard_map/ppermute | solution.py:106
  4.8 1.6 %collective-permute-start.1 = (bf16[128,1088]{1,0:T(8,128)(2,1)S(1)}, bf16[128,1088]{1,0:T(8,128)(2,1)S(1)}, u32[]{:S(2)}, u32[]{:S(2)}) collective-permute-start(bf16[128,1088]{1,0:T(8,128)(2,1)S(1)} %get-tuple-element.31), channel_id=1, source_target_pairs={{0,32},{8,40},{16,48},{24,56},{32,64},{40,72},{48,80},{56,88},{64,... | collective-permute-start | bytes 835592 | tf_op jit(solution)/shard_map/ppermute | solution.py:106
  6.5 2.1 %collective-permute-start.5 = (bf16[128,1088]{1,0:T(8,128)(2,1)S(1)}, bf16[128,1088]{1,0:T(8,128)(2,1)S(1)}, u32[]{:S(2)}, u32[]{:S(2)}) collective-permute-start(bf16[128,1088]{1,0:T(8,128)(2,1)S(1)} %get-tuple-element.31), channel_id=1, source_target_pairs={{0,96},{8,104},{16,112},{24,120},{32,0},{40,8},{48,16},{56,24},{64... | collective-permute-start | bytes 835592 | tf_op jit(solution)/shard_map/ppermute | solution.py:106
  8.6 2.2 %collective-permute-start.4 = (bf16[128,1088]{1,0:T(8,128)(2,1)S(1)}, bf16[128,1088]{1,0:T(8,128)(2,1)S(1)}, u32[]{:S(2)}, u32[]{:S(2)}) collective-permute-start(bf16[128,1088]{1,0:T(8,128)(2,1)S(1)} %get-tuple-element.31), channel_id=1, source_target_pairs={{0,80},{8,88},{16,96},{24,104},{32,112},{40,120},{48,0},{56,8},{64... | collective-permute-start | bytes 835592 | tf_op jit(solution)/shard_map/ppermute | solution.py:106
  10.8 0.9 collective-permute-start.3
  11.7 3.3 %collective-permute-done = bf16[128,1088]{1,0:T(8,128)(2,1)S(1)} collective-permute-done((bf16[128,1088]{1,0:T(8,128)(2,1)S(1)}, bf16[128,1088]{1,0:T(8,128)(2,1)S(1)}, u32[]{:S(2)}, u32[]{:S(2)}) %collective-permute-start) | collective-permute-done | bytes 278560 | tf_op jit(solution)/shard_map/ppermute | solution.py:106
  15.0 0.9 constant_dynamic-update-slice_fusion.6
  15.9 6.1 %collective-permute-done.1 = bf16[128,1088]{1,0:T(8,128)(2,1)S(1)} collective-permute-done((bf16[128,1088]{1,0:T(8,128)(2,1)S(1)}, bf16[128,1088]{1,0:T(8,128)(2,1)S(1)}, u32[]{:S(2)}, u32[]{:S(2)}) %collective-permute-start.1) | collective-permute-done | bytes 278560 | tf_op jit(solution)/shard_map/ppermute | solution.py:106
  22.1 0.9 constant_dynamic-update-slice_fusion.5
  23.0 5.5 %collective-permute-done.2 = bf16[128,1088]{1,0:T(8,128)(2,1)S(1)} collective-permute-done((bf16[128,1088]{1,0:T(8,128)(2,1)S(1)}, bf16[128,1088]{1,0:T(8,128)(2,1)S(1)}, u32[]{:S(2)}, u32[]{:S(2)}) %collective-permute-start.2) | collective-permute-done | bytes 278560 | tf_op jit(solution)/shard_map/ppermute | solution.py:106
  28.5 0.9 constant_dynamic-update-slice_fusion.4
  29.4 6.4 %collective-permute-done.3 = bf16[128,1088]{1,0:T(8,128)(2,1)S(1)} collective-permute-done((bf16[128,1088]{1,0:T(8,128)(2,1)S(1)}, bf16[128,1088]{1,0:T(8,128)(2,1)S(1)}, u32[]{:S(2)}, u32[]{:S(2)}) %collective-permute-start.3) | collective-permute-done | bytes 278560 | tf_op jit(solution)/shard_map/ppermute | solution.py:106
  35.8 0.9 constant_dynamic-update-slice_fusion.3
  36.7 0.9 constant_dynamic-update-slice_fusion.2
  37.6 0.9 constant_dynamic-update-slice_fusion.1
  38.4 0.9 constant_dynamic-update-slice_fusion
  39.4 4.2 %copy.47 = bf16[1024,1088]{0,1:T(8,128)(2,1)} copy(bf16[1024,1088]{1,0:T(8,128)(2,1)} %get-tuple-element.15) | data formatting | bytes 4456448 | tf_op jit(solution)/shard_map/concatenate | solution.py:108
  44.6 1.3 sort.17
  46.9 0.8 compare_reduce_fusion
  48.6 1.2 rsqrt.15.dn_ref
  50.6 0.9 copy.58
  52.1 4.2 %copy.48 = bf16[1024,1088]{1,0:T(8,128)(2,1)} copy(bf16[1024,1088]{0,1:T(8,128)(2,1)} %collective-permute-done.7) | data formatting | bytes 4456448 | tf_op jit(solution)/shard_map/ppermute | solution.py:109
  56.3 3.3 %constant_dynamic-update-slice_fusion.8.land_ref = bf16[2048,1088]{1,0:T(8,128)(2,1)} fusion(bf16[2048,1088]{1,0:T(8,128)(2,1)} %get-tuple-element.16, bf16[1024,1088]{1,0:T(8,128)(2,1)} %copy.48), kind=kLoop, calls=%fused_computation.22 | loop fusion | bytes 4718592 | tf_op jit(solution)/shard_map/concatenate | solution.py:111
  59.6 28.5 %shard_map.55 = (bf16[1536,2048]{1,0:T(8,128)(2,1)}, bf16[1536,2048]{1,0:T(8,128)(2,1)}, f32[1536,64]{1,0:T(8,128)S(1)}) custom-call(s32[1536]{0:T(1024)S(1)} %reshape.661.slot_ref, bf16[108,128,128]{2,1,0:T(8,128)(2,1)S(1)} %bitcast.54, f32[1536,1]{1,0:T(8,128)S(1)} %copy-done, bf16[2048,1088]{1,0:T(8,128)(2,1)} %constant_dynamic-update-slice_fusion.8.land_ref), custom_call_target="tpu_custom_call" | custom-call | tf_op jit(solution)/shard_map/pallas_call | solution.py:87
  88.1 0.9 copy-done.1
  89.0 1.4 copy.50
  90.5 17.4 %all_to_all.15 = f32[8,192,64]{1,2,0:T(8,128)S(1)} all-to-all(f32[8,192,64]{1,2,0:T(8,128)S(1)} %copy.50), channel_id=1, replica_groups=mesh['dp'=16,'land'=8] {'land'}, dimensions={0} | all-to-all | bytes 786432 | tf_op jit(solution)/shard_map/all_to_all | solution.py:116
  108.0 12.5 %all_to_all.16 = f32[8,192,64]{1,2,0:T(8,128)S(1)} all-to-all(f32[8,192,64]{1,2,0:T(8,128)S(1)} %broadcast_in_dim.9), channel_id=1, replica_groups=mesh['dp'=16,'land'=8] {'land'}, dimensions={0} | all-to-all | bytes 786432 | tf_op jit(solution)/shard_map/all_to_all | solution.py:123
  121.1 3.9 %fusion.1 = f32[2048,128]{0,1:T(8,128)S(1)} fusion(bf16[1536,2048]{1,0:T(8,128)(2,1)} %get-tuple-element.13, bf16[1536,64]{0,1:T(8,128)(2,1)S(1)} %subtract_convert_fusion, bf16[1536,64]{0,1:T(8,128)(2,1)S(1)} %convert_element_type.15), kind=kOutput, calls=%fused_computation.13 | convolution fusion | flops 806092800 | bytes 7733248 | tf_op jit(solution)/shard_map/dot_general | solution.py:150
  125.1 1.0 convolution_add_fusion
  126.8 19.9 %all_to_all.17 = f32[16,128,64]{1,2,0:T(8,128)S(1)} all-to-all(f32[16,128,64]{1,2,0:T(8,128)S(1)} %gather_fusion.1), channel_id=1, replica_groups=mesh['dp'=16,'land'=8] {'dp'}, dimensions={0} | all-to-all | bytes 1048576 | tf_op jit(solution)/shard_map/all_to_all | solution.py:116
  (52 shorter events, 7.0 us)
Async XLA Ops:
  2.7 12.3 %collective-permute-start = (bf16[128,1088]{1,0:T(8,128)(2,1)S(1)}, bf16[128,1088]{1,0:T(8,128)(2,1)S(1)}, u32[]{:S(2)}, u32[]{:S(2)}) collective-permute-start(bf16[128,1088]{1,0:T(8,128)(2,1)S(1)} %get-tuple-element.31), channel_id=1, source_target_pairs={{0,16},{8,24},{16,32},{24,40},{32,48},{40,56},{48,64},{56,72},{64,... | collective-permute-start | bytes 835592 | tf_op jit(solution)/shard_map/ppermute | solution.py:106
  4.8 17.3 %collective-permute-start.1 = (bf16[128,1088]{1,0:T(8,128)(2,1)S(1)}, bf16[128,1088]{1,0:T(8,128)(2,1)S(1)}, u32[]{:S(2)}, u32[]{:S(2)}) collective-permute-start(bf16[128,1088]{1,0:T(8,128)(2,1)S(1)} %get-tuple-element.31), channel_id=1, source_target_pairs={{0,32},{8,40},{16,48},{24,56},{32,64},{40,72},{48,80},{56,88},{64,... | collective-permute-start | bytes 835592 | tf_op jit(solution)/shard_map/ppermute | solution.py:106
  6.5 31.1 %collective-permute-start.5 = (bf16[128,1088]{1,0:T(8,128)(2,1)S(1)}, bf16[128,1088]{1,0:T(8,128)(2,1)S(1)}, u32[]{:S(2)}, u32[]{:S(2)}) collective-permute-start(bf16[128,1088]{1,0:T(8,128)(2,1)S(1)} %get-tuple-element.31), channel_id=1, source_target_pairs={{0,96},{8,104},{16,112},{24,120},{32,0},{40,8},{48,16},{56,24},{64... | collective-permute-start | bytes 835592 | tf_op jit(solution)/shard_map/ppermute | solution.py:106
  8.6 28.1 %collective-permute-start.4 = (bf16[128,1088]{1,0:T(8,128)(2,1)S(1)}, bf16[128,1088]{1,0:T(8,128)(2,1)S(1)}, u32[]{:S(2)}, u32[]{:S(2)}) collective-permute-start(bf16[128,1088]{1,0:T(8,128)(2,1)S(1)} %get-tuple-element.31), channel_id=1, source_target_pairs={{0,80},{8,88},{16,96},{24,104},{32,112},{40,120},{48,0},{56,8},{64... | collective-permute-start | bytes 835592 | tf_op jit(solution)/shard_map/ppermute | solution.py:106
  10.8 25.0 %collective-permute-start.3 = (bf16[128,1088]{1,0:T(8,128)(2,1)S(1)}, bf16[128,1088]{1,0:T(8,128)(2,1)S(1)}, u32[]{:S(2)}, u32[]{:S(2)}) collective-permute-start(bf16[128,1088]{1,0:T(8,128)(2,1)S(1)} %get-tuple-element.31), channel_id=1, source_target_pairs={{0,64},{8,72},{16,80},{24,88},{32,96},{40,104},{48,112},{56,120},{... | collective-permute-start | bytes 835592 | tf_op jit(solution)/shard_map/ppermute | solution.py:106
  15.0 13.5 %collective-permute-start.2 = (bf16[128,1088]{1,0:T(8,128)(2,1)S(1)}, bf16[128,1088]{1,0:T(8,128)(2,1)S(1)}, u32[]{:S(2)}, u32[]{:S(2)}) collective-permute-start(bf16[128,1088]{1,0:T(8,128)(2,1)S(1)} %get-tuple-element.31), channel_id=1, source_target_pairs={{0,48},{8,56},{16,64},{24,72},{32,80},{40,88},{48,96},{56,104},{64... | collective-permute-start | bytes 835592 | tf_op jit(solution)/shard_map/ppermute | solution.py:106
  22.1 16.4 %collective-permute-start.6 = (bf16[128,1088]{1,0:T(8,128)(2,1)S(1)}, bf16[128,1088]{1,0:T(8,128)(2,1)S(1)}, u32[]{:S(2)}, u32[]{:S(2)}) collective-permute-start(bf16[128,1088]{1,0:T(8,128)(2,1)S(1)} %get-tuple-element.31), channel_id=1, source_target_pairs={{0,112},{8,120},{16,0},{24,8},{32,16},{40,24},{48,32},{56,40},{64,... | collective-permute-start | bytes 835592 | tf_op jit(solution)/shard_map/ppermute | solution.py:106
  23.0 21.1 %copy-start.3 = (s32[12,8]{0,1:T(8,128)S(1)}, s32[12,8]{0,1:T(8,128)}, u32[]{:S(2)}) copy-start(s32[12,8]{0,1:T(8,128)} %param.6) | copy-start | bytes 1156
  23.0 21.2 %copy-start.4 = (s32[128,8]{0,1:T(8,128)S(1)}, s32[128,8]{0,1:T(8,128)}, u32[]{:S(2)}) copy-start(s32[128,8]{0,1:T(8,128)} %param.8) | copy-start | bytes 12292
  29.4 18.5 %copy-start.2 = (bf16[1536,1024]{1,0:T(8,128)(2,1)S(1)}, bf16[1536,1024]{1,0:T(8,128)(2,1)}, u32[]{:S(2)}) copy-start(bf16[1536,1024]{1,0:T(8,128)(2,1)} %param.5) | copy-start | bytes 9437188
  43.6 8.5 %collective-permute-start.7 = (bf16[1024,1088]{0,1:T(8,128)(2,1)}, bf16[1024,1088]{0,1:T(8,128)(2,1)}, u32[]{:S(2)}, u32[]{:S(2)}) collective-permute-start(bf16[1024,1088]{0,1:T(8,128)(2,1)} %copy.47), channel_id=1, source_target_pairs={{0,8},{8,0},{16,24},{24,16},{32,40},{40,32},{48,56},{56,48},{64,72... | collective-permute-start | bytes 6684680 | tf_op jit(solution)/shard_map/ppermute | solution.py:109
  56.3 3.3 %copy-start = (f32[1536,1]{1,0:T(8,128)S(1)}, f32[1536,1]{1,0:T(8,128)}, u32[]{:S(2)}) copy-start(f32[1536,1]{1,0:T(8,128)} %rsqrt.15.dn_ref) | copy-start | bytes 18436
  88.1 0.9 copy-start.1
  108.0 17.1 %slice-start = ((s8[6291456]{0:T(1024)(128)(4,1)}), s8[2097152]{0:T(1024)(128)(4,1)S(1)}, s32[]{:S(2)}) async-start(s8[6291456]{0:T(1024)(128)(4,1)} %bitcast.56), calls=%async_computation.3 | async-start | bytes 4194304
  121.1 4.0 %slice-start.1 = ((s8[6291456]{0:T(1024)(128)(4,1)}), s8[4194304]{0:T(1024)(128)(4,1)S(1)}, s32[]{:S(2)}) async-start(s8[6291456]{0:T(1024)(128)(4,1)} %bitcast.56), calls=%async_computation.4 | async-start | bytes 8388608

commit v3 on v2

--- a/solution.py
+++ b/solution.py
@@ -97,20 +97,6 @@
     )(slots, doc_tiles, doc_norm, land_rows)
 
 
-def gather_rows(rows, dp_count):
-    own = lax.axis_index("dp")
-    parts = [rows]
-    sources = [own]
-    for k in range(1, dp_count // 2):
-        shift = [(i, (i + 2 * k) % dp_count) for i in range(dp_count)]
-        parts.append(lax.ppermute(rows, "dp", shift))
-        sources.append((own - 2 * k) % dp_count)
-    mine = jnp.concatenate(parts, axis=0)
-    other = lax.ppermute(mine, "dp", [(i, i ^ 1) for i in range(dp_count)])
-    sources = sources + [s ^ 1 for s in sources]
-    return jnp.concatenate([mine, other], axis=0), jnp.stack(sources).astype(jnp.int32)
-
-
 def sum_over(values, axis, count):
     pieces = values.reshape((count, values.shape[0] // count) + values.shape[1:])
     pieces = lax.all_to_all(pieces, axis, 0, 0, tiled=False)
@@ -135,8 +121,8 @@
     table = land_blocks.reshape(dp_count, land_count, own_blocks, LAND_ACTIVE)
     own_table = lax.dynamic_index_in_dim(table, lax.axis_index("land"), axis=1, keepdims=False)
     own_table = own_table.reshape(dp_count * own_blocks, LAND_ACTIVE)
-    land_rows, sources = gather_rows(jnp.concatenate([land_values, coefficients], axis=1), dp_count)
-    own_table = own_table[sources]
+    land_rows = lax.all_gather(
+        jnp.concatenate([land_values, coefficients], axis=1), "dp", axis=0, tiled=True)
     doc_tiles = doc_values.reshape(doc_count, DOC_BLOCK, ACTIVE, TERM_BLOCK).transpose(0, 2, 1, 3)
     doc_tiles = jnp.pad(doc_tiles, ((0, 0), (0, 1), (0, 0), (0, 0)))
     doc_tiles = doc_tiles.reshape(doc_count * (ACTIVE + 1), DOC_BLOCK, TERM_BLOCK)
@@ -149,9 +135,7 @@
     summed = jnp.dot(tile_high.T, fitted_pair, preferred_element_type=jnp.float32)
     summed = summed + jnp.dot(tile_low.T, fitted_pair, preferred_element_type=jnp.float32)
     summed = summed[:, :targets] + summed[:, targets:]
-    order = jnp.argsort(sources)
-    summed = summed.reshape(dp_count, own_blocks * LM_BLOCK, targets)[order]
-    result = sum_over(summed.reshape(-1, targets), "dp", dp_count)
+    result = sum_over(summed, "dp", dp_count)
     return result / total_docs
 
 

time: 148 us -> 142 us (0.959)
  local copies, waits for them, and re-layouts: 27.3 us -> 10.5 us
  between operations: 0.23 us -> 13.6 us
  waiting for transfers between devices: 21.4 us -> 32.7 us
  starting transfers between devices: 9.5 us -> 0.01 us
  blocking collectives: 49.9 us -> 45 us
    all_gather x0 -> x1, waiting for transfers between devices: none -> 32.7 us  [on_device(): lax.all_gather(jnp.concatenate([land_values, coefficients], axis=1), 'dp'...]
    ppermute x8 -> x0, waiting for transfers between devices: 21.4 us -> none  [the longest x7 21.4 us: gather_rows(): parts.append(lax.ppermute(rows, 'dp', shift))]
    ppermute x8 -> x0, starting transfers between devices: 9.5 us -> none  [the longest x7 9.01 us: gather_rows(): parts.append(lax.ppermute(rows, 'dp', shift))]
    concatenate x3 -> x0, local copies, waits for them, and re-layouts: 8.46 us -> none  [the longest x2 5.14 us: gather_rows(): mine = jnp.concatenate(parts, axis=0)]
    all_to_all x2, blocking collectives: 37.3 us -> 31.6 us  [sum_over(): pieces = lax.all_to_all(pieces, axis, 0, 0, tiled=False)]
    ppermute x1 -> x0, local copies, waits for them, and re-layouts: 4.21 us -> none  [gather_rows(): other = lax.ppermute(mine, 'dp', [(i, i ^ 1) for i in range(dp_count)])]
    unnamed x23 -> x13, local copies, waits for them, and re-layouts: 8.07 us -> 4.69 us
    dot_general x1, matrix products: 3.92 us -> 1.03 us  [on_device(): jnp.dot(tile_low.T, fitted_pair, preferred_element_type=jnp.float32)]
  transfers between devices with their start and end apart: 8 -> 1, of which waited for: 4 -> 1; matrix products, arithmetic and copies ran while one was open for 9% -> 6% of each run, Pallas kernels for 0% -> 0%
where the time goes in v3:
time: 142 us; the launch traced here: 141 us
  blocking collectives  45 us (32%)
  waiting for transfers between devices  32.7 us (23%)
  Pallas kernels  28.5 us (20%)
  between operations  13.6 us (10%)
  local copies, waits for them, and re-layouts  10.5 us (7%)
  other arithmetic  6.12 us (4%)
  matrix products  4.95 us (3%)
    all_gather x1, waiting for transfers between devices, on_device(): lax.all_gather(jnp.concatenate([land_values, coefficients], axis=1), 'dp'...  32.7 us
    all_to_all x2, blocking collectives, sum_over(): pieces = lax.all_to_all(pieces, axis, 0, 0, tiled=False)  31.6 us
    pallas_call x1, Pallas kernels, forward(): pl.pallas_call(forward_kernel, grid_spec=grid_spec, out_shape=[jax.ShapeD...  28.5 us
    all_to_all x1, blocking collectives, all_sum(): return lax.all_to_all(spread, axis, 0, 0, tiled=False).reshape(values.shape)  13.4 us
    unnamed x13, local copies, waits for them, and re-layouts  4.69 us
    dot_general x1, matrix products, on_device(): jnp.dot(tile_high.T, fitted_pair, preferred_element_type=jnp.float32)  3.92 us
  transfers between devices with their start and end apart: 1, of which 1 were waited for; matrix products, arithmetic and copies ran while one was open for 6% of the time, Pallas kernels for 0%

profile of v3, /device:TPU:1, one launch (start us, length us, event | category | flops | bytes accessed | tf_op | source)
XLA Modules:
  0.0 141.3 jit_solution(13265710790515180667)
XLA Ops:
  6.5 1.0 copy.38
  7.5 1.7 %pad_maximum_fusion.1 = bf16[128,1088]{1,0:T(8,128)(2,1)} fusion(bf16[128,64]{1,0:T(8,128)(2,1)S(1)} %copy.38, bf16[128,1024]{1,0:T(8,128)(2,1)} %param.7), kind=kLoop, calls=%fused_computation.10 | loop fusion | flops 557056 | bytes 557056 | tf_op jit(solution)/shard_map/concatenate | solution.py:125
  9.2 0.0 all-gather.2.cloned.1.call-update
  9.2 0.8 copy.35
  10.0 0.8 reshape.37
  10.8 0.3 dynamic-slice_reduce_fusion
  11.1 0.2 compare_reduce_fusion.1
  11.3 0.8 compare_reduce_fusion
  12.1 0.1 copy.36
  12.2 0.1 reshape.38.slot_ref
  12.3 2.6 %multiply_reduce_fusion = f32[1536]{0:T(1024)S(1)} fusion(bf16[1536,1024]{1,0:T(8,128)(2,1)} %param.5), kind=kLoop, calls=%fused_computation | loop fusion | flops 4717056 | bytes 3151872 | tf_op jit(solution)/shard_map/reduce_sum | solution.py:120
  14.9 1.1 rsqrt.15.dn_ref
  16.1 0.8 copy.44
  16.9 0.9 copy.47
  17.8 0.5 pad.4
  18.3 32.7 %all-gather.2.cloned.1.call-done.land_ref = bf16[2048,1088]{1,0:T(8,128)(2,1)} async-done(((bf16[128,1088]{1,0:T(8,128)(2,1)}), bf16[2048,1088]{1,0:T(8,128)(2,1)}) %all-gather.2.cloned.1.call-update) | async-done | bytes 4456464 | tf_op jit(solution)/shard_map/all_gather | solution.py:124
  51.0 1.1 copy-done
  52.1 28.5 %shard_map.55 = (bf16[1536,2048]{1,0:T(8,128)(2,1)}, bf16[1536,2048]{1,0:T(8,128)(2,1)}, f32[1536,64]{1,0:T(8,128)S(1)}) custom-call(s32[1536]{0:T(1024)S(1)} %reshape.38.slot_ref, bf16[108,128,128]{2,1,0:T(8,128)(2,1)S(1)} %bitcast.19, f32[1536,1]{1,0:T(8,128)S(1)} %copy-done, bf16[2048,1088]{1,0:T(8,128)(2,1)} %all-gather.2.cloned.1.call-done.land_ref), custom_call_target="tpu_custom_call" | custom-call | tf_op jit(solution)/shard_map/pallas_call | solution.py:87
  80.6 0.9 copy-done.1
  81.5 1.4 %copy.40 = f32[8,192,64]{1,2,0:T(8,128)S(1)} copy(f32[8,192,64]{2,1,0:T(8,128)} %bitcast.20) | data formatting | bytes 786432 | tf_op jit(solution)/shard_map/reshape | solution.py:101
  83.0 16.0 %all_to_all.15 = f32[8,192,64]{1,2,0:T(8,128)S(1)} all-to-all(f32[8,192,64]{1,2,0:T(8,128)S(1)} %copy.40), channel_id=1, replica_groups=mesh['dp'=16,'land'=8] {'land'}, dimensions={0} | all-to-all | bytes 786432 | tf_op jit(solution)/shard_map/all_to_all | solution.py:102
  99.0 0.0 slice-start
  99.1 13.4 %all_to_all.16 = f32[8,192,64]{1,2,0:T(8,128)S(1)} all-to-all(f32[8,192,64]{1,2,0:T(8,128)S(1)} %broadcast_in_dim.12), channel_id=1, replica_groups=mesh['dp'=16,'land'=8] {'land'}, dimensions={0} | all-to-all | bytes 786432 | tf_op jit(solution)/shard_map/all_to_all | solution.py:109
  112.5 0.3 copy.41
  112.8 0.2 reshape.42
  113.1 0.0 slice-start.1
  113.1 3.9 %fusion.1 = f32[2048,128]{0,1:T(8,128)S(1)} fusion(bf16[1536,2048]{1,0:T(8,128)(2,1)} %get-tuple-element.10, bf16[1536,64]{0,1:T(8,128)(2,1)S(1)} %subtract_convert_fusion, bf16[1536,64]{0,1:T(8,128)(2,1)S(1)} %convert_element_type.15), kind=kOutput, calls=%fused_computation.11 | convolution fusion | flops 806092800 | bytes 7733248 | tf_op jit(solution)/shard_map/dot_general | solution.py:135
  117.0 0.1 slice-done.1
  117.1 1.0 convolution_add_fusion
  118.1 0.1 copy_bitcast_fusion.1
  118.2 15.6 %all_to_all.17 = f32[16,128,64]{1,2,0:T(8,128)S(1)} all-to-all(f32[16,128,64]{1,2,0:T(8,128)S(1)} %copy_bitcast_fusion.1), channel_id=1, replica_groups=mesh['dp'=16,'land'=8] {'dp'}, dimensions={0} | all-to-all | bytes 1048576 | tf_op jit(solution)/shard_map/all_to_all | solution.py:102
  133.8 0.6 broadcast_multiply_fusion
  (14 shorter events, 0.2 us)
Async XLA Ops:
  6.5 9.5 %copy-start.2 = (bf16[1536,1024]{1,0:T(8,128)(2,1)S(1)}, bf16[1536,1024]{1,0:T(8,128)(2,1)}, u32[]{:S(2)}) copy-start(bf16[1536,1024]{1,0:T(8,128)(2,1)} %param.5) | copy-start | bytes 9437188
  6.5 44.5 %all-gather.2.cloned.1.call-start = ((), (), s32[]{:S(2)}) async-start(), calls=%async_computation.3 | async-start | bytes 5013504 | tf_op jit(solution)/shard_map/all_gather | solution.py:124
  51.0 1.1 copy-start
  80.6 0.9 copy-start.1
  99.0 18.0 %slice-start = ((s8[6291456]{0:T(1024)(128)(4,1)}), s8[2097152]{0:T(1024)(128)(4,1)S(1)}, s32[]{:S(2)}) async-start(s8[6291456]{0:T(1024)(128)(4,1)} %bitcast.21), calls=%async_computation.4 | async-start | bytes 4194304
  113.1 4.0 %slice-start.1 = ((s8[6291456]{0:T(1024)(128)(4,1)}), s8[4194304]{0:T(1024)(128)(4,1)S(1)}, s32[]{:S(2)}) async-start(s8[6291456]{0:T(1024)(128)(4,1)} %bitcast.21), calls=%async_computation.5 | async-start | bytes 8388608
Sparse Core Ops, SparseCore 0:
  9.4 41.5 all-gather.1

commit v4 on v3

--- a/solution.py
+++ b/solution.py
@@ -121,21 +121,35 @@
     table = land_blocks.reshape(dp_count, land_count, own_blocks, LAND_ACTIVE)
     own_table = lax.dynamic_index_in_dim(table, lax.axis_index("land"), axis=1, keepdims=False)
     own_table = own_table.reshape(dp_count * own_blocks, LAND_ACTIVE)
-    land_rows = lax.all_gather(
-        jnp.concatenate([land_values, coefficients], axis=1), "dp", axis=0, tiled=True)
+    rows = jnp.concatenate([land_values, coefficients], axis=1)
+    core = lax.axis_index("dp") % 2
+    groups = [list(range(c, dp_count, 2)) for c in range(2)]
+    mine = lax.all_gather(rows, "dp", axis=0, tiled=True, axis_index_groups=groups)
+    other = lax.ppermute(mine, "dp", [(i, i ^ 1) for i in range(dp_count)])
+    half = dp_count // 2
+    sources = jnp.concatenate([core + 2 * jnp.arange(half), (1 - core) + 2 * jnp.arange(half)])
+    own_table = own_table.reshape(dp_count, own_blocks, LAND_ACTIVE)[sources]
+    own_table = own_table.reshape(-1, LAND_ACTIVE)
+    split = half * own_blocks
     doc_tiles = doc_values.reshape(doc_count, DOC_BLOCK, ACTIVE, TERM_BLOCK).transpose(0, 2, 1, 3)
     doc_tiles = jnp.pad(doc_tiles, ((0, 0), (0, 1), (0, 0), (0, 0)))
     doc_tiles = doc_tiles.reshape(doc_count * (ACTIVE + 1), DOC_BLOCK, TERM_BLOCK)
-    slots = match_table(doc_blocks, own_table)
-    tile_high, tile_low, fitted = forward(
-        slots, doc_tiles, doc_norm.reshape(doc_rows, 1), land_rows, targets)
-    fitted = all_sum(fitted, "land", land_count)
+    doc_norm = doc_norm.reshape(doc_rows, 1)
+    high_one, low_one, fitted_one = forward(
+        match_table(doc_blocks, own_table[:split]), doc_tiles, doc_norm, mine, targets)
+    high_two, low_two, fitted_two = forward(
+        match_table(doc_blocks, own_table[split:]), doc_tiles, doc_norm, other, targets)
+    fitted = all_sum(fitted_one + fitted_two, "land", land_count)
     fitted_high, fitted_low = split_pair(fitted)
     fitted_pair = jnp.concatenate([fitted_high, fitted_low], axis=1)
-    summed = jnp.dot(tile_high.T, fitted_pair, preferred_element_type=jnp.float32)
-    summed = summed + jnp.dot(tile_low.T, fitted_pair, preferred_element_type=jnp.float32)
-    summed = summed[:, :targets] + summed[:, targets:]
-    result = sum_over(summed, "dp", dp_count)
+    summed = []
+    for tile_high, tile_low in ((high_one, low_one), (high_two, low_two)):
+        part = jnp.dot(tile_high.T, fitted_pair, preferred_element_type=jnp.float32)
+        part = part + jnp.dot(tile_low.T, fitted_pair, preferred_element_type=jnp.float32)
+        summed.append(part[:, :targets] + part[:, targets:])
+    summed = jnp.concatenate(summed, axis=0).reshape(dp_count, -1, targets)
+    summed = summed[jnp.argsort(sources)]
+    result = sum_over(summed.reshape(-1, targets), "dp", dp_count)
     return result / total_docs
 
 

time: 142 us -> 187 us (1.32)
  waiting for transfers between devices: 32.7 us -> 77.6 us
  blocking collectives: 45 us -> 14.9 us
  local copies, waits for them, and re-layouts: 10.5 us -> 25.8 us
  starting transfers between devices: 0.01 us -> 10.8 us
  Pallas kernels: 28.5 us -> 32.7 us
    all_gather x1, waiting for transfers between devices: 32.7 us -> 59.3 us  [on_device(): lax.all_gather(rows, 'dp', axis=0, tiled=True, axis_index_groups=groups)]
    all_to_all x0 -> x2, waiting for transfers between devices: none -> 18.3 us  [the longest x1 10.4 us: sum_over(): pieces = lax.all_to_all(pieces, axis, 0, 0, tiled=False)]
    all_to_all x2 -> x1, blocking collectives: 31.6 us -> 14.9 us  [sum_over(): pieces = lax.all_to_all(pieces, axis, 0, 0, tiled=False)]
    all_to_all x1 -> x0, blocking collectives: 13.4 us -> none  [all_sum(): return lax.all_to_all(spread, axis, 0, 0, tiled=False).reshape(values.shape)]
    all_to_all x0 -> x2, starting transfers between devices: none -> 9.63 us  [the longest x1 6.13 us: sum_over(): pieces = lax.all_to_all(pieces, axis, 0, 0, tiled=False)]
    all_gather x0 -> x1, local copies, waits for them, and re-layouts: none -> 4.22 us  [on_device(): lax.all_gather(rows, 'dp', axis=0, tiled=True, axis_index_groups=groups)]
    pallas_call x1 -> x2, Pallas kernels: 28.5 us -> 32.7 us  [forward(): pl.pallas_call(forward_kernel, grid_spec=grid_spec, out_shape=[jax.ShapeD...]
    pad x1, local copies, waits for them, and re-layouts: 0.53 us -> 4.35 us  [on_device(): doc_tiles = jnp.pad(doc_tiles, ((0, 0), (0, 1), (0, 0), (0, 0)))]
  transfers between devices with their start and end apart: 1 -> 4, of which waited for: 1 -> 3; matrix products, arithmetic and copies ran while one was open for 6% -> 7% of each run, Pallas kernels for 0% -> 9%
where the time goes in v4:
time: 187 us; the launch traced here: 186 us
  waiting for transfers between devices  77.6 us (41%)
  Pallas kernels  32.7 us (17%)
  local copies, waits for them, and re-layouts  25.8 us (14%)
  blocking collectives  14.9 us (8%)
  between operations  13.6 us (7%)
  starting transfers between devices  10.8 us (6%)
  other arithmetic  6.43 us (3%)
  matrix products  4.21 us (2%)
    all_gather x1, waiting for transfers between devices, on_device(): lax.all_gather(rows, 'dp', axis=0, tiled=True, axis_index_groups=groups)  59.3 us
    pallas_call x2, Pallas kernels, forward(): pl.pallas_call(forward_kernel, grid_spec=grid_spec, out_shape=[jax.ShapeD...  32.7 us
    all_to_all x1, blocking collectives, sum_over(): pieces = lax.all_to_all(pieces, axis, 0, 0, tiled=False)  14.9 us
    all_to_all x1, waiting for transfers between devices, sum_over(): pieces = lax.all_to_all(pieces, axis, 0, 0, tiled=False)  10.4 us
    all_to_all x1, waiting for transfers between devices, all_sum(): return lax.all_to_all(spread, axis, 0, 0, tiled=False).reshape(values.shape)  7.85 us
    all_to_all x1, starting transfers between devices, sum_over(): pieces = lax.all_to_all(pieces, axis, 0, 0, tiled=False)  6.13 us
    unnamed x18, local copies, waits for them, and re-layouts  4.46 us
    pad x1, local copies, waits for them, and re-layouts, on_device(): doc_tiles = jnp.pad(doc_tiles, ((0, 0), (0, 1), (0, 0), (0, 0)))  4.35 us
  transfers between devices with their start and end apart: 4, of which 3 were waited for; matrix products, arithmetic and copies ran while one was open for 7% of the time, Pallas kernels for 9%

profile of v4, /device:TPU:1, one launch (start us, length us, event | category | flops | bytes accessed | tf_op | source)
XLA Modules:
  0.0 186.1 jit_solution(9354943898309179483)
XLA Ops:
  6.5 1.0 copy.48
  7.5 1.7 pad_maximum_fusion.1
  9.2 0.8 reshape.100
  10.0 59.3 %all-gather.2.cloned.1.call-done.land_ref = bf16[1024,1088]{1,0:T(8,128)(2,1)} async-done(((bf16[128,1088]{1,0:T(8,128)(2,1)}), bf16[1024,1088]{1,0:T(8,128)(2,1)}) %all-gather.2.cloned.1.call-update) | async-done | bytes 2228240 | tf_op jit(solution)/shard_map/all_gather | solution.py:127
  69.3 4.2 %copy.51 = bf16[1024,1088]{0,1:T(8,128)(2,1)} copy(bf16[1024,1088]{1,0:T(8,128)(2,1)} %all-gather.2.cloned.1.call-done.land_ref) | data formatting | bytes 4456448 | tf_op jit(solution)/shard_map/all_gather | solution.py:127
  73.5 1.2 collective-permute-start
  75.8 0.8 compare_reduce_fusion
  76.8 0.8 copy.59
  77.6 2.6 %copy.62 = bf16[12,128,8,128]{3,1,2,0:T(8,128)(2,1)} copy(bf16[12,128,8,128]{3,2,1,0:T(8,128)(2,1)S(1)} %bitcast.32) | data formatting | bytes 6291456 | tf_op jit(solution)/shard_map/reshape | solution.py:134
  80.2 0.7 multiply_reduce_fusion
  81.1 0.8 compare_reduce_fusion.2
  82.1 4.3 %pad.4 = bf16[12,9,128,128]{3,2,1,0:T(8,128)(2,1)} pad(bf16[12,8,128,128]{3,2,1,0:T(8,128)(2,1)} %bitcast.31, bf16[]{:T(256)} %constant.47.clone.1), padding=0_0x0_1x0_0x0_0 | pad | bytes 6684674 | tf_op jit(solution)/shard_map/jit(_pad)/pad | solution.py:135
  86.5 16.3 %shard_map.55 = (bf16[1536,1024]{1,0:T(8,128)(2,1)}, bf16[1536,1024]{1,0:T(8,128)(2,1)}, f32[1536,64]{1,0:T(8,128)S(1)}) custom-call(s32[768]{0:T(1024)S(1)} %reshape.101.slot_ref, bf16[108,128,128]{2,1,0:T(8,128)(2,1)} %bitcast.28, f32[1536,1]{1,0:T(8,128)S(1)} %rsqrt.15.dn_ref, bf16[1024,1088]{1,0:T(8,128)(2,1)S(1)} %copy-done), custom_call_target="tpu_custom_call" | custom-call | tf_op jit(solution)/shard_map/pallas_call | solution.py:87
  102.8 0.9 copy-done.1
  103.7 3.0 %copy.53.land_ref = bf16[1024,1088]{1,0:T(8,128)(2,1)S(1)} copy(bf16[1024,1088]{0,1:T(8,128)(2,1)} %collective-permute-done) | data formatting | bytes 4456448 | tf_op jit(solution)/shard_map/ppermute | solution.py:128
  106.7 16.4 %shard_map.56 = (bf16[1536,1024]{1,0:T(8,128)(2,1)}, bf16[1536,1024]{1,0:T(8,128)(2,1)}, f32[1536,64]{1,0:T(8,128)S(1)}) custom-call(s32[768]{0:T(1024)S(1)} %reshape.104.slot_ref, bf16[108,128,128]{2,1,0:T(8,128)(2,1)} %bitcast.29, f32[1536,1]{1,0:T(8,128)S(1)} %rsqrt.15.dn_ref, bf16[1024,1088]{1,0:T(8,128)(2,1)S(1)} %copy.53.land_ref), custom_call_target="tpu_custom_call" | custom-call | tf_op jit(solution)/shard_map/pallas_call | solution.py:87
  123.1 1.1 copy.54
  124.2 6.1 %all-to-all-start = ((f32[8,192,64]{1,2,0:T(8,128)}), f32[8,192,64]{1,2,0:T(8,128)S(1)}, u32[]{:S(2)}, u32[]{:S(2)}) async-start(f32[8,192,64]{1,2,0:T(8,128)} %copy.54), calls=%async_computation | async-start | bytes 1048576 | tf_op jit(solution)/shard_map/all_to_all | solution.py:102
  130.4 10.4 %all-to-all-done = f32[8,192,64]{1,2,0:T(8,128)S(1)} async-done(((f32[8,192,64]{1,2,0:T(8,128)}), f32[8,192,64]{1,2,0:T(8,128)S(1)}, u32[]{:S(2)}, u32[]{:S(2)}) %all-to-all-start) | async-done | bytes 393248 | tf_op jit(solution)/shard_map/all_to_all | solution.py:102
  140.9 0.8 broadcast_in_dim.10
  141.7 3.5 %all-to-all-start.1 = ((f32[8,192,64]{1,2,0:T(8,128)}), f32[8,192,64]{1,2,0:T(8,128)S(1)}, u32[]{:S(2)}, u32[]{:S(2)}) async-start(f32[8,192,64]{1,2,0:T(8,128)} %broadcast_in_dim.10), calls=%async_computation.1 | async-start | bytes 1048576 | tf_op jit(solution)/shard_map/all_to_all | solution.py:109
  145.3 1.2 sort.17
  146.5 7.8 %all-to-all-done.1 = f32[8,192,64]{1,2,0:T(8,128)S(1)} async-done(((f32[8,192,64]{1,2,0:T(8,128)}), f32[8,192,64]{1,2,0:T(8,128)S(1)}, u32[]{:S(2)}, u32[]{:S(2)}) %all-to-all-start.1) | async-done | bytes 393248 | tf_op jit(solution)/shard_map/all_to_all | solution.py:109
  154.4 1.1 copy.55
  155.5 1.4 reshape.106
  156.9 2.5 %fusion.5 = f32[1024,128]{0,1:T(8,128)S(1)} fusion(bf16[1536,1024]{1,0:T(8,128)(2,1)} %get-tuple-element.15, bf16[1536,64]{0,1:T(8,128)(2,1)S(1)} %subtract_convert_fusion, bf16[1536,64]{0,1:T(8,128)(2,1)S(1)} %convert_element_type.15), kind=kOutput, calls=%fused_computation.33 | convolution fusion | flops 403439616 | bytes 4063232 | tf_op jit(solution)/shard_map/dot_general | solution.py:147
  159.4 0.6 convolution_add_fusion.1
  160.1 1.2 copy-done.6
  162.4 0.6 convolution_add_fusion
  163.1 0.6 gather_fusion.1
  163.7 14.9 %all_to_all.15 = f32[16,128,64]{1,2,0:T(8,128)S(1)} all-to-all(f32[16,128,64]{1,2,0:T(8,128)S(1)} %gather_fusion.1), channel_id=1, replica_groups=mesh['dp'=16,'land'=8] {'dp'}, dimensions={0} | all-to-all | bytes 1048576 | tf_op jit(solution)/shard_map/all_to_all | solution.py:102
  178.6 0.6 broadcast_multiply_fusion
  (47 shorter events, 3.3 us)
Async XLA Ops:
  6.5 69.1 %copy-start.7 = (s32[12,8]{0,1:T(8,128)S(1)}, s32[12,8]{0,1:T(8,128)}, u32[]{:S(2)}) copy-start(s32[12,8]{0,1:T(8,128)} %param.6) | copy-start | bytes 1156
  6.5 70.2 %copy-start.3 = (bf16[1536,1024]{1,0:T(8,128)(2,1)S(1)}, bf16[1536,1024]{1,0:T(8,128)(2,1)}, u32[]{:S(2)}) copy-start(bf16[1536,1024]{1,0:T(8,128)(2,1)} %param.5) | copy-start | bytes 9437188
  6.5 62.8 %all-gather.2.cloned.1.call-start = ((), (), s32[]{:S(2)}) async-start(), calls=%async_computation.3 | async-start | bytes 2654208 | tf_op jit(solution)/shard_map/all_gather | solution.py:127
  73.5 30.2 %collective-permute-start = (bf16[1024,1088]{0,1:T(8,128)(2,1)}, bf16[1024,1088]{0,1:T(8,128)(2,1)}, u32[]{:S(2)}, u32[]{:S(2)}) collective-permute-start(bf16[1024,1088]{0,1:T(8,128)(2,1)} %copy.51), channel_id=1, source_target_pairs={{0,8},{8,0},{16,24},{24,16},{32,40},{40,32},{48,56},{56,48},{64,72... | collective-permute-start | bytes 6684680 | tf_op jit(solution)/shard_map/ppermute | solution.py:128
  82.1 4.4 %copy-start = (bf16[1024,1088]{1,0:T(8,128)(2,1)S(1)}, bf16[1024,1088]{1,0:T(8,128)(2,1)}, u32[]{:S(2)}) copy-start(bf16[1024,1088]{1,0:T(8,128)(2,1)} %all-gather.2.cloned.1.call-done.land_ref) | copy-start | bytes 6684676
  102.8 0.9 copy-start.1
  106.7 16.4 %copy-start.2 = (f32[1536,64]{1,0:T(8,128)S(1)}, f32[1536,64]{1,0:T(8,128)}, u32[]{:S(2)}) copy-start(f32[1536,64]{1,0:T(8,128)} %copy-done.1) | copy-start | bytes 1179652
  124.2 16.6 %all-to-all-start = ((f32[8,192,64]{1,2,0:T(8,128)}), f32[8,192,64]{1,2,0:T(8,128)S(1)}, u32[]{:S(2)}, u32[]{:S(2)}) async-start(f32[8,192,64]{1,2,0:T(8,128)} %copy.54), calls=%async_computation | async-start | bytes 1048576 | tf_op jit(solution)/shard_map/all_to_all | solution.py:102
  141.7 12.7 %all-to-all-start.1 = ((f32[8,192,64]{1,2,0:T(8,128)}), f32[8,192,64]{1,2,0:T(8,128)S(1)}, u32[]{:S(2)}, u32[]{:S(2)}) async-start(f32[8,192,64]{1,2,0:T(8,128)} %broadcast_in_dim.10), calls=%async_computation.1 | async-start | bytes 1048576 | tf_op jit(solution)/shard_map/all_to_all | solution.py:109
  155.5 3.9 %copy-start.4 = (bf16[1536,1024]{1,0:T(8,128)(2,1)S(1)}, bf16[1536,1024]{1,0:T(8,128)(2,1)}, u32[]{:S(2)}) copy-start(bf16[1536,1024]{1,0:T(8,128)(2,1)} %get-tuple-element.19) | copy-start | bytes 9437188
  159.4 1.9 %copy-start.6 = (bf16[1536,1024]{1,0:T(8,128)(2,1)S(1)}, bf16[1536,1024]{1,0:T(8,128)(2,1)}, u32[]{:S(2)}) copy-start(bf16[1536,1024]{1,0:T(8,128)(2,1)} %get-tuple-element.21) | copy-start | bytes 9437188
  160.0 2.4 %copy-start.5 = (bf16[1536,1024]{1,0:T(8,128)(2,1)S(1)}, bf16[1536,1024]{1,0:T(8,128)(2,1)}, u32[]{:S(2)}) copy-start(bf16[1536,1024]{1,0:T(8,128)(2,1)} %get-tuple-element.20) | copy-start | bytes 9437188
Sparse Core Ops, SparseCore 0:
  9.4 59.8 all-gather.1

commit v5 on v3

--- a/solution.py
+++ b/solution.py
@@ -126,14 +126,21 @@
     doc_tiles = doc_values.reshape(doc_count, DOC_BLOCK, ACTIVE, TERM_BLOCK).transpose(0, 2, 1, 3)
     doc_tiles = jnp.pad(doc_tiles, ((0, 0), (0, 1), (0, 0), (0, 0)))
     doc_tiles = doc_tiles.reshape(doc_count * (ACTIVE + 1), DOC_BLOCK, TERM_BLOCK)
-    slots = match_table(doc_blocks, own_table)
-    tile_high, tile_low, fitted = forward(
-        slots, doc_tiles, doc_norm.reshape(doc_rows, 1), land_rows, targets)
-    fitted = all_sum(fitted, "land", land_count)
-    fitted_high, fitted_low = split_pair(fitted)
-    fitted_pair = jnp.concatenate([fitted_high, fitted_low], axis=1)
-    summed = jnp.dot(tile_high.T, fitted_pair, preferred_element_type=jnp.float32)
-    summed = summed + jnp.dot(tile_low.T, fitted_pair, preferred_element_type=jnp.float32)
+    doc_norm = doc_norm.reshape(doc_rows, 1)
+    halves = 2
+    step = doc_count // halves
+    summed = None
+    for h in range(halves):
+        lo, hi = h * step, (h + 1) * step
+        tile_high, tile_low, fitted = forward(
+            match_table(doc_blocks[lo:hi], own_table), doc_tiles[lo * (ACTIVE + 1):hi * (ACTIVE + 1)],
+            doc_norm[lo * DOC_BLOCK:hi * DOC_BLOCK], land_rows, targets)
+        fitted = all_sum(fitted, "land", land_count)
+        fitted_high, fitted_low = split_pair(fitted)
+        fitted_pair = jnp.concatenate([fitted_high, fitted_low], axis=1)
+        part = jnp.dot(tile_high.T, fitted_pair, preferred_element_type=jnp.float32)
+        part = part + jnp.dot(tile_low.T, fitted_pair, preferred_element_type=jnp.float32)
+        summed = part if summed is None else summed + part
     summed = summed[:, :targets] + summed[:, targets:]
     result = sum_over(summed, "dp", dp_count)
     return result / total_docs

time: 142 us -> 177 us (1.25)
  blocking collectives: 45 us -> 17.8 us
  starting transfers between devices: 0.01 us -> 20.5 us
  waiting for transfers between devices: 32.7 us -> 49.6 us
  local copies, waits for them, and re-layouts: 10.5 us -> 26.7 us
  Pallas kernels: 28.5 us -> 38.2 us
  matrix products: 4.95 us -> 2.37 us
    all_to_all x0 -> x4, starting transfers between devices: none -> 20.5 us  [the longest x2 13.1 us: sum_over(): pieces = lax.all_to_all(pieces, axis, 0, 0, tiled=False)]
    all_to_all x0 -> x4, waiting for transfers between devices: none -> 19 us  [the longest x2 11.6 us: all_sum(): return lax.all_to_all(spread, axis, 0, 0, tiled=False).reshape(values.shape)]
    all_to_all x2 -> x1, blocking collectives: 31.6 us -> 17.8 us  [sum_over(): pieces = lax.all_to_all(pieces, axis, 0, 0, tiled=False)]
    all_to_all x1 -> x0, blocking collectives: 13.4 us -> none  [all_sum(): return lax.all_to_all(spread, axis, 0, 0, tiled=False).reshape(values.shape)]
    pallas_call x1 -> x2, Pallas kernels: 28.5 us -> 38.2 us  [forward(): pl.pallas_call(forward_kernel, grid_spec=grid_spec, out_shape=[jax.ShapeD...]
    unnamed x13 -> x20, local copies, waits for them, and re-layouts: 4.69 us -> 12.3 us
    dot_general x1 -> x2, matrix products: 3.92 us -> 1.16 us  [on_device(): part = jnp.dot(tile_high.T, fitted_pair, preferred_element_type=jnp.float32)]
    all_to_all x1 -> x2, local copies, waits for them, and re-layouts: 0.31 us -> 2.67 us  [all_sum(): return lax.all_to_all(spread, axis, 0, 0, tiled=False).reshape(values.shape)]
  transfers between devices with their start and end apart: 1 -> 5, of which waited for: 1 -> 4; matrix products, arithmetic and copies ran while one was open for 6% -> 9% of each run, Pallas kernels for 0% -> 11%
where the time goes in v5:
time: 177 us; the launch traced here: 175 us
  waiting for transfers between devices  49.6 us (28%)
  Pallas kernels  38.2 us (22%)
  local copies, waits for them, and re-layouts  26.7 us (15%)
  starting transfers between devices  20.5 us (12%)
  blocking collectives  17.8 us (10%)
  between operations  13.6 us (8%)
  other arithmetic  6.52 us (4%)
  matrix products  2.37 us (1%)
    pallas_call x2, Pallas kernels, forward(): pl.pallas_call(forward_kernel, grid_spec=grid_spec, out_shape=[jax.ShapeD...  38.2 us
    all_gather x1, waiting for transfers between devices, on_device(): lax.all_gather(jnp.concatenate([land_values, coefficients], axis=1), 'dp'...  30.6 us
    all_to_all x1, blocking collectives, sum_over(): pieces = lax.all_to_all(pieces, axis, 0, 0, tiled=False)  17.8 us
    all_to_all x2, starting transfers between devices, sum_over(): pieces = lax.all_to_all(pieces, axis, 0, 0, tiled=False)  13.1 us
    unnamed x20, local copies, waits for them, and re-layouts  12.3 us
    all_to_all x2, waiting for transfers between devices, all_sum(): return lax.all_to_all(spread, axis, 0, 0, tiled=False).reshape(values.shape)  11.6 us
    all_to_all x2, starting transfers between devices, all_sum(): return lax.all_to_all(spread, axis, 0, 0, tiled=False).reshape(values.shape)  7.45 us
    all_to_all x2, waiting for transfers between devices, sum_over(): pieces = lax.all_to_all(pieces, axis, 0, 0, tiled=False)  7.37 us
  transfers between devices with their start and end apart: 5, of which 4 were waited for; matrix products, arithmetic and copies ran while one was open for 9% of the time, Pallas kernels for 11%

profile of v5, /device:TPU:1, one launch (start us, length us, event | category | flops | bytes accessed | tf_op | source)
XLA Modules:
  0.0 175.3 jit_solution(5188025715787909885)
XLA Ops:
  6.5 0.8 copy.50
  7.4 1.7 pad_maximum_fusion
  9.1 0.8 fusion.9
  11.3 0.8 compare_reduce_fusion
  13.7 2.7 %copy.61 = bf16[192,8,8,128]{3,2,1,0:T(8,128)(2,1)S(1)} copy(bf16[192,8,8,128]{3,1,2,0:T(8,128)(2,1)} %bitcast.29) | data formatting | bytes 6291456
  16.4 0.9 copy.64
  17.3 1.0 copy-done.6
  19.0 0.9 slice.48.dn_ref
  20.2 30.6 %all-gather.2.cloned.1.call-done.land_ref = bf16[2048,1088]{1,0:T(8,128)(2,1)} async-done(((bf16[128,1088]{1,0:T(8,128)(2,1)}), bf16[2048,1088]{1,0:T(8,128)(2,1)}) %all-gather.2.cloned.1.call-update) | async-done | bytes 4456464 | tf_op jit(solution)/shard_map/all_gather | solution.py:124
  50.8 1.0 copy-done.4
  51.8 19.3 %shard_map.55 = (bf16[768,2048]{1,0:T(8,128)(2,1)S(1)}, bf16[768,2048]{1,0:T(8,128)(2,1)}, f32[768,64]{1,0:T(8,128)S(1)}) custom-call(s32[768]{0:T(1024)S(1)} %reshape.38.slot_ref, bf16[54,128,128]{2,1,0:T(8,128)(2,1)S(1)} %bitcast.26, f32[768,1]{1,0:T(8,128)S(1)} %copy-done.4, bf16[2048,1088]{1,0:T(8,128)(2,1)} %all-gather.2.cloned.1.call-done.land_ref), custom_call_target="tpu_custom_call" | custom-call | tf_op jit(solution)/shard_map/pallas_call | solution.py:87
  71.1 1.7 copy-done
  73.6 1.8 %copy.52 = f32[8,96,64]{1,2,0:T(8,128)} copy(f32[8,96,64]{2,1,0:T(8,128)} %bitcast.28) | data formatting | bytes 393216 | tf_op jit(solution)/shard_map/reshape | solution.py:101
  75.4 6.1 %all-to-all-start = ((f32[8,96,64]{1,2,0:T(8,128)}), f32[8,96,64]{1,2,0:T(8,128)S(1)}, u32[]{:S(2)}, u32[]{:S(2)}) async-start(f32[8,96,64]{1,2,0:T(8,128)} %copy.52), calls=%async_computation | async-start | bytes 524288 | tf_op jit(solution)/shard_map/all_to_all | solution.py:102
  81.6 0.8 copy.55
  82.7 18.9 %shard_map.56 = (bf16[768,2048]{1,0:T(8,128)(2,1)S(1)}, bf16[768,2048]{1,0:T(8,128)(2,1)}, f32[768,64]{1,0:T(8,128)S(1)}) custom-call(s32[768]{0:T(1024)S(1)} %reshape.42.slot_ref, bf16[54,128,128]{2,1,0:T(8,128)(2,1)S(1)} %bitcast.25, f32[768,1]{1,0:T(8,128)S(1)} %slice.49.dn_ref, bf16[2048,1088]{1,0:T(8,128)(2,1)} %all-gather.2.cloned.1.call-done.land_ref), custom_call_target="tpu_custom_call" | custom-call | tf_op jit(solution)/shard_map/pallas_call | solution.py:87
  101.6 1.7 copy-done.2
  103.2 0.9 copy.57
  104.1 6.9 %all-to-all-start.2 = ((f32[8,96,64]{1,2,0:T(8,128)}), f32[8,96,64]{1,2,0:T(8,128)}, u32[]{:S(2)}, u32[]{:S(2)}) async-start(f32[8,96,64]{1,2,0:T(8,128)} %copy.57), calls=%async_computation.2 | async-start | bytes 524288 | tf_op jit(solution)/shard_map/all_to_all | solution.py:102
  111.0 7.4 %all-to-all-done.2 = f32[8,96,64]{1,2,0:T(8,128)} async-done(((f32[8,96,64]{1,2,0:T(8,128)}), f32[8,96,64]{1,2,0:T(8,128)}, u32[]{:S(2)}, u32[]{:S(2)}) %all-to-all-start.2) | async-done | bytes 196640 | tf_op jit(solution)/shard_map/all_to_all | solution.py:102
  119.1 3.4 %all-to-all-start.1 = ((f32[8,96,64]{1,2,0:T(8,128)}), f32[8,96,64]{1,2,0:T(8,128)S(1)}, u32[]{:S(2)}, u32[]{:S(2)}) async-start(f32[8,96,64]{1,2,0:T(8,128)} %broadcast_in_dim.10), calls=%async_computation.1 | async-start | bytes 524288 | tf_op jit(solution)/shard_map/all_to_all | solution.py:109
  122.6 1.0 reduce_sum.38
  123.5 6.3 %all-to-all-done.1 = f32[8,96,64]{1,2,0:T(8,128)S(1)} async-done(((f32[8,96,64]{1,2,0:T(8,128)}), f32[8,96,64]{1,2,0:T(8,128)S(1)}, u32[]{:S(2)}, u32[]{:S(2)}) %all-to-all-start.1) | async-done | bytes 196640 | tf_op jit(solution)/shard_map/all_to_all | solution.py:109
  130.5 4.0 %all-to-all-start.3 = ((f32[8,96,64]{1,2,0:T(8,128)}), f32[8,96,64]{1,2,0:T(8,128)}, u32[]{:S(2)}, u32[]{:S(2)}) async-start(f32[8,96,64]{1,2,0:T(8,128)} %broadcast_in_dim.11), calls=%async_computation.3 | async-start | bytes 524288 | tf_op jit(solution)/shard_map/all_to_all | solution.py:109
  134.6 0.9 copy.53
  135.4 1.1 reshape.41
  136.6 5.3 %all-to-all-done.3 = f32[8,96,64]{1,2,0:T(8,128)} async-done(((f32[8,96,64]{1,2,0:T(8,128)}), f32[8,96,64]{1,2,0:T(8,128)}, u32[]{:S(2)}, u32[]{:S(2)}) %all-to-all-start.3) | async-done | bytes 196640 | tf_op jit(solution)/shard_map/all_to_all | solution.py:109
  141.9 1.8 %copy.58 = f32[8,96,64]{1,0,2:T(8,128)} copy(f32[8,96,64]{1,2,0:T(8,128)} %all-to-all-done.3) | data formatting | bytes 393216 | tf_op jit(solution)/shard_map/all_to_all | solution.py:109
  143.7 1.1 reshape.44
  145.5 1.2 copy-done.8
  148.4 0.9 copy-done.7
  150.0 17.8 %all_to_all.25 = f32[16,128,64]{1,2,0:T(8,128)S(1)} all-to-all(f32[16,128,64]{1,2,0:T(8,128)S(1)} %copy_bitcast_fusion.1), channel_id=1, replica_groups=mesh['dp'=16,'land'=8] {'dp'}, dimensions={0} | all-to-all | bytes 1048576 | tf_op jit(solution)/shard_map/all_to_all | solution.py:102
  (44 shorter events, 10.1 us)
Async XLA Ops:
  6.5 44.3 %all-gather.2.cloned.1.call-start = ((), (), s32[]{:S(2)}) async-start(), calls=%async_computation.5 | async-start | bytes 5013504 | tf_op jit(solution)/shard_map/all_gather | solution.py:124
  16.4 1.9 %copy-start.6 = (bf16[1536,1024]{1,0:T(8,128)(2,1)S(1)}, bf16[1536,1024]{1,0:T(8,128)(2,1)}, u32[]{:S(2)}) copy-start(bf16[1536,1024]{1,0:T(8,128)(2,1)} %param.5) | copy-start | bytes 9437188
  50.8 1.0 copy-start.4
  71.1 1.7 copy-start
  72.8 0.8 copy-start.5
  75.4 28.7 %all-to-all-start = ((f32[8,96,64]{1,2,0:T(8,128)}), f32[8,96,64]{1,2,0:T(8,128)S(1)}, u32[]{:S(2)}, u32[]{:S(2)}) async-start(f32[8,96,64]{1,2,0:T(8,128)} %copy.52), calls=%async_computation | async-start | bytes 524288 | tf_op jit(solution)/shard_map/all_to_all | solution.py:102
  101.6 1.7 copy-start.2
  104.1 40.8 %copy-start.1 = (bf16[768,2048]{1,0:T(8,128)(2,1)S(1)}, bf16[768,2048]{1,0:T(8,128)(2,1)}, u32[]{:S(2)}) copy-start(bf16[768,2048]{1,0:T(8,128)(2,1)} %copy-done) | copy-start | bytes 9437188
  104.1 14.3 %all-to-all-start.2 = ((f32[8,96,64]{1,2,0:T(8,128)}), f32[8,96,64]{1,2,0:T(8,128)}, u32[]{:S(2)}, u32[]{:S(2)}) async-start(f32[8,96,64]{1,2,0:T(8,128)} %copy.57), calls=%async_computation.2 | async-start | bytes 524288 | tf_op jit(solution)/shard_map/all_to_all | solution.py:102
  119.1 10.7 %all-to-all-start.1 = ((f32[8,96,64]{1,2,0:T(8,128)}), f32[8,96,64]{1,2,0:T(8,128)S(1)}, u32[]{:S(2)}, u32[]{:S(2)}) async-start(f32[8,96,64]{1,2,0:T(8,128)} %broadcast_in_dim.10), calls=%async_computation.1 | async-start | bytes 524288 | tf_op jit(solution)/shard_map/all_to_all | solution.py:109
  130.5 11.4 %all-to-all-start.3 = ((f32[8,96,64]{1,2,0:T(8,128)}), f32[8,96,64]{1,2,0:T(8,128)}, u32[]{:S(2)}, u32[]{:S(2)}) async-start(f32[8,96,64]{1,2,0:T(8,128)} %broadcast_in_dim.11), calls=%async_computation.3 | async-start | bytes 524288 | tf_op jit(solution)/shard_map/all_to_all | solution.py:109
  144.8 1.9 %copy-start.8 = (bf16[768,2048]{1,0:T(8,128)(2,1)S(1)}, bf16[768,2048]{1,0:T(8,128)(2,1)}, u32[]{:S(2)}) copy-start(bf16[768,2048]{1,0:T(8,128)(2,1)} %get-tuple-element.16) | copy-start | bytes 9437188
  145.4 2.4 %copy-start.3 = (bf16[768,2048]{1,0:T(8,128)(2,1)S(1)}, bf16[768,2048]{1,0:T(8,128)(2,1)}, u32[]{:S(2)}) copy-start(bf16[768,2048]{1,0:T(8,128)(2,1)} %copy-done.2) | copy-start | bytes 9437188
  147.3 2.0 %copy-start.7 = (bf16[768,2048]{1,0:T(8,128)(2,1)S(1)}, bf16[768,2048]{1,0:T(8,128)(2,1)}, u32[]{:S(2)}) copy-start(bf16[768,2048]{1,0:T(8,128)(2,1)} %get-tuple-element.20) | copy-start | bytes 9437188
Sparse Core Ops, SparseCore 0:
  9.2 41.5 all-gather.1

commit v6 on v3

--- a/solution.py
+++ b/solution.py
@@ -43,31 +43,27 @@
             aligned_ref[d * DOC_BLOCK:(d + 1) * DOC_BLOCK, b * TERM_BLOCK:(b + 1) * TERM_BLOCK] = (
                 doc_ref[d * (ACTIVE + 1) + a])
     width = ACTIVE * TERM_BLOCK
-    tile = land_ref[:, :width]
-    squares = jnp.zeros((LM_BLOCK, TERM_BLOCK), jnp.float32)
-    for b in range(LAND_ACTIVE):
-        part = tile[:, b * TERM_BLOCK:(b + 1) * TERM_BLOCK].astype(jnp.float32)
-        squares = squares + part * part
-    land_norm = lax.rsqrt(jnp.sum(squares.T, axis=0, keepdims=True) + 1e-06)
-    inner = lax.dot_general(
-        aligned_ref[...], tile, (((1,), (1,)), ((), ())),
-        preferred_element_type=jnp.float32)
-    cosine = inner * dn_ref[...] * land_norm
-    kern = jnp.exp(2.0 * sharpness * (cosine - 1.0))
+    tile = land_ref[:width, :]
+    squares = tile.astype(jnp.float32)
+    land_norm = lax.rsqrt(jnp.sum(squares * squares, axis=0, keepdims=True) + 1e-06)
+    inner = jnp.dot(aligned_ref[...], tile, preferred_element_type=jnp.float32)
+    kern = jnp.exp(inner * dn_ref[...] * land_norm - 2.0 * sharpness)
     high = kern.astype(jnp.bfloat16)
     low = (kern - high.astype(jnp.float32)).astype(jnp.bfloat16)
-    high_ref[...] = high
-    low_ref[...] = low
-    coef = land_ref[:, width:]
-    part = jnp.dot(high, coef, preferred_element_type=jnp.float32)
-    part = part + jnp.dot(low, coef, preferred_element_type=jnp.float32)
+    high_ref[0] = high
+    low_ref[0] = low
+    coef = land_ref[width:, :]
+    dims = (((1,), (1,)), ((), ()))
+    part = lax.dot_general(high, coef, dims, preferred_element_type=jnp.float32)
+    part = part + lax.dot_general(low, coef, dims, preferred_element_type=jnp.float32)
     fit_ref[...] += part
 
 
 def forward(slots, doc_tiles, doc_norm, land_rows, targets):
     doc_rows = doc_norm.shape[0]
-    land_count = land_rows.shape[0]
-    block_count = land_count // LM_BLOCK
+    row_height = ACTIVE * TERM_BLOCK + targets
+    block_count = land_rows.shape[0] // row_height
+    land_count = block_count * LM_BLOCK
     width = ACTIVE * TERM_BLOCK
     grid_spec = pltpu.PrefetchScalarGridSpec(
         num_scalar_prefetch=1,
@@ -75,11 +71,11 @@
         in_specs=[
             pl.BlockSpec(doc_tiles.shape, lambda l, s: (0, 0, 0)),
             pl.BlockSpec((doc_rows, 1), lambda l, s: (0, 0)),
-            pl.BlockSpec((LM_BLOCK, land_rows.shape[1]), lambda l, s: (l, 0)),
+            pl.BlockSpec((row_height, LM_BLOCK), lambda l, s: (l, 0)),
         ],
         out_specs=[
-            pl.BlockSpec((doc_rows, LM_BLOCK), lambda l, s: (0, l)),
-            pl.BlockSpec((doc_rows, LM_BLOCK), lambda l, s: (0, l)),
+            pl.BlockSpec((1, doc_rows, LM_BLOCK), lambda l, s: (l, 0, 0)),
+            pl.BlockSpec((1, doc_rows, LM_BLOCK), lambda l, s: (l, 0, 0)),
             pl.BlockSpec((doc_rows, targets), lambda l, s: (0, 0)),
         ],
         scratch_shapes=[pltpu.VMEM((doc_rows, width), jnp.bfloat16)],
@@ -88,8 +84,8 @@
         forward_kernel,
         grid_spec=grid_spec,
         out_shape=[
-            jax.ShapeDtypeStruct((doc_rows, land_count), jnp.bfloat16),
-            jax.ShapeDtypeStruct((doc_rows, land_count), jnp.bfloat16),
+            jax.ShapeDtypeStruct((block_count, doc_rows, LM_BLOCK), jnp.bfloat16),
+            jax.ShapeDtypeStruct((block_count, doc_rows, LM_BLOCK), jnp.bfloat16),
             jax.ShapeDtypeStruct((doc_rows, targets), jnp.float32),
         ],
         compiler_params=pltpu.CompilerParams(
@@ -122,19 +118,19 @@
     own_table = lax.dynamic_index_in_dim(table, lax.axis_index("land"), axis=1, keepdims=False)
     own_table = own_table.reshape(dp_count * own_blocks, LAND_ACTIVE)
     land_rows = lax.all_gather(
-        jnp.concatenate([land_values, coefficients], axis=1), "dp", axis=0, tiled=True)
+        jnp.concatenate([land_values, coefficients], axis=1).T, "dp", axis=0, tiled=True)
     doc_tiles = doc_values.reshape(doc_count, DOC_BLOCK, ACTIVE, TERM_BLOCK).transpose(0, 2, 1, 3)
     doc_tiles = jnp.pad(doc_tiles, ((0, 0), (0, 1), (0, 0), (0, 0)))
     doc_tiles = doc_tiles.reshape(doc_count * (ACTIVE + 1), DOC_BLOCK, TERM_BLOCK)
     slots = match_table(doc_blocks, own_table)
     tile_high, tile_low, fitted = forward(
-        slots, doc_tiles, doc_norm.reshape(doc_rows, 1), land_rows, targets)
+        slots, doc_tiles, (2.0 * sharpness) * doc_norm.reshape(doc_rows, 1), land_rows, targets)
     fitted = all_sum(fitted, "land", land_count)
     fitted_high, fitted_low = split_pair(fitted)
     fitted_pair = jnp.concatenate([fitted_high, fitted_low], axis=1)
-    summed = jnp.dot(tile_high.T, fitted_pair, preferred_element_type=jnp.float32)
-    summed = summed + jnp.dot(tile_low.T, fitted_pair, preferred_element_type=jnp.float32)
-    summed = summed[:, :targets] + summed[:, targets:]
+    summed = jnp.einsum("qnl,nt->qlt", tile_high, fitted_pair, preferred_element_type=jnp.float32)
+    summed = summed + jnp.einsum("qnl,nt->qlt", tile_low, fitted_pair, preferred_element_type=jnp.float32)
+    summed = (summed[:, :, :targets] + summed[:, :, targets:]).reshape(-1, targets)
     result = sum_over(summed, "dp", dp_count)
     return result / total_docs
 

time: 142 us -> 141 us (level)
    concatenate x1 -> x0, other arithmetic: 1.7 us -> none  [on_device(): jnp.concatenate([land_values, coefficients], axis=1)]
    transpose x0 -> x1, other arithmetic: none -> 1.45 us  [on_device(): jnp.concatenate([land_values, coefficients], axis=1)]
where the time goes in v6:
time: 141 us
  blocking collectives  44.8 us (32%)
  waiting for transfers between devices  32.4 us (23%)
  Pallas kernels  28.2 us (20%)
  between operations  13.6 us (10%)
  local copies, waits for them, and re-layouts  10.8 us (8%)
  other arithmetic  5.87 us (4%)
  matrix products  4.92 us (3%)
    all_gather x1, waiting for transfers between devices, on_device(): lax.all_gather(jnp.concatenate([land_values, coefficients], axis=1).T, 'd...  32.4 us
    all_to_all x2, blocking collectives, sum_over(): pieces = lax.all_to_all(pieces, axis, 0, 0, tiled=False)  31.4 us
    pallas_call x1, Pallas kernels, forward(): pl.pallas_call(forward_kernel, grid_spec=grid_spec, out_shape=[jax.ShapeD...  28.2 us
    all_to_all x1, blocking collectives, all_sum(): return lax.all_to_all(spread, axis, 0, 0, tiled=False).reshape(values.shape)  13.4 us
    unnamed x13, local copies, waits for them, and re-layouts  4.98 us
    dot_general x1, matrix products, on_device(): jnp.einsum('qnl,nt->qlt', tile_high, fitted_pair, preferred_element_type=...  3.92 us
  transfers between devices with their start and end apart: 1, of which 1 were waited for; matrix products, arithmetic and copies ran while one was open for 6% of the time, Pallas kernels for 0%

profile of v6, /device:TPU:1, one launch (start us, length us, event | category | flops | bytes accessed | tf_op | source)
XLA Modules:
  0.0 140.5 jit_solution(78461417644472467)
XLA Ops:
  6.5 1.3 copy.32
  7.8 1.5 %maximum_bitcast_fusion.1 = bf16[1088,128]{1,0:T(8,128)(2,1)} fusion(bf16[128,64]{0,1:T(8,128)(2,1)} %param.9, bf16[128,1024]{0,1:T(8,128)(2,1)S(1)} %copy.32), kind=kLoop, calls=%fused_computation.8 | loop fusion | flops 557056 | bytes 557056 | tf_op jit(solution)/shard_map/transpose | solution.py:121
  9.3 0.0 all-gather.2.cloned.1.call-update
  9.3 0.8 copy.29
  10.1 0.8 reshape.40
  10.8 0.3 dynamic-slice_reduce_fusion
  11.1 0.2 compare_reduce_fusion.1
  11.3 0.8 compare_reduce_fusion
  12.2 0.1 copy.30
  12.3 0.1 reshape.41.slot_ref
  12.4 2.6 %multiply_reduce_fusion = f32[1536]{0:T(1024)S(1)} fusion(bf16[1536,1024]{1,0:T(8,128)(2,1)} %param.5), kind=kLoop, calls=%fused_computation | loop fusion | flops 4717056 | bytes 3151872 | tf_op jit(solution)/shard_map/reduce_sum | solution.py:116
  15.0 1.1 mul.11.dn_ref
  16.1 0.8 copy.39
  17.0 0.9 copy.41
  17.8 0.5 pad.4
  18.4 32.4 %all-gather.2.cloned.1.call-done.land_ref = bf16[17408,128]{1,0:T(8,128)(2,1)} async-done(((bf16[1088,128]{1,0:T(8,128)(2,1)}), bf16[17408,128]{1,0:T(8,128)(2,1)}) %all-gather.2.cloned.1.call-update) | async-done | bytes 4456464 | tf_op jit(solution)/shard_map/all_gather | solution.py:120
  50.8 1.1 copy-done
  51.9 28.2 %shard_map.55 = (bf16[16,1536,128]{2,1,0:T(8,128)(2,1)}, bf16[16,1536,128]{2,1,0:T(8,128)(2,1)}, f32[1536,64]{1,0:T(8,128)S(1)}) custom-call(s32[1536]{0:T(1024)S(1)} %reshape.41.slot_ref, bf16[108,128,128]{2,1,0:T(8,128)(2,1)S(1)} %bitcast.20, f32[1536,1]{1,0:T(8,128)S(1)} %copy-done, bf16[17408,128]{1,0:T(8,128)(2,1)} %all-gather.2.cloned.1.call-done.land_ref), custom_call_target="tpu_custom_call" | custom-call | tf_op jit(solution)/shard_map/pallas_call | solution.py:83
  80.1 0.9 copy-done.1
  81.0 1.4 %copy.34 = f32[8,192,64]{1,2,0:T(8,128)S(1)} copy(f32[8,192,64]{2,1,0:T(8,128)} %bitcast.21) | data formatting | bytes 786432 | tf_op jit(solution)/shard_map/reshape | solution.py:97
  82.5 16.0 %all_to_all.15 = f32[8,192,64]{1,2,0:T(8,128)S(1)} all-to-all(f32[8,192,64]{1,2,0:T(8,128)S(1)} %copy.34), channel_id=1, replica_groups=mesh['dp'=16,'land'=8] {'land'}, dimensions={0} | all-to-all | bytes 786432 | tf_op jit(solution)/shard_map/all_to_all | solution.py:98
  98.5 0.0 slice-start
  98.6 13.4 %all_to_all.16 = f32[8,192,64]{1,2,0:T(8,128)S(1)} all-to-all(f32[8,192,64]{1,2,0:T(8,128)S(1)} %broadcast_in_dim.12), channel_id=1, replica_groups=mesh['dp'=16,'land'=8] {'land'}, dimensions={0} | all-to-all | bytes 786432 | tf_op jit(solution)/shard_map/all_to_all | solution.py:105
  112.0 0.3 copy.37
  112.4 0.2 reshape.45
  112.6 0.0 slice-start.1
  112.6 3.9 %fusion = f32[16,128,128]{1,2,0:T(8,128)S(1)} fusion(bf16[16,1536,128]{2,1,0:T(8,128)(2,1)} %get-tuple-element.10, bf16[1536,64]{0,1:T(8,128)(2,1)S(1)} %subtract_convert_fusion, bf16[1536,64]{0,1:T(8,128)(2,1)S(1)} %convert_element_type.15), kind=kOutput, calls=%fused_computation.9 | convolution fusion | flops 806092800 | bytes 7733248 | tf_op jit(solution)/shard_map/qnl,nt->qlt/dot_general | solution.py:131
  116.6 0.1 slice-done.1
  116.6 1.0 convolution_add_fusion
  117.6 0.1 slice_add_fusion
  117.7 15.3 %all_to_all.17 = f32[16,128,64]{1,2,0:T(8,128)S(1)} all-to-all(f32[16,128,64]{1,2,0:T(8,128)S(1)} %slice_add_fusion), channel_id=1, replica_groups=mesh['dp'=16,'land'=8] {'dp'}, dimensions={0} | all-to-all | bytes 1048576 | tf_op jit(solution)/shard_map/all_to_all | solution.py:98
  133.1 0.6 broadcast_multiply_fusion
  (14 shorter events, 0.2 us)
Async XLA Ops:
  6.5 9.6 %copy-start.2 = (bf16[1536,1024]{1,0:T(8,128)(2,1)S(1)}, bf16[1536,1024]{1,0:T(8,128)(2,1)}, u32[]{:S(2)}) copy-start(bf16[1536,1024]{1,0:T(8,128)(2,1)} %param.5) | copy-start | bytes 9437188
  6.5 44.3 %all-gather.2.cloned.1.call-start = ((), (), s32[]{:S(2)}) async-start(), calls=%async_computation.3 | async-start | bytes 4734976 | tf_op jit(solution)/shard_map/all_gather | solution.py:120
  50.8 1.1 copy-start
  80.1 0.9 copy-start.1
  98.5 18.0 %slice-start = ((s8[6291456]{0:T(1024)(128)(4,1)}), s8[2097152]{0:T(1024)(128)(4,1)S(1)}, s32[]{:S(2)}) async-start(s8[6291456]{0:T(1024)(128)(4,1)} %bitcast.25), calls=%async_computation.4 | async-start | bytes 4194304
  112.6 4.0 %slice-start.1 = ((s8[6291456]{0:T(1024)(128)(4,1)}), s8[4194304]{0:T(1024)(128)(4,1)S(1)}, s32[]{:S(2)}) async-start(s8[6291456]{0:T(1024)(128)(4,1)} %bitcast.25), calls=%async_computation.5 | async-start | bytes 8388608
Sparse Core Ops, SparseCore 0:
  9.4 41.3 all-gather.1

commit v7 on v6

--- a/solution.py
+++ b/solution.py
@@ -117,8 +117,10 @@
     table = land_blocks.reshape(dp_count, land_count, own_blocks, LAND_ACTIVE)
     own_table = lax.dynamic_index_in_dim(table, lax.axis_index("land"), axis=1, keepdims=False)
     own_table = own_table.reshape(dp_count * own_blocks, LAND_ACTIVE)
-    land_rows = lax.all_gather(
-        jnp.concatenate([land_values, coefficients], axis=1).T, "dp", axis=0, tiled=True)
+    rows = jnp.concatenate([land_values, coefficients], axis=1).T
+    land_rows = lax.all_to_all(
+        jnp.broadcast_to(rows[None], (dp_count,) + rows.shape), "dp", 0, 0, tiled=False)
+    land_rows = land_rows.reshape(-1, rows.shape[1])
     doc_tiles = doc_values.reshape(doc_count, DOC_BLOCK, ACTIVE, TERM_BLOCK).transpose(0, 2, 1, 3)
     doc_tiles = jnp.pad(doc_tiles, ((0, 0), (0, 1), (0, 0), (0, 0)))
     doc_tiles = doc_tiles.reshape(doc_count * (ACTIVE + 1), DOC_BLOCK, TERM_BLOCK)

time: 141 us -> 148 us (1.050)
  waiting for transfers between devices: 32.4 us -> 46.6 us
  between operations: 13.6 us -> 0.2 us
  starting transfers between devices: 0.01 us -> 7.83 us
  other arithmetic: 5.87 us -> 3.52 us
    all_to_all x0 -> x1, waiting for transfers between devices: none -> 46.6 us  [on_device(): lax.all_to_all(jnp.broadcast_to(rows[None], (dp_count,) + rows.shape), 'd...]
    all_gather x1 -> x0, waiting for transfers between devices: 32.4 us -> none  [on_device(): lax.all_gather(jnp.concatenate([land_values, coefficients], axis=1).T, 'd...]
    all_to_all x0 -> x1, starting transfers between devices: none -> 7.83 us  [on_device(): lax.all_to_all(jnp.broadcast_to(rows[None], (dp_count,) + rows.shape), 'd...]
    broadcast_in_dim x0 -> x1, local copies, waits for them, and re-layouts: none -> 2.89 us  [on_device(): jnp.broadcast_to(rows[None], (dp_count,) + rows.shape)]
    reduce_sum x1, other arithmetic: 2.57 us -> 0.68 us  [on_device(): jnp.sum(jnp.square(doc_values.astype(jnp.float32)), axis=1) + 1e-06]
    all_to_all x1, blocking collectives: 13.4 us -> 11.6 us  [all_sum(): return lax.all_to_all(spread, axis, 0, 0, tiled=False).reshape(values.shape)]
    unnamed x13 -> x17, local copies, waits for them, and re-layouts: 4.98 us -> 3.86 us
  transfers between devices with their start and end apart: 1 -> 1, of which waited for: 1 -> 1; matrix products, arithmetic and copies ran while one was open for 6% -> 4% of each run, Pallas kernels for 0% -> 0%
where the time goes in v7:
time: 148 us
  waiting for transfers between devices  46.6 us (31%)
  blocking collectives  43.9 us (30%)
  Pallas kernels  28.8 us (19%)
  local copies, waits for them, and re-layouts  11.9 us (8%)
  starting transfers between devices  7.83 us (5%)
  matrix products  4.92 us (3%)
  other arithmetic  3.52 us (2%)
    all_to_all x1, waiting for transfers between devices, on_device(): lax.all_to_all(jnp.broadcast_to(rows[None], (dp_count,) + rows.shape), 'd...  46.6 us
    all_to_all x2, blocking collectives, sum_over(): pieces = lax.all_to_all(pieces, axis, 0, 0, tiled=False)  32.2 us
    pallas_call x1, Pallas kernels, forward(): pl.pallas_call(forward_kernel, grid_spec=grid_spec, out_shape=[jax.ShapeD...  28.8 us
    all_to_all x1, blocking collectives, all_sum(): return lax.all_to_all(spread, axis, 0, 0, tiled=False).reshape(values.shape)  11.6 us
    all_to_all x1, starting transfers between devices, on_device(): lax.all_to_all(jnp.broadcast_to(rows[None], (dp_count,) + rows.shape), 'd...  7.83 us
    dot_general x1, matrix products, on_device(): jnp.einsum('qnl,nt->qlt', tile_high, fitted_pair, preferred_element_type=...  3.92 us
    unnamed x17, local copies, waits for them, and re-layouts  3.86 us
  transfers between devices with their start and end apart: 1, of which 1 were waited for; matrix products, arithmetic and copies ran while one was open for 4% of the time, Pallas kernels for 0%

profile of v7, /device:TPU:1, one launch (start us, length us, event | category | flops | bytes accessed | tf_op | source)
XLA Modules:
  0.0 147.7 jit_solution(2106281646282333456)
XLA Ops:
  0.0 0.8 copy.36
  0.8 1.0 maximum_bitcast_fusion.1
  1.8 0.2 copy.37
  2.0 2.9 %broadcast_in_dim.9 = bf16[16,1088,128]{2,1,0:T(8,128)(2,1)} broadcast(bf16[1088,128]{1,0:T(8,128)(2,1)S(1)} %copy.37), dimensions={1,2} | broadcast | bytes 4734976 | tf_op jit(solution)/shard_map/broadcast_in_dim | solution.py:122
  4.9 7.8 %all-to-all-start = ((bf16[16,1088,128]{2,1,0:T(8,128)(2,1)}), bf16[16,1088,128]{2,1,0:T(8,128)(2,1)}, u32[]{:S(2)}, u32[]{:S(2)}) async-start(bf16[16,1088,128]{2,1,0:T(8,128)(2,1)} %broadcast_in_dim.9), calls=%async_computation | async-start | bytes 8912896 | tf_op jit(solution)/shard_map/all_to_all | solution.py:121
  12.8 0.1 copy.33
  12.9 0.1 reshape.44
  12.9 0.3 dynamic-slice_reduce_fusion
  13.2 0.2 compare_reduce_fusion.1
  13.4 0.8 compare_reduce_fusion
  14.3 0.1 copy.34
  14.4 0.1 reshape.45.slot_ref
  14.5 0.7 multiply_reduce_fusion
  15.2 1.2 mul.11.dn_ref
  16.4 0.8 copy.44
  17.2 0.9 copy.46
  18.1 0.4 pad.4
  18.5 46.6 %all-to-all-done = bf16[16,1088,128]{2,1,0:T(8,128)(2,1)} async-done(((bf16[16,1088,128]{2,1,0:T(8,128)(2,1)}), bf16[16,1088,128]{2,1,0:T(8,128)(2,1)}, u32[]{:S(2)}, u32[]{:S(2)}) %all-to-all-start) | async-done | bytes 4456480 | tf_op jit(solution)/shard_map/all_to_all | solution.py:121
  65.1 1.1 copy-done
  66.2 28.8 %shard_map.55 = (bf16[16,1536,128]{2,1,0:T(8,128)(2,1)}, bf16[16,1536,128]{2,1,0:T(8,128)(2,1)}, f32[1536,64]{1,0:T(8,128)S(1)}) custom-call(s32[1536]{0:T(1024)S(1)} %reshape.45.slot_ref, bf16[108,128,128]{2,1,0:T(8,128)(2,1)S(1)} %bitcast.21, f32[1536,1]{1,0:T(8,128)S(1)} %copy-done, bf16[17408,128]{1,0:T(8,128)(2,1)} %bitcast.3.land_ref), custom_call_target="tpu_custom_call" | custom-call | tf_op jit(solution)/shard_map/pallas_call | solution.py:83
  95.1 0.9 copy-done.1
  96.0 1.4 copy.39
  97.4 15.8 %all_to_all.20 = f32[8,192,64]{1,2,0:T(8,128)S(1)} all-to-all(f32[8,192,64]{1,2,0:T(8,128)S(1)} %copy.39), channel_id=1, replica_groups=mesh['dp'=16,'land'=8] {'land'}, dimensions={0} | all-to-all | bytes 786432 | tf_op jit(solution)/shard_map/all_to_all | solution.py:98
  113.4 11.6 %all_to_all.21 = f32[8,192,64]{1,2,0:T(8,128)S(1)} all-to-all(f32[8,192,64]{1,2,0:T(8,128)S(1)} %broadcast_in_dim.10), channel_id=1, replica_groups=mesh['dp'=16,'land'=8] {'land'}, dimensions={0} | all-to-all | bytes 786432 | tf_op jit(solution)/shard_map/all_to_all | solution.py:105
  125.0 0.3 copy.42
  125.3 0.2 reshape.50
  125.6 3.9 %fusion = f32[16,128,128]{1,2,0:T(8,128)S(1)} fusion(bf16[16,1536,128]{2,1,0:T(8,128)(2,1)} %get-tuple-element.10, bf16[1536,64]{0,1:T(8,128)(2,1)S(1)} %subtract_convert_fusion, bf16[1536,64]{0,1:T(8,128)(2,1)S(1)} %convert_element_type.15), kind=kOutput, calls=%fused_computation.9 | convolution fusion | flops 806092800 | bytes 7733248 | tf_op jit(solution)/shard_map/qnl,nt->qlt/dot_general | solution.py:133
  129.5 0.1 slice-done.1
  129.6 1.0 convolution_add_fusion
  130.6 0.1 slice_add_fusion
  130.6 16.4 %all_to_all.22 = f32[16,128,64]{1,2,0:T(8,128)S(1)} all-to-all(f32[16,128,64]{1,2,0:T(8,128)S(1)} %slice_add_fusion), channel_id=1, replica_groups=mesh['dp'=16,'land'=8] {'dp'}, dimensions={0} | all-to-all | bytes 1048576 | tf_op jit(solution)/shard_map/all_to_all | solution.py:98
  147.1 0.6 broadcast_multiply_fusion
  (19 shorter events, 0.2 us)
Async XLA Ops:
  2.0 10.8 %copy-start.3 = (s32[12,8]{0,1:T(8,128)S(1)}, s32[12,8]{0,1:T(8,128)}, u32[]{:S(2)}) copy-start(s32[12,8]{0,1:T(8,128)} %param.6) | copy-start | bytes 1156
  2.0 10.8 %copy-start.4 = (s32[128,8]{0,1:T(8,128)S(1)}, s32[128,8]{0,1:T(8,128)}, u32[]{:S(2)}) copy-start(s32[128,8]{0,1:T(8,128)} %param.8) | copy-start | bytes 12292
  2.0 12.5 %copy-start.2 = (bf16[1536,1024]{1,0:T(8,128)(2,1)S(1)}, bf16[1536,1024]{1,0:T(8,128)(2,1)}, u32[]{:S(2)}) copy-start(bf16[1536,1024]{1,0:T(8,128)(2,1)} %param.5) | copy-start | bytes 9437188
  4.9 60.2 %all-to-all-start = ((bf16[16,1088,128]{2,1,0:T(8,128)(2,1)}), bf16[16,1088,128]{2,1,0:T(8,128)(2,1)}, u32[]{:S(2)}, u32[]{:S(2)}) async-start(bf16[16,1088,128]{2,1,0:T(8,128)(2,1)} %broadcast_in_dim.9), calls=%async_computation | async-start | bytes 8912896 | tf_op jit(solution)/shard_map/all_to_all | solution.py:121
  65.1 1.1 copy-start
  95.1 0.9 copy-start.1
  113.3 16.2 %slice-start = ((s8[6291456]{0:T(1024)(128)(4,1)}), s8[2097152]{0:T(1024)(128)(4,1)S(1)}, s32[]{:S(2)}) async-start(s8[6291456]{0:T(1024)(128)(4,1)} %bitcast.26), calls=%async_computation.4 | async-start | bytes 4194304
  125.6 4.0 %slice-start.1 = ((s8[6291456]{0:T(1024)(128)(4,1)}), s8[4194304]{0:T(1024)(128)(4,1)S(1)}, s32[]{:S(2)}) async-start(s8[6291456]{0:T(1024)(128)(4,1)} %bitcast.26), calls=%async_computation.5 | async-start | bytes 8388608

commit v8 on v6

--- a/solution.py
+++ b/solution.py
@@ -28,35 +28,43 @@
     return jnp.where(has, first, ACTIVE).astype(jnp.int32).reshape(-1)
 
 
+GROUP = 2
+
+
 def forward_kernel(slot_ref, doc_ref, dn_ref, land_ref,
                    high_ref, low_ref, fit_ref, aligned_ref):
     step = pl.program_id(0)
     doc_count = dn_ref.shape[0] // DOC_BLOCK
+    width = ACTIVE * TERM_BLOCK
+    row_height = land_ref.shape[0] // GROUP
 
     @pl.when(step == 0)
     def _():
         fit_ref[...] = jnp.zeros_like(fit_ref)
 
-    for d in range(doc_count):
-        for b in range(LAND_ACTIVE):
-            a = slot_ref[(step * doc_count + d) * LAND_ACTIVE + b]
-            aligned_ref[d * DOC_BLOCK:(d + 1) * DOC_BLOCK, b * TERM_BLOCK:(b + 1) * TERM_BLOCK] = (
-                doc_ref[d * (ACTIVE + 1) + a])
-    width = ACTIVE * TERM_BLOCK
-    tile = land_ref[:width, :]
-    squares = tile.astype(jnp.float32)
-    land_norm = lax.rsqrt(jnp.sum(squares * squares, axis=0, keepdims=True) + 1e-06)
-    inner = jnp.dot(aligned_ref[...], tile, preferred_element_type=jnp.float32)
-    kern = jnp.exp(inner * dn_ref[...] * land_norm - 2.0 * sharpness)
-    high = kern.astype(jnp.bfloat16)
-    low = (kern - high.astype(jnp.float32)).astype(jnp.bfloat16)
-    high_ref[0] = high
-    low_ref[0] = low
-    coef = land_ref[width:, :]
-    dims = (((1,), (1,)), ((), ()))
-    part = lax.dot_general(high, coef, dims, preferred_element_type=jnp.float32)
-    part = part + lax.dot_general(low, coef, dims, preferred_element_type=jnp.float32)
-    fit_ref[...] += part
+    for g in range(GROUP):
+        block = step * GROUP + g
+        for d in range(doc_count):
+            for b in range(LAND_ACTIVE):
+                a = slot_ref[(block * doc_count + d) * LAND_ACTIVE + b]
+                aligned_ref[g, d * DOC_BLOCK:(d + 1) * DOC_BLOCK, b * TERM_BLOCK:(b + 1) * TERM_BLOCK] = (
+                    doc_ref[d * (ACTIVE + 1) + a])
+    for g in range(GROUP):
+        top = g * row_height
+        tile = land_ref[top:top + width, :]
+        squares = tile.astype(jnp.float32)
+        land_norm = lax.rsqrt(jnp.sum(squares * squares, axis=0, keepdims=True) + 1e-06)
+        inner = jnp.dot(aligned_ref[g], tile, preferred_element_type=jnp.float32)
+        kern = jnp.exp(inner * dn_ref[...] * land_norm - 2.0 * sharpness)
+        high = kern.astype(jnp.bfloat16)
+        low = (kern - high.astype(jnp.float32)).astype(jnp.bfloat16)
+        high_ref[g] = high
+        low_ref[g] = low
+        coef = land_ref[top + width:top + row_height, :]
+        dims = (((1,), (1,)), ((), ()))
+        part = lax.dot_general(high, coef, dims, preferred_element_type=jnp.float32)
+        part = part + lax.dot_general(low, coef, dims, preferred_element_type=jnp.float32)
+        fit_ref[...] += part
 
 
 def forward(slots, doc_tiles, doc_norm, land_rows, targets):
@@ -67,18 +75,18 @@
     width = ACTIVE * TERM_BLOCK
     grid_spec = pltpu.PrefetchScalarGridSpec(
         num_scalar_prefetch=1,
-        grid=(block_count,),
+        grid=(block_count // GROUP,),
         in_specs=[
             pl.BlockSpec(doc_tiles.shape, lambda l, s: (0, 0, 0)),
             pl.BlockSpec((doc_rows, 1), lambda l, s: (0, 0)),
-            pl.BlockSpec((row_height, LM_BLOCK), lambda l, s: (l, 0)),
+            pl.BlockSpec((GROUP * row_height, LM_BLOCK), lambda l, s: (l, 0)),
         ],
         out_specs=[
-            pl.BlockSpec((1, doc_rows, LM_BLOCK), lambda l, s: (l, 0, 0)),
-            pl.BlockSpec((1, doc_rows, LM_BLOCK), lambda l, s: (l, 0, 0)),
+            pl.BlockSpec((GROUP, doc_rows, LM_BLOCK), lambda l, s: (l, 0, 0)),
+            pl.BlockSpec((GROUP, doc_rows, LM_BLOCK), lambda l, s: (l, 0, 0)),
             pl.BlockSpec((doc_rows, targets), lambda l, s: (0, 0)),
         ],
-        scratch_shapes=[pltpu.VMEM((doc_rows, width), jnp.bfloat16)],
+        scratch_shapes=[pltpu.VMEM((GROUP, doc_rows, width), jnp.bfloat16)],
     )
     return pl.pallas_call(
         forward_kernel,

time: 141 us -> 149 us (1.057)
  Pallas kernels: 28.2 us -> 35.9 us
    pallas_call x1, Pallas kernels: 28.2 us -> 35.9 us  [forward(): pl.pallas_call(forward_kernel, grid_spec=grid_spec, out_shape=[jax.ShapeD...]
where the time goes in v8:
time: 149 us; the launch traced here: 148 us
  blocking collectives  44.8 us (30%)
  Pallas kernels  35.9 us (24%)
  waiting for transfers between devices  32.4 us (22%)
  between operations  13.6 us (9%)
  local copies, waits for them, and re-layouts  10.8 us (7%)
  other arithmetic  5.87 us (4%)
  matrix products  4.92 us (3%)
    pallas_call x1, Pallas kernels, forward(): pl.pallas_call(forward_kernel, grid_spec=grid_spec, out_shape=[jax.ShapeD...  35.9 us
    all_gather x1, waiting for transfers between devices, on_device(): lax.all_gather(jnp.concatenate([land_values, coefficients], axis=1).T, 'd...  32.4 us
    all_to_all x2, blocking collectives, sum_over(): pieces = lax.all_to_all(pieces, axis, 0, 0, tiled=False)  31.4 us
    all_to_all x1, blocking collectives, all_sum(): return lax.all_to_all(spread, axis, 0, 0, tiled=False).reshape(values.shape)  13.4 us
    unnamed x13, local copies, waits for them, and re-layouts  4.98 us
    dot_general x1, matrix products, on_device(): jnp.einsum('qnl,nt->qlt', tile_high, fitted_pair, preferred_element_type=...  3.92 us
  transfers between devices with their start and end apart: 1, of which 1 were waited for; matrix products, arithmetic and copies ran while one was open for 6% of the time, Pallas kernels for 0%

profile of v8, /device:TPU:1, one launch (start us, length us, event | category | flops | bytes accessed | tf_op | source)
XLA Modules:
  0.0 148.2 jit_solution(13858243329689160435)
XLA Ops:
  6.5 1.3 copy.32
  7.8 1.5 maximum_bitcast_fusion.1
  9.3 0.0 all-gather.2.cloned.1.call-update
  9.3 0.8 copy.29
  10.1 0.8 reshape.40
  10.8 0.3 dynamic-slice_reduce_fusion
  11.1 0.2 compare_reduce_fusion.1
  11.3 0.8 compare_reduce_fusion
  12.2 0.1 copy.30
  12.3 0.1 reshape.41.slot_ref
  12.4 2.6 %multiply_reduce_fusion = f32[1536]{0:T(1024)S(1)} fusion(bf16[1536,1024]{1,0:T(8,128)(2,1)} %param.5), kind=kLoop, calls=%fused_computation | loop fusion | flops 4717056 | bytes 3151872 | tf_op jit(solution)/shard_map/reduce_sum | solution.py:124
  15.0 1.1 mul.11.dn_ref
  16.1 0.8 copy.39
  17.0 0.9 copy.41
  17.8 0.5 pad.4
  18.4 32.4 %all-gather.2.cloned.1.call-done.land_ref = bf16[17408,128]{1,0:T(8,128)(2,1)} async-done(((bf16[1088,128]{1,0:T(8,128)(2,1)}), bf16[17408,128]{1,0:T(8,128)(2,1)}) %all-gather.2.cloned.1.call-update) | async-done | bytes 4456464 | tf_op jit(solution)/shard_map/all_gather | solution.py:128
  50.8 1.1 copy-done
  51.9 35.9 %shard_map.55 = (bf16[16,1536,128]{2,1,0:T(8,128)(2,1)}, bf16[16,1536,128]{2,1,0:T(8,128)(2,1)}, f32[1536,64]{1,0:T(8,128)S(1)}) custom-call(s32[1536]{0:T(1024)S(1)} %reshape.41.slot_ref, bf16[108,128,128]{2,1,0:T(8,128)(2,1)S(1)} %bitcast.20, f32[1536,1]{1,0:T(8,128)S(1)} %copy-done, bf16[17408,128]{1,0:T(8,128)(2,1)} %all-gather.2.cloned.1.call-done.land_ref), custom_call_target="tpu_custom_call" | custom-call | tf_op jit(solution)/shard_map/pallas_call | solution.py:91
  87.8 0.9 copy-done.1
  88.8 1.4 copy.34
  90.2 16.0 %all_to_all.15 = f32[8,192,64]{1,2,0:T(8,128)S(1)} all-to-all(f32[8,192,64]{1,2,0:T(8,128)S(1)} %copy.34), channel_id=1, replica_groups=mesh['dp'=16,'land'=8] {'land'}, dimensions={0} | all-to-all | bytes 786432 | tf_op jit(solution)/shard_map/all_to_all | solution.py:106
  106.2 0.0 slice-start
  106.3 13.4 %all_to_all.16 = f32[8,192,64]{1,2,0:T(8,128)S(1)} all-to-all(f32[8,192,64]{1,2,0:T(8,128)S(1)} %broadcast_in_dim.12), channel_id=1, replica_groups=mesh['dp'=16,'land'=8] {'land'}, dimensions={0} | all-to-all | bytes 786432 | tf_op jit(solution)/shard_map/all_to_all | solution.py:113
  119.7 0.3 copy.37
  120.0 0.2 reshape.45
  120.3 0.0 slice-start.1
  120.3 3.9 %fusion = f32[16,128,128]{1,2,0:T(8,128)S(1)} fusion(bf16[16,1536,128]{2,1,0:T(8,128)(2,1)} %get-tuple-element.10, bf16[1536,64]{0,1:T(8,128)(2,1)S(1)} %subtract_convert_fusion, bf16[1536,64]{0,1:T(8,128)(2,1)S(1)} %convert_element_type.15), kind=kOutput, calls=%fused_computation.9 | convolution fusion | flops 806092800 | bytes 7733248 | tf_op jit(solution)/shard_map/qnl,nt->qlt/dot_general | solution.py:139
  124.2 0.1 slice-done.1
  124.3 1.0 convolution_add_fusion
  125.3 0.1 slice_add_fusion
  125.4 15.4 %all_to_all.17 = f32[16,128,64]{1,2,0:T(8,128)S(1)} all-to-all(f32[16,128,64]{1,2,0:T(8,128)S(1)} %slice_add_fusion), channel_id=1, replica_groups=mesh['dp'=16,'land'=8] {'dp'}, dimensions={0} | all-to-all | bytes 1048576 | tf_op jit(solution)/shard_map/all_to_all | solution.py:106
  140.8 0.6 broadcast_multiply_fusion
  (14 shorter events, 0.2 us)
Async XLA Ops:
  6.5 9.6 %copy-start.2 = (bf16[1536,1024]{1,0:T(8,128)(2,1)S(1)}, bf16[1536,1024]{1,0:T(8,128)(2,1)}, u32[]{:S(2)}) copy-start(bf16[1536,1024]{1,0:T(8,128)(2,1)} %param.5) | copy-start | bytes 9437188
  6.5 44.3 %all-gather.2.cloned.1.call-start = ((), (), s32[]{:S(2)}) async-start(), calls=%async_computation.3 | async-start | bytes 4734976 | tf_op jit(solution)/shard_map/all_gather | solution.py:128
  50.8 1.1 copy-start
  87.8 0.9 copy-start.1
  106.2 18.0 %slice-start = ((s8[6291456]{0:T(1024)(128)(4,1)}), s8[2097152]{0:T(1024)(128)(4,1)S(1)}, s32[]{:S(2)}) async-start(s8[6291456]{0:T(1024)(128)(4,1)} %bitcast.25), calls=%async_computation.4 | async-start | bytes 4194304
  120.3 4.0 %slice-start.1 = ((s8[6291456]{0:T(1024)(128)(4,1)}), s8[4194304]{0:T(1024)(128)(4,1)S(1)}, s32[]{:S(2)}) async-start(s8[6291456]{0:T(1024)(128)(4,1)} %bitcast.25), calls=%async_computation.5 | async-start | bytes 8388608
Sparse Core Ops, SparseCore 0:
  9.4 41.3 all-gather.1

commit v9 on v6

--- a/solution.py
+++ b/solution.py
@@ -53,10 +53,10 @@
     high_ref[0] = high
     low_ref[0] = low
     coef = land_ref[width:, :]
+    pair = jnp.concatenate([high, low], axis=1)
+    coef_pair = jnp.concatenate([coef, coef], axis=1)
     dims = (((1,), (1,)), ((), ()))
-    part = lax.dot_general(high, coef, dims, preferred_element_type=jnp.float32)
-    part = part + lax.dot_general(low, coef, dims, preferred_element_type=jnp.float32)
-    fit_ref[...] += part
+    fit_ref[...] += lax.dot_general(pair, coef_pair, dims, preferred_element_type=jnp.float32)
 
 
 def forward(slots, doc_tiles, doc_norm, land_rows, targets):

time: 141 us -> 138 us (0.979)
  Pallas kernels: 28.2 us -> 24.9 us
    pallas_call x1, Pallas kernels: 28.2 us -> 24.9 us  [forward(): pl.pallas_call(forward_kernel, grid_spec=grid_spec, out_shape=[jax.ShapeD...]
  transfers between devices with their start and end apart: 1 -> 1, of which waited for: 1 -> 1; matrix products, arithmetic and copies ran while one was open for 6% -> 7% of each run, Pallas kernels for 0% -> 0%
where the time goes in v9:
time: 138 us; the launch traced here: 137 us
  blocking collectives  44.8 us (32%)
  waiting for transfers between devices  32.4 us (23%)
  Pallas kernels  24.9 us (18%)
  between operations  13.6 us (10%)
  local copies, waits for them, and re-layouts  10.8 us (8%)
  other arithmetic  5.87 us (4%)
  matrix products  4.92 us (4%)
    all_gather x1, waiting for transfers between devices, on_device(): lax.all_gather(jnp.concatenate([land_values, coefficients], axis=1).T, 'd...  32.4 us
    all_to_all x2, blocking collectives, sum_over(): pieces = lax.all_to_all(pieces, axis, 0, 0, tiled=False)  31.3 us
    pallas_call x1, Pallas kernels, forward(): pl.pallas_call(forward_kernel, grid_spec=grid_spec, out_shape=[jax.ShapeD...  24.9 us
    all_to_all x1, blocking collectives, all_sum(): return lax.all_to_all(spread, axis, 0, 0, tiled=False).reshape(values.shape)  13.4 us
    unnamed x13, local copies, waits for them, and re-layouts  4.98 us
    dot_general x1, matrix products, on_device(): jnp.einsum('qnl,nt->qlt', tile_high, fitted_pair, preferred_element_type=...  3.92 us
  transfers between devices with their start and end apart: 1, of which 1 were waited for; matrix products, arithmetic and copies ran while one was open for 7% of the time, Pallas kernels for 0%

profile of v9, /device:TPU:1, one launch (start us, length us, event | category | flops | bytes accessed | tf_op | source)
XLA Modules:
  0.0 137.2 jit_solution(12146877362318604937)
XLA Ops:
  6.5 1.3 copy.32
  7.8 1.5 %maximum_bitcast_fusion.1 = bf16[1088,128]{1,0:T(8,128)(2,1)} fusion(bf16[128,64]{0,1:T(8,128)(2,1)} %param.9, bf16[128,1024]{0,1:T(8,128)(2,1)S(1)} %copy.32), kind=kLoop, calls=%fused_computation.8 | loop fusion | flops 557056 | bytes 557056 | tf_op jit(solution)/shard_map/transpose | solution.py:121
  9.3 0.0 all-gather.2.cloned.1.call-update
  9.3 0.8 copy.29
  10.1 0.8 reshape.40
  10.8 0.3 dynamic-slice_reduce_fusion
  11.1 0.2 compare_reduce_fusion.1
  11.3 0.8 compare_reduce_fusion
  12.2 0.1 copy.30
  12.3 0.1 reshape.41.slot_ref
  12.4 2.6 %multiply_reduce_fusion = f32[1536]{0:T(1024)S(1)} fusion(bf16[1536,1024]{1,0:T(8,128)(2,1)} %param.5), kind=kLoop, calls=%fused_computation | loop fusion | flops 4717056 | bytes 3151872 | tf_op jit(solution)/shard_map/reduce_sum | solution.py:116
  15.0 1.1 mul.11.dn_ref
  16.1 0.8 copy.39
  17.0 0.9 copy.41
  17.8 0.5 pad.4
  18.4 32.4 %all-gather.2.cloned.1.call-done.land_ref = bf16[17408,128]{1,0:T(8,128)(2,1)} async-done(((bf16[1088,128]{1,0:T(8,128)(2,1)}), bf16[17408,128]{1,0:T(8,128)(2,1)}) %all-gather.2.cloned.1.call-update) | async-done | bytes 4456464 | tf_op jit(solution)/shard_map/all_gather | solution.py:120
  50.8 1.1 copy-done
  51.9 24.9 %shard_map.55 = (bf16[16,1536,128]{2,1,0:T(8,128)(2,1)}, bf16[16,1536,128]{2,1,0:T(8,128)(2,1)}, f32[1536,64]{1,0:T(8,128)S(1)}) custom-call(s32[1536]{0:T(1024)S(1)} %reshape.41.slot_ref, bf16[108,128,128]{2,1,0:T(8,128)(2,1)S(1)} %bitcast.20, f32[1536,1]{1,0:T(8,128)S(1)} %copy-done, bf16[17408,128]{1,0:T(8,128)(2,1)} %all-gather.2.cloned.1.call-done.land_ref), custom_call_target="tpu_custom_call" | custom-call | tf_op jit(solution)/shard_map/pallas_call | solution.py:83
  76.8 0.9 copy-done.1
  77.8 1.4 %copy.34 = f32[8,192,64]{1,2,0:T(8,128)S(1)} copy(f32[8,192,64]{2,1,0:T(8,128)} %bitcast.21) | data formatting | bytes 786432 | tf_op jit(solution)/shard_map/reshape | solution.py:97
  79.2 16.0 %all_to_all.15 = f32[8,192,64]{1,2,0:T(8,128)S(1)} all-to-all(f32[8,192,64]{1,2,0:T(8,128)S(1)} %copy.34), channel_id=1, replica_groups=mesh['dp'=16,'land'=8] {'land'}, dimensions={0} | all-to-all | bytes 786432 | tf_op jit(solution)/shard_map/all_to_all | solution.py:98
  95.2 0.0 slice-start
  95.3 13.4 %all_to_all.16 = f32[8,192,64]{1,2,0:T(8,128)S(1)} all-to-all(f32[8,192,64]{1,2,0:T(8,128)S(1)} %broadcast_in_dim.12), channel_id=1, replica_groups=mesh['dp'=16,'land'=8] {'land'}, dimensions={0} | all-to-all | bytes 786432 | tf_op jit(solution)/shard_map/all_to_all | solution.py:105
  108.7 0.3 copy.37
  109.0 0.2 reshape.45
  109.3 0.0 slice-start.1
  109.3 3.9 %fusion = f32[16,128,128]{1,2,0:T(8,128)S(1)} fusion(bf16[16,1536,128]{2,1,0:T(8,128)(2,1)} %get-tuple-element.10, bf16[1536,64]{0,1:T(8,128)(2,1)S(1)} %subtract_convert_fusion, bf16[1536,64]{0,1:T(8,128)(2,1)S(1)} %convert_element_type.15), kind=kOutput, calls=%fused_computation.9 | convolution fusion | flops 806092800 | bytes 7733248 | tf_op jit(solution)/shard_map/qnl,nt->qlt/dot_general | solution.py:131
  113.2 0.1 slice-done.1
  113.3 1.0 convolution_add_fusion
  114.3 0.1 slice_add_fusion
  114.4 15.4 %all_to_all.17 = f32[16,128,64]{1,2,0:T(8,128)S(1)} all-to-all(f32[16,128,64]{1,2,0:T(8,128)S(1)} %slice_add_fusion), channel_id=1, replica_groups=mesh['dp'=16,'land'=8] {'dp'}, dimensions={0} | all-to-all | bytes 1048576 | tf_op jit(solution)/shard_map/all_to_all | solution.py:98
  129.8 0.6 broadcast_multiply_fusion
  (14 shorter events, 0.2 us)
Async XLA Ops:
  6.5 9.6 %copy-start.2 = (bf16[1536,1024]{1,0:T(8,128)(2,1)S(1)}, bf16[1536,1024]{1,0:T(8,128)(2,1)}, u32[]{:S(2)}) copy-start(bf16[1536,1024]{1,0:T(8,128)(2,1)} %param.5) | copy-start | bytes 9437188
  6.5 44.3 %all-gather.2.cloned.1.call-start = ((), (), s32[]{:S(2)}) async-start(), calls=%async_computation.3 | async-start | bytes 4734976 | tf_op jit(solution)/shard_map/all_gather | solution.py:120
  50.8 1.1 copy-start
  76.8 0.9 copy-start.1
  95.2 18.0 %slice-start = ((s8[6291456]{0:T(1024)(128)(4,1)}), s8[2097152]{0:T(1024)(128)(4,1)S(1)}, s32[]{:S(2)}) async-start(s8[6291456]{0:T(1024)(128)(4,1)} %bitcast.25), calls=%async_computation.4 | async-start | bytes 4194304
  109.3 4.0 %slice-start.1 = ((s8[6291456]{0:T(1024)(128)(4,1)}), s8[4194304]{0:T(1024)(128)(4,1)S(1)}, s32[]{:S(2)}) async-start(s8[6291456]{0:T(1024)(128)(4,1)} %bitcast.25), calls=%async_computation.5 | async-start | bytes 8388608
Sparse Core Ops, SparseCore 0:
  9.4 41.3 all-gather.1

commit v10 on v9

--- a/solution.py
+++ b/solution.py
@@ -29,7 +29,7 @@
 
 
 def forward_kernel(slot_ref, doc_ref, dn_ref, land_ref,
-                   high_ref, low_ref, fit_ref, aligned_ref):
+                   tile_ref, fit_ref, aligned_ref):
     step = pl.program_id(0)
     doc_count = dn_ref.shape[0] // DOC_BLOCK
 
@@ -50,8 +50,8 @@
     kern = jnp.exp(inner * dn_ref[...] * land_norm - 2.0 * sharpness)
     high = kern.astype(jnp.bfloat16)
     low = (kern - high.astype(jnp.float32)).astype(jnp.bfloat16)
-    high_ref[0] = high
-    low_ref[0] = low
+    tile_ref[0, 0] = high
+    tile_ref[0, 1] = low
     coef = land_ref[width:, :]
     pair = jnp.concatenate([high, low], axis=1)
     coef_pair = jnp.concatenate([coef, coef], axis=1)
@@ -74,8 +74,7 @@
             pl.BlockSpec((row_height, LM_BLOCK), lambda l, s: (l, 0)),
         ],
         out_specs=[
-            pl.BlockSpec((1, doc_rows, LM_BLOCK), lambda l, s: (l, 0, 0)),
-            pl.BlockSpec((1, doc_rows, LM_BLOCK), lambda l, s: (l, 0, 0)),
+            pl.BlockSpec((1, 2, doc_rows, LM_BLOCK), lambda l, s: (l, 0, 0, 0)),
             pl.BlockSpec((doc_rows, targets), lambda l, s: (0, 0)),
         ],
         scratch_shapes=[pltpu.VMEM((doc_rows, width), jnp.bfloat16)],
@@ -84,8 +83,7 @@
         forward_kernel,
         grid_spec=grid_spec,
         out_shape=[
-            jax.ShapeDtypeStruct((block_count, doc_rows, LM_BLOCK), jnp.bfloat16),
-            jax.ShapeDtypeStruct((block_count, doc_rows, LM_BLOCK), jnp.bfloat16),
+            jax.ShapeDtypeStruct((block_count, 2, doc_rows, LM_BLOCK), jnp.bfloat16),
             jax.ShapeDtypeStruct((doc_rows, targets), jnp.float32),
         ],
         compiler_params=pltpu.CompilerParams(
@@ -123,13 +121,13 @@
     doc_tiles = jnp.pad(doc_tiles, ((0, 0), (0, 1), (0, 0), (0, 0)))
     doc_tiles = doc_tiles.reshape(doc_count * (ACTIVE + 1), DOC_BLOCK, TERM_BLOCK)
     slots = match_table(doc_blocks, own_table)
-    tile_high, tile_low, fitted = forward(
+    tiles, fitted = forward(
         slots, doc_tiles, (2.0 * sharpness) * doc_norm.reshape(doc_rows, 1), land_rows, targets)
     fitted = all_sum(fitted, "land", land_count)
     fitted_high, fitted_low = split_pair(fitted)
     fitted_pair = jnp.concatenate([fitted_high, fitted_low], axis=1)
-    summed = jnp.einsum("qnl,nt->qlt", tile_high, fitted_pair, preferred_element_type=jnp.float32)
-    summed = summed + jnp.einsum("qnl,nt->qlt", tile_low, fitted_pair, preferred_element_type=jnp.float32)
+    pairs = jnp.stack([fitted_pair, fitted_pair])
+    summed = jnp.einsum("qsnl,snt->qlt", tiles, pairs, preferred_element_type=jnp.float32)
     summed = (summed[:, :, :targets] + summed[:, :, targets:]).reshape(-1, targets)
     result = sum_over(summed, "dp", dp_count)
     return result / total_docs

time: 138 us -> 139 us (level)
  matrix products: 4.92 us -> 6.37 us
    dot_general x2 -> x1, matrix products: 4.92 us -> 6.37 us  [on_device(): jnp.einsum('qsnl,snt->qlt', tiles, pairs, preferred_element_type=jnp.floa...]
    unnamed x13 -> x9, local copies, waits for them, and re-layouts: 4.98 us -> 4.91 us
  transfers between devices with their start and end apart: 1 -> 1, of which waited for: 1 -> 1; matrix products, arithmetic and copies ran while one was open for 7% -> 6% of each run, Pallas kernels for 0% -> 0%
where the time goes in v10:
time: 139 us
  blocking collectives  44.7 us (32%)
  waiting for transfers between devices  32.6 us (23%)
  Pallas kernels  25.3 us (18%)
  between operations  13.5 us (10%)
  local copies, waits for them, and re-layouts  10.5 us (8%)
  matrix products  6.37 us (5%)
  other arithmetic  5.91 us (4%)
    all_gather x1, waiting for transfers between devices, on_device(): lax.all_gather(jnp.concatenate([land_values, coefficients], axis=1).T, 'd...  32.6 us
    all_to_all x2, blocking collectives, sum_over(): pieces = lax.all_to_all(pieces, axis, 0, 0, tiled=False)  31.3 us
    pallas_call x1, Pallas kernels, forward(): pl.pallas_call(forward_kernel, grid_spec=grid_spec, out_shape=[jax.ShapeD...  25.3 us
    all_to_all x1, blocking collectives, all_sum(): return lax.all_to_all(spread, axis, 0, 0, tiled=False).reshape(values.shape)  13.4 us
    dot_general x1, matrix products, on_device(): jnp.einsum('qsnl,snt->qlt', tiles, pairs, preferred_element_type=jnp.floa...  6.37 us
    unnamed x9, local copies, waits for them, and re-layouts  4.91 us
  transfers between devices with their start and end apart: 1, of which 1 were waited for; matrix products, arithmetic and copies ran while one was open for 6% of the time, Pallas kernels for 0%

profile of v10, /device:TPU:1, one launch (start us, length us, event | category | flops | bytes accessed | tf_op | source)
XLA Modules:
  0.0 138.9 jit_solution(10482939943588953953)
XLA Ops:
  6.5 0.0 copy-start.2
  6.5 0.0 all-gather.2.cloned.1.call-start
  6.5 1.3 copy.32
  7.8 1.5 %maximum_bitcast_fusion.3 = bf16[1088,128]{1,0:T(8,128)(2,1)} fusion(bf16[128,64]{0,1:T(8,128)(2,1)} %param.9, bf16[128,1024]{0,1:T(8,128)(2,1)S(1)} %copy.32), kind=kLoop, calls=%fused_computation.11 | loop fusion | flops 557056 | bytes 557056 | tf_op jit(solution)/shard_map/transpose | solution.py:119
  9.3 0.0 all-gather.2.cloned.1.call-update
  9.3 0.8 copy.29
  10.1 0.8 reshape.40
  10.8 0.3 dynamic-slice_reduce_fusion
  11.1 0.2 compare_reduce_fusion.1
  11.3 0.8 compare_reduce_fusion
  12.2 0.1 copy.30
  12.3 0.1 reshape.41.slot_ref
  12.4 2.6 %multiply_reduce_fusion = f32[1536]{0:T(1024)S(1)} fusion(bf16[1536,1024]{1,0:T(8,128)(2,1)} %param.5), kind=kLoop, calls=%fused_computation | loop fusion | flops 4717056 | bytes 3151872 | tf_op jit(solution)/shard_map/reduce_sum | solution.py:114
  15.0 1.1 mul.11.dn_ref
  16.1 0.0 copy-done.2
  16.1 0.8 copy.40
  17.0 0.9 copy.42
  17.8 0.4 pad.4
  18.2 32.6 %all-gather.2.cloned.1.call-done.land_ref = bf16[17408,128]{1,0:T(8,128)(2,1)} async-done(((bf16[1088,128]{1,0:T(8,128)(2,1)}), bf16[17408,128]{1,0:T(8,128)(2,1)}) %all-gather.2.cloned.1.call-update) | async-done | bytes 4456464 | tf_op jit(solution)/shard_map/all_gather | solution.py:118
  50.8 1.1 copy-done
  51.9 25.3 %shard_map.55 = (bf16[16,2,1536,128]{3,2,1,0:T(8,128)(2,1)}, f32[1536,64]{1,0:T(8,128)S(1)}) custom-call(s32[1536]{0:T(1024)S(1)} %reshape.41.slot_ref, bf16[108,128,128]{2,1,0:T(8,128)(2,1)S(1)} %bitcast.23, f32[1536,1]{1,0:T(8,128)S(1)} %copy-done, bf16[17408,128]{1,0:T(8,128)(2,1)} %all-gather.2.cloned.1.call-done.land_ref), custom_call_target="tpu_custom_call" | custom-call | tf_op jit(solution)/shard_map/pallas_call | solution.py:82
  77.3 0.9 copy-done.1
  78.2 1.4 %copy.34 = f32[8,192,64]{1,2,0:T(8,128)S(1)} copy(f32[8,192,64]{2,1,0:T(8,128)} %bitcast.24) | data formatting | bytes 786432 | tf_op jit(solution)/shard_map/reshape | solution.py:95
  79.6 15.9 %all_to_all.15 = f32[8,192,64]{1,2,0:T(8,128)S(1)} all-to-all(f32[8,192,64]{1,2,0:T(8,128)S(1)} %copy.34), channel_id=1, replica_groups=mesh['dp'=16,'land'=8] {'land'}, dimensions={0} | all-to-all | bytes 786432 | tf_op jit(solution)/shard_map/all_to_all | solution.py:96
  95.6 13.4 %all_to_all.16 = f32[8,192,64]{1,2,0:T(8,128)S(1)} all-to-all(f32[8,192,64]{1,2,0:T(8,128)S(1)} %broadcast_in_dim.12), channel_id=1, replica_groups=mesh['dp'=16,'land'=8] {'land'}, dimensions={0} | all-to-all | bytes 786432 | tf_op jit(solution)/shard_map/all_to_all | solution.py:103
  109.0 0.3 copy.37
  109.3 0.2 reshape.45
  109.6 0.1 subtract_convert_fusion
  109.7 6.4 %convolution_bitcast_fusion = f32[16,128,128]{1,2,0:T(8,128)S(1)} fusion(bf16[16,2,1536,128]{3,2,1,0:T(8,128)(2,1)} %get-tuple-element.9, bf16[1,1536,128]{1,2,0:T(8,128)(2,1)S(1)} %maximum_bitcast_fusion.2), kind=kOutput, calls=%fused_computation.2 | convolution fusion | flops 1612185600 | bytes 14024704 | tf_op jit(solution)/shard_map/qsnl,snt->qlt/dot_general | solution.py:130
  116.0 0.1 slice_add_fusion
  116.1 15.4 %all_to_all.17 = f32[16,128,64]{1,2,0:T(8,128)S(1)} all-to-all(f32[16,128,64]{1,2,0:T(8,128)S(1)} %slice_add_fusion), channel_id=1, replica_groups=mesh['dp'=16,'land'=8] {'dp'}, dimensions={0} | all-to-all | bytes 1048576 | tf_op jit(solution)/shard_map/all_to_all | solution.py:96
  131.5 0.6 broadcast_multiply_fusion
  (9 shorter events, 0.2 us)
Async XLA Ops:
  6.5 9.6 %copy-start.2 = (bf16[1536,1024]{1,0:T(8,128)(2,1)S(1)}, bf16[1536,1024]{1,0:T(8,128)(2,1)}, u32[]{:S(2)}) copy-start(bf16[1536,1024]{1,0:T(8,128)(2,1)} %param.5) | copy-start | bytes 9437188
  6.5 44.3 %all-gather.2.cloned.1.call-start = ((), (), s32[]{:S(2)}) async-start(), calls=%async_computation.3 | async-start | bytes 4734976 | tf_op jit(solution)/shard_map/all_gather | solution.py:118
  50.8 1.1 copy-start
  77.3 0.9 copy-start.1
Sparse Core Ops, SparseCore 0:
  9.4 41.3 all-gather.1

commit v11 on v9

--- a/solution.py
+++ b/solution.py
@@ -55,6 +55,7 @@
     coef = land_ref[width:, :]
     pair = jnp.concatenate([high, low], axis=1)
     coef_pair = jnp.concatenate([coef, coef], axis=1)
+    coef_pair = jnp.concatenate([coef_pair, jnp.zeros_like(coef_pair)], axis=0)
     dims = (((1,), (1,)), ((), ()))
     fit_ref[...] += lax.dot_general(pair, coef_pair, dims, preferred_element_type=jnp.float32)
 
@@ -76,21 +77,22 @@
         out_specs=[
             pl.BlockSpec((1, doc_rows, LM_BLOCK), lambda l, s: (l, 0, 0)),
             pl.BlockSpec((1, doc_rows, LM_BLOCK), lambda l, s: (l, 0, 0)),
-            pl.BlockSpec((doc_rows, targets), lambda l, s: (0, 0)),
+            pl.BlockSpec((doc_rows, 2 * targets), lambda l, s: (0, 0)),
         ],
         scratch_shapes=[pltpu.VMEM((doc_rows, width), jnp.bfloat16)],
     )
-    return pl.pallas_call(
+    high, low, fitted = pl.pallas_call(
         forward_kernel,
         grid_spec=grid_spec,
         out_shape=[
             jax.ShapeDtypeStruct((block_count, doc_rows, LM_BLOCK), jnp.bfloat16),
             jax.ShapeDtypeStruct((block_count, doc_rows, LM_BLOCK), jnp.bfloat16),
-            jax.ShapeDtypeStruct((doc_rows, targets), jnp.float32),
+            jax.ShapeDtypeStruct((doc_rows, 2 * targets), jnp.float32),
         ],
         compiler_params=pltpu.CompilerParams(
             dimension_semantics=("arbitrary",), vmem_limit_bytes=48 * 1024 * 1024),
     )(slots, doc_tiles, doc_norm, land_rows)
+    return high, low, fitted[:, :targets]
 
 
 def sum_over(values, axis, count):

time: 138 us -> 138 us (level)
  no operation moved by 1% of the time
where the time goes in v11:
time: 138 us; the launch traced here: 137 us
  blocking collectives  44.8 us (32%)
  waiting for transfers between devices  32.4 us (23%)
  Pallas kernels  24.9 us (18%)
  between operations  13.6 us (10%)
  local copies, waits for them, and re-layouts  10.8 us (8%)
  other arithmetic  5.87 us (4%)
  matrix products  4.92 us (4%)
    all_gather x1, waiting for transfers between devices, on_device(): lax.all_gather(jnp.concatenate([land_values, coefficients], axis=1).T, 'd...  32.4 us
    all_to_all x2, blocking collectives, sum_over(): pieces = lax.all_to_all(pieces, axis, 0, 0, tiled=False)  31.3 us
    pallas_call x1, Pallas kernels, forward(): pl.pallas_call(forward_kernel, grid_spec=grid_spec, out_shape=[jax.ShapeD...  24.9 us
    all_to_all x1, blocking collectives, all_sum(): return lax.all_to_all(spread, axis, 0, 0, tiled=False).reshape(values.shape)  13.4 us
    unnamed x13, local copies, waits for them, and re-layouts  4.98 us
    dot_general x1, matrix products, on_device(): jnp.einsum('qnl,nt->qlt', tile_high, fitted_pair, preferred_element_type=...  3.92 us
  transfers between devices with their start and end apart: 1, of which 1 were waited for; matrix products, arithmetic and copies ran while one was open for 7% of the time, Pallas kernels for 0%

profile of v11, /device:TPU:1, one launch (start us, length us, event | category | flops | bytes accessed | tf_op | source)
XLA Modules:
  0.0 137.2 jit_solution(4948900720446275928)
XLA Ops:
  6.5 1.3 copy.32
  7.8 1.5 %maximum_bitcast_fusion.1 = bf16[1088,128]{1,0:T(8,128)(2,1)} fusion(bf16[128,64]{0,1:T(8,128)(2,1)} %param.9, bf16[128,1024]{0,1:T(8,128)(2,1)S(1)} %copy.32), kind=kLoop, calls=%fused_computation.8 | loop fusion | flops 557056 | bytes 557056 | tf_op jit(solution)/shard_map/transpose | solution.py:123
  9.3 0.0 all-gather.2.cloned.1.call-update
  9.3 0.8 copy.29
  10.1 0.8 reshape.40
  10.8 0.3 dynamic-slice_reduce_fusion
  11.1 0.2 compare_reduce_fusion.1
  11.3 0.8 compare_reduce_fusion
  12.2 0.1 copy.30
  12.3 0.1 reshape.41.slot_ref
  12.4 2.6 %multiply_reduce_fusion = f32[1536]{0:T(1024)S(1)} fusion(bf16[1536,1024]{1,0:T(8,128)(2,1)} %param.5), kind=kLoop, calls=%fused_computation | loop fusion | flops 4717056 | bytes 3151872 | tf_op jit(solution)/shard_map/reduce_sum | solution.py:118
  15.0 1.1 mul.11.dn_ref
  16.1 0.8 copy.39
  17.0 0.9 copy.41
  17.8 0.5 pad.4
  18.4 32.4 %all-gather.2.cloned.1.call-done.land_ref = bf16[17408,128]{1,0:T(8,128)(2,1)} async-done(((bf16[1088,128]{1,0:T(8,128)(2,1)}), bf16[17408,128]{1,0:T(8,128)(2,1)}) %all-gather.2.cloned.1.call-update) | async-done | bytes 4456464 | tf_op jit(solution)/shard_map/all_gather | solution.py:122
  50.8 1.1 copy-done
  51.9 24.9 %shard_map.55 = (bf16[16,1536,128]{2,1,0:T(8,128)(2,1)}, bf16[16,1536,128]{2,1,0:T(8,128)(2,1)}, f32[1536,128]{1,0:T(8,128)S(1)}) custom-call(s32[1536]{0:T(1024)S(1)} %reshape.41.slot_ref, bf16[108,128,128]{2,1,0:T(8,128)(2,1)S(1)} %bitcast.21, f32[1536,1]{1,0:T(8,128)S(1)} %copy-done, bf16[17408,128]{1,0:T(8,128)(2,1)} %all-gather.2.cloned.1.call-done.land_ref), custom_call_target="tpu_custom_call" | custom-call | tf_op jit(solution)/shard_map/pallas_call | solution.py:84
  76.8 0.9 copy-done.1
  77.8 1.4 %copy.34 = f32[8,192,64]{1,2,0:T(8,128)S(1)} copy(f32[8,192,64]{2,1,0:T(8,128)} %bitcast.22) | data formatting | bytes 786432 | tf_op jit(solution)/shard_map/reshape | solution.py:99
  79.2 16.0 %all_to_all.15 = f32[8,192,64]{1,2,0:T(8,128)S(1)} all-to-all(f32[8,192,64]{1,2,0:T(8,128)S(1)} %copy.34), channel_id=1, replica_groups=mesh['dp'=16,'land'=8] {'land'}, dimensions={0} | all-to-all | bytes 786432 | tf_op jit(solution)/shard_map/all_to_all | solution.py:100
  95.2 0.0 slice-start
  95.3 13.4 %all_to_all.16 = f32[8,192,64]{1,2,0:T(8,128)S(1)} all-to-all(f32[8,192,64]{1,2,0:T(8,128)S(1)} %broadcast_in_dim.12), channel_id=1, replica_groups=mesh['dp'=16,'land'=8] {'land'}, dimensions={0} | all-to-all | bytes 786432 | tf_op jit(solution)/shard_map/all_to_all | solution.py:107
  108.7 0.3 copy.37
  109.0 0.2 reshape.45
  109.3 0.0 slice-start.1
  109.3 3.9 %fusion = f32[16,128,128]{1,2,0:T(8,128)S(1)} fusion(bf16[16,1536,128]{2,1,0:T(8,128)(2,1)} %get-tuple-element.10, bf16[1536,64]{0,1:T(8,128)(2,1)S(1)} %subtract_convert_fusion, bf16[1536,64]{0,1:T(8,128)(2,1)S(1)} %convert_element_type.15), kind=kOutput, calls=%fused_computation.9 | convolution fusion | flops 806092800 | bytes 7733248 | tf_op jit(solution)/shard_map/qnl,nt->qlt/dot_general | solution.py:133
  113.2 0.1 slice-done.1
  113.3 1.0 convolution_add_fusion
  114.3 0.1 slice_add_fusion
  114.4 15.4 %all_to_all.17 = f32[16,128,64]{1,2,0:T(8,128)S(1)} all-to-all(f32[16,128,64]{1,2,0:T(8,128)S(1)} %slice_add_fusion), channel_id=1, replica_groups=mesh['dp'=16,'land'=8] {'dp'}, dimensions={0} | all-to-all | bytes 1048576 | tf_op jit(solution)/shard_map/all_to_all | solution.py:100
  129.8 0.6 broadcast_multiply_fusion
  (14 shorter events, 0.2 us)
Async XLA Ops:
  6.5 9.6 %copy-start.2 = (bf16[1536,1024]{1,0:T(8,128)(2,1)S(1)}, bf16[1536,1024]{1,0:T(8,128)(2,1)}, u32[]{:S(2)}) copy-start(bf16[1536,1024]{1,0:T(8,128)(2,1)} %param.5) | copy-start | bytes 9437188
  6.5 44.3 %all-gather.2.cloned.1.call-start = ((), (), s32[]{:S(2)}) async-start(), calls=%async_computation.3 | async-start | bytes 4734976 | tf_op jit(solution)/shard_map/all_gather | solution.py:122
  50.8 1.1 copy-start
  76.8 0.9 copy-start.1
  95.2 18.0 %slice-start = ((s8[6291456]{0:T(1024)(128)(4,1)}), s8[2097152]{0:T(1024)(128)(4,1)S(1)}, s32[]{:S(2)}) async-start(s8[6291456]{0:T(1024)(128)(4,1)} %bitcast.26), calls=%async_computation.4 | async-start | bytes 4194304
  109.3 4.0 %slice-start.1 = ((s8[6291456]{0:T(1024)(128)(4,1)}), s8[4194304]{0:T(1024)(128)(4,1)S(1)}, s32[]{:S(2)}) async-start(s8[6291456]{0:T(1024)(128)(4,1)} %bitcast.26), calls=%async_computation.5 | async-start | bytes 8388608
Sparse Core Ops, SparseCore 0:
  9.4 41.3 all-gather.1

commit v12 on v9

--- a/solution.py
+++ b/solution.py
@@ -28,7 +28,7 @@
     return jnp.where(has, first, ACTIVE).astype(jnp.int32).reshape(-1)
 
 
-def forward_kernel(slot_ref, doc_ref, dn_ref, land_ref,
+def forward_kernel(slot_ref, block_ref, doc_ref, dn_ref, land_ref,
                    high_ref, low_ref, fit_ref, aligned_ref):
     step = pl.program_id(0)
     doc_count = dn_ref.shape[0] // DOC_BLOCK
@@ -59,24 +59,24 @@
     fit_ref[...] += lax.dot_general(pair, coef_pair, dims, preferred_element_type=jnp.float32)
 
 
-def forward(slots, doc_tiles, doc_norm, land_rows, targets):
+def forward(slots, doc_tiles, doc_norm, land_rows, targets, blocks):
     doc_rows = doc_norm.shape[0]
     row_height = ACTIVE * TERM_BLOCK + targets
-    block_count = land_rows.shape[0] // row_height
+    block_count = blocks.shape[0]
     land_count = block_count * LM_BLOCK
     width = ACTIVE * TERM_BLOCK
     grid_spec = pltpu.PrefetchScalarGridSpec(
-        num_scalar_prefetch=1,
+        num_scalar_prefetch=2,
         grid=(block_count,),
         in_specs=[
-            pl.BlockSpec(doc_tiles.shape, lambda l, s: (0, 0, 0)),
-            pl.BlockSpec((doc_rows, 1), lambda l, s: (0, 0)),
-            pl.BlockSpec((row_height, LM_BLOCK), lambda l, s: (l, 0)),
+            pl.BlockSpec(doc_tiles.shape, lambda l, s, k: (0, 0, 0)),
+            pl.BlockSpec((doc_rows, 1), lambda l, s, k: (0, 0)),
+            pl.BlockSpec((row_height, LM_BLOCK), lambda l, s, k: (k[l], 0)),
         ],
         out_specs=[
-            pl.BlockSpec((1, doc_rows, LM_BLOCK), lambda l, s: (l, 0, 0)),
-            pl.BlockSpec((1, doc_rows, LM_BLOCK), lambda l, s: (l, 0, 0)),
-            pl.BlockSpec((doc_rows, targets), lambda l, s: (0, 0)),
+            pl.BlockSpec((1, doc_rows, LM_BLOCK), lambda l, s, k: (l, 0, 0)),
+            pl.BlockSpec((1, doc_rows, LM_BLOCK), lambda l, s, k: (l, 0, 0)),
+            pl.BlockSpec((doc_rows, targets), lambda l, s, k: (0, 0)),
         ],
         scratch_shapes=[pltpu.VMEM((doc_rows, width), jnp.bfloat16)],
     )
@@ -90,7 +90,7 @@
         ],
         compiler_params=pltpu.CompilerParams(
             dimension_semantics=("arbitrary",), vmem_limit_bytes=48 * 1024 * 1024),
-    )(slots, doc_tiles, doc_norm, land_rows)
+    )(slots, blocks, doc_tiles, doc_norm, land_rows)
 
 
 def sum_over(values, axis, count):
@@ -117,20 +117,32 @@
     table = land_blocks.reshape(dp_count, land_count, own_blocks, LAND_ACTIVE)
     own_table = lax.dynamic_index_in_dim(table, lax.axis_index("land"), axis=1, keepdims=False)
     own_table = own_table.reshape(dp_count * own_blocks, LAND_ACTIVE)
-    land_rows = lax.all_gather(
-        jnp.concatenate([land_values, coefficients], axis=1).T, "dp", axis=0, tiled=True)
+    own_rows = jnp.concatenate([land_values, coefficients], axis=1).T
+    land_rows = lax.all_gather(own_rows, "dp", axis=0, tiled=True)
+    own = lax.axis_index("dp")
+    rest = jnp.arange(dp_count - 1, dtype=jnp.int32)
+    rest = rest + (rest >= own).astype(jnp.int32)
     doc_tiles = doc_values.reshape(doc_count, DOC_BLOCK, ACTIVE, TERM_BLOCK).transpose(0, 2, 1, 3)
     doc_tiles = jnp.pad(doc_tiles, ((0, 0), (0, 1), (0, 0), (0, 0)))
     doc_tiles = doc_tiles.reshape(doc_count * (ACTIVE + 1), DOC_BLOCK, TERM_BLOCK)
-    slots = match_table(doc_blocks, own_table)
-    tile_high, tile_low, fitted = forward(
-        slots, doc_tiles, (2.0 * sharpness) * doc_norm.reshape(doc_rows, 1), land_rows, targets)
+    doc_norm = (2.0 * sharpness) * doc_norm.reshape(doc_rows, 1)
+    first_high, first_low, fitted_first = forward(
+        match_table(doc_blocks, own_table[own][None]), doc_tiles, doc_norm, own_rows, targets,
+        jnp.zeros((1,), jnp.int32))
+    rest_high, rest_low, fitted = forward(
+        match_table(doc_blocks, own_table[rest]), doc_tiles, doc_norm, land_rows, targets, rest)
+    fitted = fitted + fitted_first
     fitted = all_sum(fitted, "land", land_count)
     fitted_high, fitted_low = split_pair(fitted)
     fitted_pair = jnp.concatenate([fitted_high, fitted_low], axis=1)
+    tile_high = jnp.concatenate([rest_high, first_high], axis=0)
+    tile_low = jnp.concatenate([rest_low, first_low], axis=0)
     summed = jnp.einsum("qnl,nt->qlt", tile_high, fitted_pair, preferred_element_type=jnp.float32)
     summed = summed + jnp.einsum("qnl,nt->qlt", tile_low, fitted_pair, preferred_element_type=jnp.float32)
-    summed = (summed[:, :, :targets] + summed[:, :, targets:]).reshape(-1, targets)
+    summed = summed[:, :, :targets] + summed[:, :, targets:]
+    index = jnp.arange(dp_count, dtype=jnp.int32)
+    order = jnp.where(index == own, dp_count - 1, index - (index > own).astype(jnp.int32))
+    summed = summed[order].reshape(-1, targets)
     result = sum_over(summed, "dp", dp_count)
     return result / total_docs
 

time: 138 us -> 137 us (level)
  blocking collectives: 44.8 us -> 32.5 us
  local copies, waits for them, and re-layouts: 10.8 us -> 20.1 us
  waiting for transfers between devices: 32.4 us -> 28.4 us
  starting transfers between devices: 0.01 us -> 3.82 us
    all_to_all x1 -> x0, blocking collectives: 13.4 us -> none  [all_sum(): return lax.all_to_all(spread, axis, 0, 0, tiled=False).reshape(values.shape)]
    all_gather x1, waiting for transfers between devices: 32.4 us -> 19.7 us  [on_device(): land_rows = lax.all_gather(own_rows, 'dp', axis=0, tiled=True)]
    all_to_all x0 -> x1, waiting for transfers between devices: none -> 8.61 us  [all_sum(): return lax.all_to_all(spread, axis, 0, 0, tiled=False).reshape(values.shape)]
    unnamed x13 -> x27, local copies, waits for them, and re-layouts: 4.98 us -> 9.36 us
    all_to_all x0 -> x1, starting transfers between devices: none -> 3.82 us  [all_sum(): return lax.all_to_all(spread, axis, 0, 0, tiled=False).reshape(values.shape)]
    reduce_sum x1, other arithmetic: 2.57 us -> 0.68 us  [on_device(): jnp.sum(jnp.square(doc_values.astype(jnp.float32)), axis=1) + 1e-06]
    pad x1, local copies, waits for them, and re-layouts: 0.53 us -> 2.41 us  [on_device(): doc_tiles = jnp.pad(doc_tiles, ((0, 0), (0, 1), (0, 0), (0, 0)))]
    reshape x1, local copies, waits for them, and re-layouts: 0.88 us -> 2.55 us  [on_device(): doc_values.reshape(doc_count, DOC_BLOCK, ACTIVE, TERM_BLOCK)]
  transfers between devices with their start and end apart: 1 -> 2, of which waited for: 1 -> 2; matrix products, arithmetic and copies ran while one was open for 7% -> 12% of each run, Pallas kernels for 0% -> 1%
where the time goes in v12:
time: 137 us; the launch traced here: 136 us
  blocking collectives  32.5 us (24%)
  waiting for transfers between devices  28.4 us (21%)
  Pallas kernels  26.2 us (19%)
  local copies, waits for them, and re-layouts  20.1 us (15%)
  between operations  13.6 us (10%)
  other arithmetic  6.19 us (5%)
  matrix products  5.41 us (4%)
  starting transfers between devices  3.82 us (3%)
    all_to_all x2, blocking collectives, sum_over(): pieces = lax.all_to_all(pieces, axis, 0, 0, tiled=False)  32.5 us
    pallas_call x2, Pallas kernels, forward(): pl.pallas_call(forward_kernel, grid_spec=grid_spec, out_shape=[jax.ShapeD...  26.2 us
    all_gather x1, waiting for transfers between devices, on_device(): land_rows = lax.all_gather(own_rows, 'dp', axis=0, tiled=True)  19.7 us
    unnamed x27, local copies, waits for them, and re-layouts  9.36 us
    all_to_all x1, waiting for transfers between devices, all_sum(): return lax.all_to_all(spread, axis, 0, 0, tiled=False).reshape(values.shape)  8.61 us
    dot_general x1, matrix products, on_device(): jnp.einsum('qnl,nt->qlt', tile_high, fitted_pair, preferred_element_type=...  4.42 us
    all_to_all x1, starting transfers between devices, all_sum(): return lax.all_to_all(spread, axis, 0, 0, tiled=False).reshape(values.shape)  3.82 us
  transfers between devices with their start and end apart: 2, of which 2 were waited for; matrix products, arithmetic and copies ran while one was open for 12% of the time, Pallas kernels for 1%

profile of v12, /device:TPU:1, one launch (start us, length us, event | category | flops | bytes accessed | tf_op | source)
XLA Modules:
  0.0 136.3 jit_solution(16006286260744024926)
XLA Ops:
  6.5 1.1 copy.49
  7.7 1.5 %maximum_bitcast_fusion.1.land_ref = bf16[1088,128]{1,0:T(8,128)(2,1)} fusion(bf16[128,64]{0,1:T(8,128)(2,1)} %param.9, bf16[128,1024]{0,1:T(8,128)(2,1)S(1)} %copy.49), kind=kLoop, calls=%fused_computation.18 | loop fusion | flops 557056 | bytes 557056 | tf_op jit(solution)/shard_map/transpose | solution.py:120
  9.1 0.8 reshape.117
  9.9 0.8 copy.44
  11.0 0.8 compare_reduce_fusion.3
  11.8 1.3 compare_reduce_fusion.2
  13.3 2.9 %copy.59 = bf16[192,8,8,128]{3,2,1,0:T(8,128)(2,1)S(1)} copy(bf16[192,8,8,128]{3,1,2,0:T(8,128)(2,1)} %bitcast.27) | data formatting | bytes 6291456
  16.2 2.6 %copy.61 = bf16[12,128,8,128]{3,1,2,0:T(8,128)(2,1)} copy(bf16[12,128,8,128]{3,2,1,0:T(8,128)(2,1)S(1)} %bitcast.29) | data formatting | bytes 6291456 | tf_op jit(solution)/shard_map/reshape | solution.py:125
  18.7 0.7 multiply_reduce_fusion
  19.4 1.2 mul.11.dn_ref
  20.9 0.6 gather_fusion
  21.7 0.8 compare_reduce_fusion
  22.8 2.4 %pad.4 = bf16[12,9,128,128]{3,2,1,0:T(8,128)(2,1)S(1)} pad(bf16[12,8,128,128]{3,2,1,0:T(8,128)(2,1)} %bitcast.28, bf16[]{:T(256)} %constant.61.clone.1), padding=0_0x0_1x0_0x0_0 | pad | bytes 6684674 | tf_op jit(solution)/shard_map/jit(_pad)/pad | solution.py:126
  25.3 1.0 copy-done.2
  26.2 2.0 %shard_map.56 = (bf16[1,1536,128]{2,1,0:T(8,128)(2,1)S(1)}, bf16[1,1536,128]{2,1,0:T(8,128)(2,1)S(1)}, f32[1536,64]{1,0:T(8,128)S(1)}) custom-call(s32[96]{0:T(128)S(1)} %reshape.122.slot_ref, s32[1]{0:T(128)} %constant.67.clone.1.block_ref, bf16[108,128,128]{2,1,0:T(8,128)(2,1)S(1)} %bitcast.25, f32[1536,1]{1,0:T(8,128)S(1)} %copy-done, ...), custom_call_target="tpu_custom_call" | custom-call | tf_op jit(solution)/shard_map/pallas_call | solution.py:83
  28.3 0.9 copy-done.3
  29.2 0.7 copy-done.5
  29.9 0.8 copy-done.7
  30.7 19.7 %all-gather.2.cloned.1.call-done.land_ref = bf16[17408,128]{1,0:T(8,128)(2,1)} async-done(((bf16[1088,128]{1,0:T(8,128)(2,1)}), bf16[17408,128]{1,0:T(8,128)(2,1)}) %all-gather.2.cloned.1.call-update) | async-done | bytes 4456464 | tf_op jit(solution)/shard_map/all_gather | solution.py:121
  50.4 1.1 copy-done.1
  51.5 24.2 %shard_map.55 = (bf16[15,1536,128]{2,1,0:T(8,128)(2,1)}, bf16[15,1536,128]{2,1,0:T(8,128)(2,1)}, f32[1536,64]{1,0:T(8,128)S(1)}) custom-call(s32[1440]{0:T(1024)S(1)} %reshape.119.slot_ref, s32[15]{0:T(128)S(1)} %fusion.12.block_ref, bf16[108,128,128]{2,1,0:T(8,128)(2,1)S(1)} %bitcast.26, f32[1536,1]{1,0:T(8,128)S(1)} %copy-done.1, ...), custom_call_target="tpu_custom_call" | custom-call | tf_op jit(solution)/shard_map/pallas_call | solution.py:83
  75.8 0.3 copy.53
  76.1 16.2 %all_to_all.15 = f32[8,192,64]{1,2,0:T(8,128)S(1)} all-to-all(f32[8,192,64]{1,2,0:T(8,128)S(1)} %copy.53), channel_id=1, replica_groups=mesh['dp'=16,'land'=8] {'land'}, dimensions={0} | all-to-all | bytes 786432 | tf_op jit(solution)/shard_map/all_to_all | solution.py:98
  92.4 0.8 broadcast_in_dim.25
  93.2 3.8 %all-to-all-start.1 = ((f32[8,192,64]{1,2,0:T(8,128)}), f32[8,192,64]{1,2,0:T(8,128)S(1)}, u32[]{:S(2)}, u32[]{:S(2)}) async-start(f32[8,192,64]{1,2,0:T(8,128)} %broadcast_in_dim.25), calls=%async_computation.1 | async-start | bytes 1048576 | tf_op jit(solution)/shard_map/all_to_all | solution.py:105
  97.1 8.6 %all-to-all-done.1 = f32[8,192,64]{1,2,0:T(8,128)S(1)} async-done(((f32[8,192,64]{1,2,0:T(8,128)}), f32[8,192,64]{1,2,0:T(8,128)S(1)}, u32[]{:S(2)}, u32[]{:S(2)}) %all-to-all-start.1) | async-done | bytes 393248 | tf_op jit(solution)/shard_map/all_to_all | solution.py:105
  105.7 0.3 copy.56
  106.3 4.4 %fusion = f32[16,128,128]{1,2,0:T(8,128)S(1)} fusion(bf16[1,1536,128]{2,1,0:T(8,128)(2,1)S(1)} %copy-done.8, bf16[15,1536,128]{2,1,0:T(8,128)(2,1)} %get-tuple-element.14, bf16[1536,64]{0,1:T(8,128)(2,1)S(1)} %subtract_convert_fusion, bf16[1536,64]{0,1:T(8,128)(2,1)S(1)} %convert_element_type.39), kind=kOutput, calls=%fused_computation.2 | convolution fusion | flops 818675712 | bytes 7733248 | tf_op jit(solution)/shard_map/qnl,nt->qlt/dot_general | solution.py:140
  110.8 1.0 fusion.8
  111.9 0.6 gather_fusion.1
  112.5 16.3 %all_to_all.16 = f32[16,128,64]{1,2,0:T(8,128)S(1)} all-to-all(f32[16,128,64]{1,2,0:T(8,128)S(1)} %gather_fusion.1), channel_id=1, replica_groups=mesh['dp'=16,'land'=8] {'dp'}, dimensions={0} | all-to-all | bytes 1048576 | tf_op jit(solution)/shard_map/all_to_all | solution.py:98
  128.8 0.6 broadcast_multiply_fusion
  (46 shorter events, 1.9 us)
Async XLA Ops:
  6.5 43.9 %all-gather.2.cloned.1.call-start = ((), (), s32[]{:S(2)}) async-start(), calls=%async_computation.3 | async-start | bytes 4734976 | tf_op jit(solution)/shard_map/all_gather | solution.py:121
  13.3 5.4 %copy-start.9 = (bf16[1536,1024]{1,0:T(8,128)(2,1)S(1)}, bf16[1536,1024]{1,0:T(8,128)(2,1)}, u32[]{:S(2)}) copy-start(bf16[1536,1024]{1,0:T(8,128)(2,1)} %param.5) | copy-start | bytes 9437188
  22.8 2.4 %copy-start = (f32[1536,1]{1,0:T(8,128)S(1)}, f32[1536,1]{1,0:T(8,128)}, u32[]{:S(2)}) copy-start(f32[1536,1]{1,0:T(8,128)} %mul.11.dn_ref) | copy-start | bytes 18436
  25.2 1.0 copy-start.2
  28.3 0.9 copy-start.3
  29.2 0.8 copy-start.5
  29.9 0.8 copy-start.7
  50.4 1.1 copy-start.1
  51.5 24.2 %copy-start.4 = (f32[1536,64]{1,0:T(8,128)S(1)}, f32[1536,64]{1,0:T(8,128)}, u32[]{:S(2)}) copy-start(f32[1536,64]{1,0:T(8,128)} %copy-done.3) | copy-start | bytes 1179652
  75.7 30.6 %copy-start.8 = (bf16[1,1536,128]{2,1,0:T(8,128)(2,1)S(1)}, bf16[1,1536,128]{2,1,0:T(8,128)(2,1)}, u32[]{:S(2)}) copy-start(bf16[1,1536,128]{2,1,0:T(8,128)(2,1)} %copy-done.7) | copy-start | bytes 1179652
  93.2 12.5 %all-to-all-start.1 = ((f32[8,192,64]{1,2,0:T(8,128)}), f32[8,192,64]{1,2,0:T(8,128)S(1)}, u32[]{:S(2)}, u32[]{:S(2)}) async-start(f32[8,192,64]{1,2,0:T(8,128)} %broadcast_in_dim.25), calls=%async_computation.1 | async-start | bytes 1048576 | tf_op jit(solution)/shard_map/all_to_all | solution.py:105
  106.2 4.5 %slice-start = ((s8[5898240]{0:T(1024)(128)(4,1)}), s8[4194304]{0:T(1024)(128)(4,1)S(1)}, s32[]{:S(2)}) async-start(s8[5898240]{0:T(1024)(128)(4,1)} %bitcast.32), calls=%async_computation.4 | async-start | bytes 8388608
  106.3 4.5 %copy-start.6 = (bf16[1,1536,128]{2,1,0:T(8,128)(2,1)S(1)}, bf16[1,1536,128]{2,1,0:T(8,128)(2,1)}, u32[]{:S(2)}) copy-start(bf16[1,1536,128]{2,1,0:T(8,128)(2,1)} %copy-done.5) | copy-start | bytes 1179652
  106.3 4.5 %slice-start.1 = ((s8[5898240]{0:T(1024)(128)(4,1)}), s8[1703936]{0:T(1024)(128)(4,1)S(1)}, s32[]{:S(2)}) async-start(s8[5898240]{0:T(1024)(128)(4,1)} %bitcast.32), calls=%async_computation.5 | async-start | bytes 3407872
Sparse Core Ops, SparseCore 0:
  9.3 41.0 all-gather.1

commit v13 on v12

--- a/solution.py
+++ b/solution.py
@@ -120,15 +120,18 @@
     own_rows = jnp.concatenate([land_values, coefficients], axis=1).T
     land_rows = lax.all_gather(own_rows, "dp", axis=0, tiled=True)
     own = lax.axis_index("dp")
-    rest = jnp.arange(dp_count - 1, dtype=jnp.int32)
-    rest = rest + (rest >= own).astype(jnp.int32)
+    partner_rows = lax.ppermute(own_rows, "dp", [(i, i ^ 1) for i in range(dp_count)])
+    first_rows = jnp.concatenate([own_rows, partner_rows], axis=0)
+    pair_base = own - own % 2
+    rest = jnp.arange(dp_count - 2, dtype=jnp.int32)
+    rest = rest + 2 * (rest >= pair_base).astype(jnp.int32)
     doc_tiles = doc_values.reshape(doc_count, DOC_BLOCK, ACTIVE, TERM_BLOCK).transpose(0, 2, 1, 3)
     doc_tiles = jnp.pad(doc_tiles, ((0, 0), (0, 1), (0, 0), (0, 0)))
     doc_tiles = doc_tiles.reshape(doc_count * (ACTIVE + 1), DOC_BLOCK, TERM_BLOCK)
     doc_norm = (2.0 * sharpness) * doc_norm.reshape(doc_rows, 1)
     first_high, first_low, fitted_first = forward(
-        match_table(doc_blocks, own_table[own][None]), doc_tiles, doc_norm, own_rows, targets,
-        jnp.zeros((1,), jnp.int32))
+        match_table(doc_blocks, own_table[jnp.stack([own, own ^ 1])]), doc_tiles, doc_norm, first_rows,
+        targets, jnp.arange(2, dtype=jnp.int32))
     rest_high, rest_low, fitted = forward(
         match_table(doc_blocks, own_table[rest]), doc_tiles, doc_norm, land_rows, targets, rest)
     fitted = fitted + fitted_first
@@ -141,7 +144,9 @@
     summed = summed + jnp.einsum("qnl,nt->qlt", tile_low, fitted_pair, preferred_element_type=jnp.float32)
     summed = summed[:, :, :targets] + summed[:, :, targets:]
     index = jnp.arange(dp_count, dtype=jnp.int32)
-    order = jnp.where(index == own, dp_count - 1, index - (index > own).astype(jnp.int32))
+    order = index - 2 * (index > pair_base + 1).astype(jnp.int32)
+    order = jnp.where(index == own, dp_count - 2, order)
+    order = jnp.where(index == (own ^ 1), dp_count - 1, order)
     summed = summed[order].reshape(-1, targets)
     result = sum_over(summed, "dp", dp_count)
     return result / total_docs

time: 137 us -> 136 us (level)
  waiting for transfers between devices: 28.4 us -> 26 us
  local copies, waits for them, and re-layouts: 20.1 us -> 17.9 us
  Pallas kernels: 26.2 us -> 28.2 us
  starting transfers between devices: 3.82 us -> 5.22 us
    dot_general x1, matrix products: 0.99 us -> 4.79 us  [on_device(): jnp.einsum('qnl,nt->qlt', tile_low, fitted_pair, preferred_element_type=j...]
    dot_general x1, matrix products: 4.42 us -> 0.99 us  [on_device(): jnp.einsum('qnl,nt->qlt', tile_high, fitted_pair, preferred_element_type=...]
    all_gather x1, waiting for transfers between devices: 19.7 us -> 17.4 us  [on_device(): land_rows = lax.all_gather(own_rows, 'dp', axis=0, tiled=True)]
    pallas_call x2, Pallas kernels: 26.2 us -> 28.2 us  [forward(): pl.pallas_call(forward_kernel, grid_spec=grid_spec, out_shape=[jax.ShapeD...]
    reshape x1, local copies, waits for them, and re-layouts: 2.55 us -> 0.88 us  [on_device(): doc_values.reshape(doc_count, DOC_BLOCK, ACTIVE, TERM_BLOCK)]
    ppermute x0 -> x1, starting transfers between devices: none -> 1.46 us  [on_device(): lax.ppermute(own_rows, 'dp', [(i, i ^ 1) for i in range(dp_count)])]
    unnamed x27 -> x29, local copies, waits for them, and re-layouts: 9.36 us -> 8.62 us
  transfers between devices with their start and end apart: 2 -> 3, of which waited for: 2 -> 2; matrix products, arithmetic and copies ran while one was open for 12% -> 11% of each run, Pallas kernels for 1% -> 4%
where the time goes in v13:
time: 136 us; the launch traced here: 135 us
  blocking collectives  32.2 us (24%)
  Pallas kernels  28.2 us (21%)
  waiting for transfers between devices  26 us (19%)
  local copies, waits for them, and re-layouts  17.9 us (13%)
  between operations  13.7 us (10%)
  other arithmetic  6.21 us (5%)
  matrix products  5.78 us (4%)
  starting transfers between devices  5.22 us (4%)
    all_to_all x2, blocking collectives, sum_over(): pieces = lax.all_to_all(pieces, axis, 0, 0, tiled=False)  32.2 us
    pallas_call x2, Pallas kernels, forward(): pl.pallas_call(forward_kernel, grid_spec=grid_spec, out_shape=[jax.ShapeD...  28.2 us
    all_gather x1, waiting for transfers between devices, on_device(): land_rows = lax.all_gather(own_rows, 'dp', axis=0, tiled=True)  17.4 us
    unnamed x29, local copies, waits for them, and re-layouts  8.62 us
    all_to_all x1, waiting for transfers between devices, all_sum(): return lax.all_to_all(spread, axis, 0, 0, tiled=False).reshape(values.shape)  8.61 us
    dot_general x1, matrix products, on_device(): jnp.einsum('qnl,nt->qlt', tile_low, fitted_pair, preferred_element_type=j...  4.79 us
    all_to_all x1, starting transfers between devices, all_sum(): return lax.all_to_all(spread, axis, 0, 0, tiled=False).reshape(values.shape)  3.76 us
  transfers between devices with their start and end apart: 3, of which 2 were waited for; matrix products, arithmetic and copies ran while one was open for 11% of the time, Pallas kernels for 4%

profile of v13, /device:TPU:1, one launch (start us, length us, event | category | flops | bytes accessed | tf_op | source)
XLA Modules:
  0.0 135.2 jit_solution(5130562255822408439)
XLA Ops:
  6.5 1.1 copy.45
  7.7 1.4 %maximum_bitcast_fusion.1 = bf16[1088,128]{1,0:T(8,128)(2,1)} fusion(bf16[128,64]{0,1:T(8,128)(2,1)} %param.9, bf16[128,1024]{0,1:T(8,128)(2,1)S(1)} %copy.45), kind=kLoop, calls=%fused_computation.20 | loop fusion | flops 557056 | bytes 557056 | tf_op jit(solution)/shard_map/transpose | solution.py:120
  9.1 1.5 %collective-permute-start = (bf16[1088,128]{1,0:T(8,128)(2,1)}, bf16[1088,128]{1,0:T(8,128)(2,1)}, u32[]{:S(2)}, u32[]{:S(2)}) collective-permute-start(bf16[1088,128]{1,0:T(8,128)(2,1)} %maximum_bitcast_fusion.1), channel_id=1, source_target_pairs={{0,8},{8,0},{16,24},{24,16},{32,40},{40,32},{48,56},{56,48},{64,72... | collective-permute-start | bytes 835592 | tf_op jit(solution)/shard_map/ppermute | solution.py:123
  10.6 0.8 reshape.202
  11.6 0.6 gather_fusion
  12.3 0.8 copy.40
  13.2 0.8 compare_reduce_fusion
  14.4 2.9 %copy.56 = bf16[192,8,8,128]{3,2,1,0:T(8,128)(2,1)S(1)} copy(bf16[192,8,8,128]{3,1,2,0:T(8,128)(2,1)} %bitcast.29) | data formatting | bytes 6291456
  17.3 0.9 copy.58
  18.2 0.7 multiply_reduce_fusion
  18.9 1.2 mul.22.dn_ref
  20.1 0.6 gather_fusion.1
  20.8 0.7 compare_reduce_fusion.2
  21.7 2.3 %pad.4 = bf16[12,9,128,128]{3,2,1,0:T(8,128)(2,1)} pad(bf16[12,8,128,128]{3,2,1,0:T(8,128)(2,1)S(1)} %bitcast.30, bf16[]{:T(256)} %constant.35.clone.1), padding=0_0x0_1x0_0x0_0 | pad | bytes 6684674 | tf_op jit(solution)/shard_map/jit(_pad)/pad | solution.py:129
  24.0 1.3 pad_maximum_fusion.land_ref
  25.3 5.4 %shard_map.56 = (bf16[2,1536,128]{2,1,0:T(8,128)(2,1)S(1)}, bf16[2,1536,128]{2,1,0:T(8,128)(2,1)S(1)}, f32[1536,64]{1,0:T(8,128)S(1)}) custom-call(s32[192]{0:T(256)S(1)} %reshape.207.slot_ref, s32[2]{0:T(128)S(1)} %iota.43.block_ref, bf16[108,128,128]{2,1,0:T(8,128)(2,1)} %bitcast.27, f32[1536,1]{1,0:T(8,128)S(1)} %copy-done.1, ...), custom_call_target="tpu_custom_call" | custom-call | tf_op jit(solution)/shard_map/pallas_call | solution.py:83
  30.7 0.9 copy-done.3
  31.6 0.9 copy-done.5
  32.5 0.9 copy-done.7
  33.4 17.4 %all-gather.2.cloned.1.call-done.land_ref = bf16[17408,128]{1,0:T(8,128)(2,1)} async-done(((bf16[1088,128]{1,0:T(8,128)(2,1)}), bf16[17408,128]{1,0:T(8,128)(2,1)}) %all-gather.2.cloned.1.call-update) | async-done | bytes 4456464 | tf_op jit(solution)/shard_map/all_gather | solution.py:121
  50.8 1.1 copy-done.2
  51.9 22.8 %shard_map.55 = (bf16[14,1536,128]{2,1,0:T(8,128)(2,1)}, bf16[14,1536,128]{2,1,0:T(8,128)(2,1)}, f32[1536,64]{1,0:T(8,128)S(1)}) custom-call(s32[1344]{0:T(1024)S(1)} %reshape.204.slot_ref, s32[14]{0:T(128)S(1)} %fusion.12.block_ref, bf16[108,128,128]{2,1,0:T(8,128)(2,1)S(1)} %bitcast.28, f32[1536,1]{1,0:T(8,128)S(1)} %copy-done.2, ...), custom_call_target="tpu_custom_call" | custom-call | tf_op jit(solution)/shard_map/pallas_call | solution.py:83
  74.8 0.3 copy.50
  75.1 15.9 %all_to_all.15 = f32[8,192,64]{1,2,0:T(8,128)S(1)} all-to-all(f32[8,192,64]{1,2,0:T(8,128)S(1)} %copy.50), channel_id=1, replica_groups=mesh['dp'=16,'land'=8] {'land'}, dimensions={0} | all-to-all | bytes 786432 | tf_op jit(solution)/shard_map/all_to_all | solution.py:98
  91.0 0.9 broadcast_in_dim.30
  91.8 3.8 %all-to-all-start.1 = ((f32[8,192,64]{1,2,0:T(8,128)}), f32[8,192,64]{1,2,0:T(8,128)S(1)}, u32[]{:S(2)}, u32[]{:S(2)}) async-start(f32[8,192,64]{1,2,0:T(8,128)} %broadcast_in_dim.30), calls=%async_computation.1 | async-start | bytes 1048576 | tf_op jit(solution)/shard_map/all_to_all | solution.py:105
  95.6 8.6 %all-to-all-done.1 = f32[8,192,64]{1,2,0:T(8,128)S(1)} async-done(((f32[8,192,64]{1,2,0:T(8,128)}), f32[8,192,64]{1,2,0:T(8,128)S(1)}, u32[]{:S(2)}, u32[]{:S(2)}) %all-to-all-start.1) | async-done | bytes 393248 | tf_op jit(solution)/shard_map/all_to_all | solution.py:105
  104.8 4.8 %fusion.4 = f32[16,128,128]{1,2,0:T(8,128)S(1)} fusion(bf16[2,1536,128]{2,1,0:T(8,128)(2,1)S(1)} %copy-done.8, bf16[14,1536,128]{2,1,0:T(8,128)(2,1)} %get-tuple-element.19, bf16[1536,64]{0,1:T(8,128)(2,1)S(1)} %subtract_convert_fusion, bf16[1536,64]{0,1:T(8,128)(2,1)S(1)} %convert_element_type.17), kind=kOutput, calls=%fused_computation.7 | convolution fusion | flops 818675712 | bytes 7733248 | tf_op jit(solution)/shard_map/qnl,nt->qlt/dot_general | solution.py:144
  109.7 1.0 fusion.8
  110.7 0.6 gather_fusion.2
  111.3 16.4 %all_to_all.16 = f32[16,128,64]{1,2,0:T(8,128)S(1)} all-to-all(f32[16,128,64]{1,2,0:T(8,128)S(1)} %gather_fusion.2), channel_id=1, replica_groups=mesh['dp'=16,'land'=8] {'dp'}, dimensions={0} | all-to-all | bytes 1048576 | tf_op jit(solution)/shard_map/all_to_all | solution.py:98
  127.7 0.6 broadcast_multiply_fusion
  (54 shorter events, 2.0 us)
Async XLA Ops:
  6.5 44.2 %all-gather.2.cloned.1.call-start = ((), (), s32[]{:S(2)}) async-start(), calls=%async_computation.3 | async-start | bytes 4734976 | tf_op jit(solution)/shard_map/all_gather | solution.py:121
  9.1 14.8 %collective-permute-start = (bf16[1088,128]{1,0:T(8,128)(2,1)}, bf16[1088,128]{1,0:T(8,128)(2,1)}, u32[]{:S(2)}, u32[]{:S(2)}) collective-permute-start(bf16[1088,128]{1,0:T(8,128)(2,1)} %maximum_bitcast_fusion.1), channel_id=1, source_target_pairs={{0,8},{8,0},{16,24},{24,16},{32,40},{40,32},{48,56},{56,48},{64,72... | collective-permute-start | bytes 835592 | tf_op jit(solution)/shard_map/ppermute | solution.py:123
  14.4 3.8 %copy-start.9 = (bf16[1536,1024]{1,0:T(8,128)(2,1)S(1)}, bf16[1536,1024]{1,0:T(8,128)(2,1)}, u32[]{:S(2)}) copy-start(bf16[1536,1024]{1,0:T(8,128)(2,1)} %param.5) | copy-start | bytes 9437188
  17.3 3.4 %copy-start.10 = (s32[12,8]{0,1:T(8,128)S(1)}, s32[12,8]{0,1:T(8,128)}, u32[]{:S(2)}) copy-start(s32[12,8]{0,1:T(8,128)} %param.6) | copy-start | bytes 1156
  21.7 3.6 %copy-start.1 = (f32[1536,1]{1,0:T(8,128)S(1)}, f32[1536,1]{1,0:T(8,128)}, u32[]{:S(2)}) copy-start(f32[1536,1]{1,0:T(8,128)} %mul.22.dn_ref) | copy-start | bytes 18436
  24.0 26.8 %copy-start = (bf16[12,9,128,128]{3,2,1,0:T(8,128)(2,1)S(1)}, bf16[12,9,128,128]{3,2,1,0:T(8,128)(2,1)}, u32[]{:S(2)}) copy-start(bf16[12,9,128,128]{3,2,1,0:T(8,128)(2,1)} %pad.4) | copy-start | bytes 10616836
  30.7 0.9 copy-start.3
  31.6 0.9 copy-start.5
  32.5 0.9 copy-start.7
  50.8 1.1 copy-start.2
  51.9 22.8 %copy-start.4 = (f32[1536,64]{1,0:T(8,128)S(1)}, f32[1536,64]{1,0:T(8,128)}, u32[]{:S(2)}) copy-start(f32[1536,64]{1,0:T(8,128)} %copy-done.3) | copy-start | bytes 1179652
  74.7 30.1 %copy-start.8 = (bf16[2,1536,128]{2,1,0:T(8,128)(2,1)S(1)}, bf16[2,1536,128]{2,1,0:T(8,128)(2,1)}, u32[]{:S(2)}) copy-start(bf16[2,1536,128]{2,1,0:T(8,128)(2,1)} %copy-done.7) | copy-start | bytes 2359300
  91.8 12.4 %all-to-all-start.1 = ((f32[8,192,64]{1,2,0:T(8,128)}), f32[8,192,64]{1,2,0:T(8,128)S(1)}, u32[]{:S(2)}, u32[]{:S(2)}) async-start(f32[8,192,64]{1,2,0:T(8,128)} %broadcast_in_dim.30), calls=%async_computation.1 | async-start | bytes 1048576 | tf_op jit(solution)/shard_map/all_to_all | solution.py:105
  104.8 4.9 %slice-start = ((s8[5505024]{0:T(1024)(128)(4,1)}), s8[4194304]{0:T(1024)(128)(4,1)S(1)}, s32[]{:S(2)}) async-start(s8[5505024]{0:T(1024)(128)(4,1)} %bitcast.35), calls=%async_computation.4 | async-start | bytes 8388608
  104.8 4.8 %copy-start.6 = (bf16[2,1536,128]{2,1,0:T(8,128)(2,1)S(1)}, bf16[2,1536,128]{2,1,0:T(8,128)(2,1)}, u32[]{:S(2)}) copy-start(bf16[2,1536,128]{2,1,0:T(8,128)(2,1)} %copy-done.5) | copy-start | bytes 2359300
  104.8 4.8 %slice-start.1 = ((s8[5505024]{0:T(1024)(128)(4,1)}), s8[1310720]{0:T(1024)(128)(4,1)S(1)}, s32[]{:S(2)}) async-start(s8[5505024]{0:T(1024)(128)(4,1)} %bitcast.35), calls=%async_computation.5 | async-start | bytes 2621440
Sparse Core Ops, SparseCore 0:
  9.3 41.4 all-gather.1

commit v14 on v12

--- a/solution.py
+++ b/solution.py
@@ -120,15 +120,20 @@
     own_rows = jnp.concatenate([land_values, coefficients], axis=1).T
     land_rows = lax.all_gather(own_rows, "dp", axis=0, tiled=True)
     own = lax.axis_index("dp")
-    rest = jnp.arange(dp_count - 1, dtype=jnp.int32)
-    rest = rest + (rest >= own).astype(jnp.int32)
+    near = 4
+    first_rows = jnp.concatenate(
+        [own_rows] + [lax.ppermute(own_rows, "dp", [(i, i ^ t) for i in range(dp_count)])
+                      for t in range(1, near)], axis=0)
+    pair_base = own - own % near
+    rest = jnp.arange(dp_count - near, dtype=jnp.int32)
+    rest = rest + near * (rest >= pair_base).astype(jnp.int32)
     doc_tiles = doc_values.reshape(doc_count, DOC_BLOCK, ACTIVE, TERM_BLOCK).transpose(0, 2, 1, 3)
     doc_tiles = jnp.pad(doc_tiles, ((0, 0), (0, 1), (0, 0), (0, 0)))
     doc_tiles = doc_tiles.reshape(doc_count * (ACTIVE + 1), DOC_BLOCK, TERM_BLOCK)
     doc_norm = (2.0 * sharpness) * doc_norm.reshape(doc_rows, 1)
     first_high, first_low, fitted_first = forward(
-        match_table(doc_blocks, own_table[own][None]), doc_tiles, doc_norm, own_rows, targets,
-        jnp.zeros((1,), jnp.int32))
+        match_table(doc_blocks, own_table[jnp.stack([own ^ t for t in range(near)])]), doc_tiles,
+        doc_norm, first_rows, targets, jnp.arange(near, dtype=jnp.int32))
     rest_high, rest_low, fitted = forward(
         match_table(doc_blocks, own_table[rest]), doc_tiles, doc_norm, land_rows, targets, rest)
     fitted = fitted + fitted_first
@@ -141,7 +146,9 @@
     summed = summed + jnp.einsum("qnl,nt->qlt", tile_low, fitted_pair, preferred_element_type=jnp.float32)
     summed = summed[:, :, :targets] + summed[:, :, targets:]
     index = jnp.arange(dp_count, dtype=jnp.int32)
-    order = jnp.where(index == own, dp_count - 1, index - (index > own).astype(jnp.int32))
+    order = index - near * (index >= pair_base + near).astype(jnp.int32)
+    group = (index >= pair_base) & (index < pair_base + near)
+    order = jnp.where(group, dp_count - near + (index ^ own), order)
     summed = summed[order].reshape(-1, targets)
     result = sum_over(summed, "dp", dp_count)
     return result / total_docs

time: 137 us -> 134 us (0.978)
  waiting for transfers between devices: 28.4 us -> 21.8 us
  starting transfers between devices: 3.82 us -> 6.95 us
  other arithmetic: 6.19 us -> 8 us
    all_gather x1, waiting for transfers between devices: 19.7 us -> 12.5 us  [on_device(): land_rows = lax.all_gather(own_rows, 'dp', axis=0, tiled=True)]
    dot_general x1, matrix products: 4.42 us -> 0.99 us  [on_device(): jnp.einsum('qnl,nt->qlt', tile_high, fitted_pair, preferred_element_type=...]
    ppermute x0 -> x3, starting transfers between devices: none -> 3.19 us  [on_device(): lax.ppermute(own_rows, 'dp', [(i, i ^ t) for i in range(dp_count)])]
    dot_general x1, matrix products: 0.99 us -> 3.53 us  [on_device(): jnp.einsum('qnl,nt->qlt', tile_low, fitted_pair, preferred_element_type=j...]
    concatenate x0 -> x1, other arithmetic: none -> 1.69 us  [on_device(): jnp.concatenate([own_rows] + [lax.ppermute(own_rows, 'dp', [(i, i ^ t) fo...]
    reshape x1, local copies, waits for them, and re-layouts: 2.55 us -> 0.88 us  [on_device(): doc_values.reshape(doc_count, DOC_BLOCK, ACTIVE, TERM_BLOCK)]
    unnamed x27 -> x28, local copies, waits for them, and re-layouts: 9.36 us -> 9.73 us
  transfers between devices with their start and end apart: 2 -> 5, of which waited for: 2 -> 3; matrix products, arithmetic and copies ran while one was open for 12% -> 11% of each run, Pallas kernels for 1% -> 6%
where the time goes in v14:
time: 134 us; the launch traced here: 133 us
  blocking collectives  32.5 us (24%)
  Pallas kernels  27 us (20%)
  waiting for transfers between devices  21.8 us (16%)
  local copies, waits for them, and re-layouts  18.9 us (14%)
  between operations  13.7 us (10%)
  other arithmetic  8 us (6%)
  starting transfers between devices  6.95 us (5%)
  matrix products  4.52 us (3%)
    all_to_all x2, blocking collectives, sum_over(): pieces = lax.all_to_all(pieces, axis, 0, 0, tiled=False)  32.5 us
    pallas_call x2, Pallas kernels, forward(): pl.pallas_call(forward_kernel, grid_spec=grid_spec, out_shape=[jax.ShapeD...  27 us
    all_gather x1, waiting for transfers between devices, on_device(): land_rows = lax.all_gather(own_rows, 'dp', axis=0, tiled=True)  12.5 us
    unnamed x28, local copies, waits for them, and re-layouts  9.73 us
    all_to_all x1, waiting for transfers between devices, all_sum(): return lax.all_to_all(spread, axis, 0, 0, tiled=False).reshape(values.shape)  8.61 us
    all_to_all x1, starting transfers between devices, all_sum(): return lax.all_to_all(spread, axis, 0, 0, tiled=False).reshape(values.shape)  3.76 us
    dot_general x1, matrix products, on_device(): jnp.einsum('qnl,nt->qlt', tile_low, fitted_pair, preferred_element_type=j...  3.53 us
    ppermute x3, starting transfers between devices, on_device(): lax.ppermute(own_rows, 'dp', [(i, i ^ t) for i in range(dp_count)])  3.19 us
  transfers between devices with their start and end apart: 5, of which 3 were waited for; matrix products, arithmetic and copies ran while one was open for 11% of the time, Pallas kernels for 6%

profile of v14, /device:TPU:1, one launch (start us, length us, event | category | flops | bytes accessed | tf_op | source)
XLA Modules:
  0.0 133.3 jit_solution(12980193055339233158)
XLA Ops:
  6.5 1.1 copy.43
  7.7 1.4 %maximum_bitcast_fusion.1 = bf16[1088,128]{1,0:T(8,128)(2,1)} fusion(bf16[128,64]{0,1:T(8,128)(2,1)} %param.9, bf16[128,1024]{0,1:T(8,128)(2,1)S(1)} %copy.43), kind=kLoop, calls=%fused_computation.20 | loop fusion | flops 557056 | bytes 557056 | tf_op jit(solution)/shard_map/transpose | solution.py:120
  9.1 1.5 %collective-permute-start = (bf16[1088,128]{1,0:T(8,128)(2,1)}, bf16[1088,128]{1,0:T(8,128)(2,1)}, u32[]{:S(2)}, u32[]{:S(2)}) collective-permute-start(bf16[1088,128]{1,0:T(8,128)(2,1)} %maximum_bitcast_fusion.1), channel_id=1, source_target_pairs={{0,8},{8,0},{16,24},{24,16},{32,40},{40,32},{48,56},{56,48},{64,72... | collective-permute-start | bytes 835592 | tf_op jit(solution)/shard_map/ppermute | solution.py:125
  10.6 1.4 %collective-permute-start.1 = (bf16[1088,128]{1,0:T(8,128)(2,1)}, bf16[1088,128]{1,0:T(8,128)(2,1)}, u32[]{:S(2)}, u32[]{:S(2)}) collective-permute-start(bf16[1088,128]{1,0:T(8,128)(2,1)} %maximum_bitcast_fusion.1), channel_id=1, source_target_pairs={{0,16},{8,24},{16,0},{24,8},{32,48},{40,56},{48,32},{56,40},{64,80... | collective-permute-start | bytes 835592 | tf_op jit(solution)/shard_map/ppermute | solution.py:125
  12.3 0.8 reshape.287
  13.9 0.8 compare_reduce_fusion.1
  14.8 1.5 %compare_reduce_fusion = (pred[12,12,8]{1,2,0:T(8,128)(4,1)}, s32[12,12,8]{1,2,0:T(8,128)S(1)}) fusion(s32[12,8]{1,0:T(8,128)S(1)} %gather_fusion, s32[12,8]{0,1:T(8,128)} %param.6), kind=kLoop, calls=%fused_computation.16 | loop fusion | flops 65664 | bytes 6528 | tf_op jit(solution)/shard_map/match_table/reduce | solution.py:27
  16.5 2.7 %copy.54 = bf16[192,8,8,128]{3,2,1,0:T(8,128)(2,1)S(1)} copy(bf16[192,8,8,128]{3,1,2,0:T(8,128)(2,1)} %bitcast.31) | data formatting | bytes 6291456
  19.2 0.9 copy.56
  20.1 1.0 copy-done.9
  21.1 0.7 multiply_reduce_fusion
  21.8 1.2 mul.22.dn_ref
  23.7 0.8 compare_reduce_fusion.2
  24.7 2.3 %pad.4 = bf16[12,9,128,128]{3,2,1,0:T(8,128)(2,1)} pad(bf16[12,8,128,128]{3,2,1,0:T(8,128)(2,1)S(1)} %bitcast.32, bf16[]{:T(256)} %constant.35.clone.1), padding=0_0x0_1x0_0x0_0 | pad | bytes 6684674 | tf_op jit(solution)/shard_map/jit(_pad)/pad | solution.py:131
  27.0 0.7 collective-permute-done.2
  27.7 1.7 %pad_maximum_fusion.land_ref = bf16[4352,128]{1,0:T(8,128)(2,1)S(1)} fusion(bf16[1088,128]{1,0:T(8,128)(2,1)} %collective-permute-done.2, bf16[1088,128]{1,0:T(8,128)(2,1)} %collective-permute-done.1, bf16[1088,128]{1,0:T(8,128)(2,1)} %collective-permute-done, bf16[1088,128]{1,0:T(8,128)(2,1)} %maximum_bitcast_fusion.1), kind=kLoop, calls=%fused_computation.14 | loop fusion | flops 4456448 | bytes 2228224 | tf_op jit(solution)/shard_map/concatenate | solution.py:124
  29.4 8.2 %shard_map.56 = (bf16[4,1536,128]{2,1,0:T(8,128)(2,1)S(1)}, bf16[4,1536,128]{2,1,0:T(8,128)(2,1)S(1)}, f32[1536,64]{1,0:T(8,128)S(1)}) custom-call(s32[384]{0:T(512)S(1)} %reshape.292.slot_ref, s32[4]{0:T(128)S(1)} %iota.45.block_ref, bf16[108,128,128]{2,1,0:T(8,128)(2,1)} %bitcast.29, f32[1536,1]{1,0:T(8,128)S(1)} %copy-done.1, ...), custom_call_target="tpu_custom_call" | custom-call | tf_op jit(solution)/shard_map/pallas_call | solution.py:83
  37.6 0.9 copy-done.3
  38.5 1.1 copy-done.5
  39.7 1.1 copy-done.7
  40.8 12.5 %all-gather.2.cloned.1.call-done.land_ref = bf16[17408,128]{1,0:T(8,128)(2,1)} async-done(((bf16[1088,128]{1,0:T(8,128)(2,1)}), bf16[17408,128]{1,0:T(8,128)(2,1)}) %all-gather.2.cloned.1.call-update) | async-done | bytes 4456464 | tf_op jit(solution)/shard_map/all_gather | solution.py:121
  53.3 1.1 copy-done.2
  54.4 18.8 %shard_map.55 = (bf16[12,1536,128]{2,1,0:T(8,128)(2,1)}, bf16[12,1536,128]{2,1,0:T(8,128)(2,1)}, f32[1536,64]{1,0:T(8,128)S(1)}) custom-call(s32[1152]{0:T(1024)S(1)} %reshape.289.slot_ref, s32[12]{0:T(128)S(1)} %fusion.12.block_ref, bf16[108,128,128]{2,1,0:T(8,128)(2,1)S(1)} %bitcast.30, f32[1536,1]{1,0:T(8,128)S(1)} %copy-done.2, ...), custom_call_target="tpu_custom_call" | custom-call | tf_op jit(solution)/shard_map/pallas_call | solution.py:83
  73.7 16.3 %all_to_all.15 = f32[8,192,64]{1,2,0:T(8,128)S(1)} all-to-all(f32[8,192,64]{1,2,0:T(8,128)S(1)} %copy.48), channel_id=1, replica_groups=mesh['dp'=16,'land'=8] {'land'}, dimensions={0} | all-to-all | bytes 786432 | tf_op jit(solution)/shard_map/all_to_all | solution.py:98
  90.1 0.8 broadcast_in_dim.12
  90.9 3.8 %all-to-all-start.1 = ((f32[8,192,64]{1,2,0:T(8,128)}), f32[8,192,64]{1,2,0:T(8,128)S(1)}, u32[]{:S(2)}, u32[]{:S(2)}) async-start(f32[8,192,64]{1,2,0:T(8,128)} %broadcast_in_dim.12), calls=%async_computation.1 | async-start | bytes 1048576 | tf_op jit(solution)/shard_map/all_to_all | solution.py:105
  94.7 8.6 %all-to-all-done.1 = f32[8,192,64]{1,2,0:T(8,128)S(1)} async-done(((f32[8,192,64]{1,2,0:T(8,128)}), f32[8,192,64]{1,2,0:T(8,128)S(1)}, u32[]{:S(2)}, u32[]{:S(2)}) %all-to-all-start.1) | async-done | bytes 393248 | tf_op jit(solution)/shard_map/all_to_all | solution.py:105
  103.9 3.5 %fusion.4 = f32[16,128,128]{1,2,0:T(8,128)S(1)} fusion(bf16[4,1536,128]{2,1,0:T(8,128)(2,1)S(1)} %copy-done.8, bf16[12,1536,128]{2,1,0:T(8,128)(2,1)} %get-tuple-element.19, bf16[1536,64]{0,1:T(8,128)(2,1)S(1)} %subtract_convert_fusion, bf16[1536,64]{0,1:T(8,128)(2,1)S(1)} %convert_element_type.17), kind=kOutput, calls=%fused_computation.7 | convolution fusion | flops 818675712 | bytes 7733248 | tf_op jit(solution)/shard_map/qnl,nt->qlt/dot_general | solution.py:146
  108.0 1.0 fusion.8
  109.1 0.6 gather_fusion.2
  109.7 16.1 %all_to_all.16 = f32[16,128,64]{1,2,0:T(8,128)S(1)} all-to-all(f32[16,128,64]{1,2,0:T(8,128)S(1)} %gather_fusion.2), channel_id=1, replica_groups=mesh['dp'=16,'land'=8] {'dp'}, dimensions={0} | all-to-all | bytes 1048576 | tf_op jit(solution)/shard_map/all_to_all | solution.py:98
  125.9 0.6 broadcast_multiply_fusion
  (56 shorter events, 4.1 us)
Async XLA Ops:
  6.5 46.8 %all-gather.2.cloned.1.call-start = ((), (), s32[]{:S(2)}) async-start(), calls=%async_computation.3 | async-start | bytes 4734976 | tf_op jit(solution)/shard_map/all_gather | solution.py:121
  9.1 17.9 %collective-permute-start = (bf16[1088,128]{1,0:T(8,128)(2,1)}, bf16[1088,128]{1,0:T(8,128)(2,1)}, u32[]{:S(2)}, u32[]{:S(2)}) collective-permute-start(bf16[1088,128]{1,0:T(8,128)(2,1)} %maximum_bitcast_fusion.1), channel_id=1, source_target_pairs={{0,8},{8,0},{16,24},{24,16},{32,40},{40,32},{48,56},{56,48},{64,72... | collective-permute-start | bytes 835592 | tf_op jit(solution)/shard_map/ppermute | solution.py:125
  10.6 16.4 %collective-permute-start.1 = (bf16[1088,128]{1,0:T(8,128)(2,1)}, bf16[1088,128]{1,0:T(8,128)(2,1)}, u32[]{:S(2)}, u32[]{:S(2)}) collective-permute-start(bf16[1088,128]{1,0:T(8,128)(2,1)} %maximum_bitcast_fusion.1), channel_id=1, source_target_pairs={{0,16},{8,24},{16,0},{24,8},{32,48},{40,56},{48,32},{56,40},{64,80... | collective-permute-start | bytes 835592 | tf_op jit(solution)/shard_map/ppermute | solution.py:125
  12.0 15.7 %collective-permute-start.2 = (bf16[1088,128]{1,0:T(8,128)(2,1)}, bf16[1088,128]{1,0:T(8,128)(2,1)}, u32[]{:S(2)}, u32[]{:S(2)}) collective-permute-start(bf16[1088,128]{1,0:T(8,128)(2,1)} %maximum_bitcast_fusion.1), channel_id=1, source_target_pairs={{0,24},{8,16},{16,8},{24,0},{32,56},{40,48},{48,40},{56,32},{64,88... | collective-permute-start | bytes 835592 | tf_op jit(solution)/shard_map/ppermute | solution.py:125
  19.2 1.9 %copy-start.9 = (bf16[1536,1024]{1,0:T(8,128)(2,1)S(1)}, bf16[1536,1024]{1,0:T(8,128)(2,1)}, u32[]{:S(2)}) copy-start(bf16[1536,1024]{1,0:T(8,128)(2,1)} %param.5) | copy-start | bytes 9437188
  21.1 2.5 %copy-start.10 = (s32[12,8]{0,1:T(8,128)S(1)}, s32[12,8]{0,1:T(8,128)}, u32[]{:S(2)}) copy-start(s32[12,8]{0,1:T(8,128)} %param.6) | copy-start | bytes 1156
  24.7 4.7 %copy-start.1 = (f32[1536,1]{1,0:T(8,128)S(1)}, f32[1536,1]{1,0:T(8,128)}, u32[]{:S(2)}) copy-start(f32[1536,1]{1,0:T(8,128)} %mul.22.dn_ref) | copy-start | bytes 18436
  27.0 26.3 %copy-start = (bf16[12,9,128,128]{3,2,1,0:T(8,128)(2,1)S(1)}, bf16[12,9,128,128]{3,2,1,0:T(8,128)(2,1)}, u32[]{:S(2)}) copy-start(bf16[12,9,128,128]{3,2,1,0:T(8,128)(2,1)} %pad.4) | copy-start | bytes 10616836
  37.6 0.9 copy-start.3
  38.5 1.1 copy-start.5
  39.7 1.1 copy-start.7
  53.3 1.1 copy-start.2
  54.4 18.8 %copy-start.4 = (f32[1536,64]{1,0:T(8,128)S(1)}, f32[1536,64]{1,0:T(8,128)}, u32[]{:S(2)}) copy-start(f32[1536,64]{1,0:T(8,128)} %copy-done.3) | copy-start | bytes 1179652
  73.7 30.2 %copy-start.8 = (bf16[4,1536,128]{2,1,0:T(8,128)(2,1)S(1)}, bf16[4,1536,128]{2,1,0:T(8,128)(2,1)}, u32[]{:S(2)}) copy-start(bf16[4,1536,128]{2,1,0:T(8,128)(2,1)} %copy-done.7) | copy-start | bytes 4718596
  90.9 12.4 %all-to-all-start.1 = ((f32[8,192,64]{1,2,0:T(8,128)}), f32[8,192,64]{1,2,0:T(8,128)S(1)}, u32[]{:S(2)}, u32[]{:S(2)}) async-start(f32[8,192,64]{1,2,0:T(8,128)} %broadcast_in_dim.12), calls=%async_computation.1 | async-start | bytes 1048576 | tf_op jit(solution)/shard_map/all_to_all | solution.py:105
  103.8 3.6 %slice-start = ((s8[4718592]{0:T(1024)(128)(4,1)}), s8[4194304]{0:T(1024)(128)(4,1)S(1)}, s32[]{:S(2)}) async-start(s8[4718592]{0:T(1024)(128)(4,1)} %bitcast.37), calls=%async_computation.4 | async-start | bytes 8388608
  103.9 4.0 %copy-start.6 = (bf16[4,1536,128]{2,1,0:T(8,128)(2,1)S(1)}, bf16[4,1536,128]{2,1,0:T(8,128)(2,1)}, u32[]{:S(2)}) copy-start(bf16[4,1536,128]{2,1,0:T(8,128)(2,1)} %copy-done.5) | copy-start | bytes 4718596
  103.9 4.1 %slice-start.1 = ((s8[4718592]{0:T(1024)(128)(4,1)}), s8[524288]{0:T(1024)(128)(4,1)S(1)}, s32[]{:S(2)}) async-start(s8[4718592]{0:T(1024)(128)(4,1)} %bitcast.37), calls=%async_computation.5 | async-start | bytes 1048576
Sparse Core Ops, SparseCore 0:
  9.3 44.0 all-gather.1

commit v15 on v14

--- a/solution.py
+++ b/solution.py
@@ -120,7 +120,7 @@
     own_rows = jnp.concatenate([land_values, coefficients], axis=1).T
     land_rows = lax.all_gather(own_rows, "dp", axis=0, tiled=True)
     own = lax.axis_index("dp")
-    near = 4
+    near = 8
     first_rows = jnp.concatenate(
         [own_rows] + [lax.ppermute(own_rows, "dp", [(i, i ^ t) for i in range(dp_count)])
                       for t in range(1, near)], axis=0)

time: 134 us -> 150 us (1.12)
  blocking collectives: 32.5 us -> 45.8 us
  waiting for transfers between devices: 21.8 us -> 19.3 us
  Pallas kernels: 27 us -> 29.4 us
    ppermute x3 -> x7, waiting for transfers between devices: 0.7 us -> 19.3 us  [on_device(): lax.ppermute(own_rows, 'dp', [(i, i ^ t) for i in range(dp_count)])]
    all_gather x1, waiting for transfers between devices: 12.5 us -> 0.01 us  [on_device(): land_rows = lax.all_gather(own_rows, 'dp', axis=0, tiled=True)]
    all_to_all x0 -> x1, blocking collectives: none -> 11.6 us  [all_sum(): return lax.all_to_all(spread, axis, 0, 0, tiled=False).reshape(values.shape)]
    all_to_all x1 -> x0, waiting for transfers between devices: 8.61 us -> none  [all_sum(): return lax.all_to_all(spread, axis, 0, 0, tiled=False).reshape(values.shape)]
    ppermute x3 -> x7, starting transfers between devices: 3.19 us -> 7.48 us  [on_device(): lax.ppermute(own_rows, 'dp', [(i, i ^ t) for i in range(dp_count)])]
    all_to_all x1 -> x0, starting transfers between devices: 3.76 us -> none  [all_sum(): return lax.all_to_all(spread, axis, 0, 0, tiled=False).reshape(values.shape)]
    pallas_call x2, Pallas kernels: 27 us -> 29.4 us  [forward(): pl.pallas_call(forward_kernel, grid_spec=grid_spec, out_shape=[jax.ShapeD...]
    reduce_sum x1, other arithmetic: 0.68 us -> 2.57 us  [on_device(): jnp.sum(jnp.square(doc_values.astype(jnp.float32)), axis=1) + 1e-06]
  transfers between devices with their start and end apart: 5 -> 8, of which waited for: 3 -> 3; matrix products, arithmetic and copies ran while one was open for 11% -> 14% of each run, Pallas kernels for 6% -> 10%
where the time goes in v15:
time: 150 us
  blocking collectives  45.8 us (31%)
  Pallas kernels  29.4 us (20%)
  local copies, waits for them, and re-layouts  19.7 us (13%)
  waiting for transfers between devices  19.3 us (13%)
  between operations  13.7 us (9%)
  other arithmetic  9.41 us (6%)
  starting transfers between devices  7.48 us (5%)
  matrix products  4.96 us (3%)
    all_to_all x2, blocking collectives, sum_over(): pieces = lax.all_to_all(pieces, axis, 0, 0, tiled=False)  34.2 us
    pallas_call x2, Pallas kernels, forward(): pl.pallas_call(forward_kernel, grid_spec=grid_spec, out_shape=[jax.ShapeD...  29.4 us
    ppermute x7, waiting for transfers between devices, on_device(): lax.ppermute(own_rows, 'dp', [(i, i ^ t) for i in range(dp_count)])  19.3 us
    all_to_all x1, blocking collectives, all_sum(): return lax.all_to_all(spread, axis, 0, 0, tiled=False).reshape(values.shape)  11.6 us
    unnamed x20, local copies, waits for them, and re-layouts  11.2 us
    ppermute x7, starting transfers between devices, on_device(): lax.ppermute(own_rows, 'dp', [(i, i ^ t) for i in range(dp_count)])  7.48 us
    dot_general x1, matrix products, on_device(): jnp.einsum('qnl,nt->qlt', tile_low, fitted_pair, preferred_element_type=j...  3.97 us
  transfers between devices with their start and end apart: 8, of which 3 were waited for; matrix products, arithmetic and copies ran while one was open for 14% of the time, Pallas kernels for 10%

profile of v15, /device:TPU:1, one launch (start us, length us, event | category | flops | bytes accessed | tf_op | source)
XLA Modules:
  0.0 149.6 jit_solution(15459837038273864547)
XLA Ops:
  6.5 1.1 copy.39
  7.7 1.4 maximum_bitcast_fusion.1
  9.1 4.1 %collective-permute-start.6 = (bf16[1088,128]{1,0:T(8,128)(2,1)}, bf16[1088,128]{1,0:T(8,128)(2,1)}, u32[]{:S(2)}, u32[]{:S(2)}) collective-permute-start(bf16[1088,128]{1,0:T(8,128)(2,1)} %maximum_bitcast_fusion.1), channel_id=1, source_target_pairs={{0,56},{8,48},{16,40},{24,32},{32,24},{40,16},{48,8},{56,0},{64,12... | collective-permute-start | bytes 835592 | tf_op jit(solution)/shard_map/ppermute | solution.py:125
  13.2 1.3 collective-permute-start.4
  14.6 1.3 collective-permute-start.1
  16.6 0.8 reshape.439
  18.9 0.8 compare_reduce_fusion.3
  19.7 1.4 compare_reduce_fusion
  21.2 1.4 compare_reduce_fusion.2
  22.6 0.7 constant_dynamic-update-slice_fusion.7
  23.3 2.6 %multiply_reduce_fusion = f32[1536]{0:T(1024)S(1)} fusion(bf16[1536,1024]{1,0:T(8,128)(2,1)} %param.5), kind=kLoop, calls=%fused_computation.11 | loop fusion | flops 4717056 | bytes 3151872 | tf_op jit(solution)/shard_map/reduce_sum | solution.py:116
  26.6 2.7 %copy.50 = bf16[192,8,8,128]{3,2,1,0:T(8,128)(2,1)S(1)} copy(bf16[192,8,8,128]{3,1,2,0:T(8,128)(2,1)} %bitcast.37) | data formatting | bytes 6291456
  29.4 0.9 copy.52
  30.3 2.3 %pad.4 = bf16[12,9,128,128]{3,2,1,0:T(8,128)(2,1)} pad(bf16[12,8,128,128]{3,2,1,0:T(8,128)(2,1)S(1)} %bitcast.38, bf16[]{:T(256)} %constant.32.clone.1), padding=0_0x0_1x0_0x0_0 | pad | bytes 6684674 | tf_op jit(solution)/shard_map/jit(_pad)/pad | solution.py:131
  32.6 1.0 constant_dynamic-update-slice_fusion.6
  33.6 7.4 %collective-permute-done.1 = bf16[1088,128]{1,0:T(8,128)(2,1)} collective-permute-done((bf16[1088,128]{1,0:T(8,128)(2,1)}, bf16[1088,128]{1,0:T(8,128)(2,1)}, u32[]{:S(2)}, u32[]{:S(2)}) %collective-permute-start.1) | collective-permute-done | bytes 278560 | tf_op jit(solution)/shard_map/ppermute | solution.py:125
  41.0 1.0 constant_dynamic-update-slice_fusion.5
  42.0 10.8 %collective-permute-done.2 = bf16[1088,128]{1,0:T(8,128)(2,1)S(1)} collective-permute-done((bf16[1088,128]{1,0:T(8,128)(2,1)S(1)}, bf16[1088,128]{1,0:T(8,128)(2,1)S(1)}, u32[]{:S(2)}, u32[]{:S(2)}) %collective-permute-start.2) | collective-permute-done | bytes 278560 | tf_op jit(solution)/shard_map/ppermute | solution.py:125
  52.9 1.0 collective-permute-done.3
  54.0 1.0 constant_dynamic-update-slice_fusion.2
  55.0 1.0 constant_dynamic-update-slice_fusion.1
  56.0 1.0 constant_dynamic-update-slice_fusion.land_ref
  57.0 14.7 %shard_map.56 = (bf16[8,1536,128]{2,1,0:T(8,128)(2,1)}, bf16[8,1536,128]{2,1,0:T(8,128)(2,1)}, f32[1536,64]{1,0:T(8,128)S(1)}) custom-call(s32[768]{0:T(1024)S(1)} %reshape.444.slot_ref, s32[8]{0:T(128)S(1)} %iota.42.block_ref, bf16[108,128,128]{2,1,0:T(8,128)(2,1)} %bitcast.35, f32[1536,1]{1,0:T(8,128)S(1)} %mul.22.dn_ref, ...), custom_call_target="tpu_custom_call" | custom-call | tf_op jit(solution)/shard_map/pallas_call | solution.py:83
  71.7 0.9 copy-done
  72.5 14.7 %shard_map.55 = (bf16[8,1536,128]{2,1,0:T(8,128)(2,1)S(1)}, bf16[8,1536,128]{2,1,0:T(8,128)(2,1)}, f32[1536,64]{1,0:T(8,128)S(1)}) custom-call(s32[768]{0:T(1024)S(1)} %reshape.441.slot_ref, s32[8]{0:T(128)S(1)} %fusion.12.block_ref, bf16[108,128,128]{2,1,0:T(8,128)(2,1)} %bitcast.36, f32[1536,1]{1,0:T(8,128)S(1)} %mul.22.dn_ref, ...), custom_call_target="tpu_custom_call" | custom-call | tf_op jit(solution)/shard_map/pallas_call | solution.py:83
  87.2 1.7 %copy-done.2 = bf16[8,1536,128]{2,1,0:T(8,128)(2,1)} copy-done((bf16[8,1536,128]{2,1,0:T(8,128)(2,1)}, bf16[8,1536,128]{2,1,0:T(8,128)(2,1)S(1)}, u32[]{:S(2)}) %copy-start.2) | copy-done | bytes 3145752
  89.3 15.2 %all_to_all.15 = f32[8,192,64]{1,2,0:T(8,128)S(1)} all-to-all(f32[8,192,64]{1,2,0:T(8,128)S(1)} %copy.44), channel_id=1, replica_groups=mesh['dp'=16,'land'=8] {'land'}, dimensions={0} | all-to-all | bytes 786432 | tf_op jit(solution)/shard_map/all_to_all | solution.py:98
  104.6 11.6 %all_to_all.16 = f32[8,192,64]{1,2,0:T(8,128)S(1)} all-to-all(f32[8,192,64]{1,2,0:T(8,128)S(1)} %broadcast_in_dim.8), channel_id=1, replica_groups=mesh['dp'=16,'land'=8] {'land'}, dimensions={0} | all-to-all | bytes 786432 | tf_op jit(solution)/shard_map/all_to_all | solution.py:105
  116.8 4.0 %fusion.4 = f32[16,128,128]{1,2,0:T(8,128)S(1)} fusion(bf16[8,1536,128]{2,1,0:T(8,128)(2,1)} %get-tuple-element.20, bf16[8,1536,128]{2,1,0:T(8,128)(2,1)} %get-tuple-element.19, bf16[1536,64]{0,1:T(8,128)(2,1)S(1)} %subtract_convert_fusion, bf16[1536,64]{0,1:T(8,128)(2,1)S(1)} %convert_element_type.17), kind=kOutput, calls=%fused_computation.7 | convolution fusion | flops 818675712 | bytes 7733248 | tf_op jit(solution)/shard_map/qnl,nt->qlt/dot_general | solution.py:146
  120.8 0.7 copy-done.5
  121.5 1.0 fusion.8
  123.1 19.0 %all_to_all.17 = f32[16,128,64]{1,2,0:T(8,128)S(1)} all-to-all(f32[16,128,64]{1,2,0:T(8,128)S(1)} %gather_fusion.2), channel_id=1, replica_groups=mesh['dp'=16,'land'=8] {'dp'}, dimensions={0} | all-to-all | bytes 1048576 | tf_op jit(solution)/shard_map/all_to_all | solution.py:98
  (54 shorter events, 5.4 us)
Async XLA Ops:
  6.5 66.0 %all-gather.2.cloned.1.call-start = ((), (), s32[]{:S(2)}) async-start(), calls=%async_computation.3 | async-start | bytes 4734976 | tf_op jit(solution)/shard_map/all_gather | solution.py:121
  9.1 46.8 %collective-permute-start.6 = (bf16[1088,128]{1,0:T(8,128)(2,1)}, bf16[1088,128]{1,0:T(8,128)(2,1)}, u32[]{:S(2)}, u32[]{:S(2)}) collective-permute-start(bf16[1088,128]{1,0:T(8,128)(2,1)} %maximum_bitcast_fusion.1), channel_id=1, source_target_pairs={{0,56},{8,48},{16,40},{24,32},{32,24},{40,16},{48,8},{56,0},{64,12... | collective-permute-start | bytes 835592 | tf_op jit(solution)/shard_map/ppermute | solution.py:125
  13.2 41.7 %collective-permute-start.5 = (bf16[1088,128]{1,0:T(8,128)(2,1)}, bf16[1088,128]{1,0:T(8,128)(2,1)}, u32[]{:S(2)}, u32[]{:S(2)}) collective-permute-start(bf16[1088,128]{1,0:T(8,128)(2,1)} %maximum_bitcast_fusion.1), channel_id=1, source_target_pairs={{0,48},{8,56},{16,32},{24,40},{32,16},{40,24},{48,0},{56,8},{64,11... | collective-permute-start | bytes 835592 | tf_op jit(solution)/shard_map/ppermute | solution.py:125
  13.2 40.7 %collective-permute-start.4 = (bf16[1088,128]{1,0:T(8,128)(2,1)}, bf16[1088,128]{1,0:T(8,128)(2,1)}, u32[]{:S(2)}, u32[]{:S(2)}) collective-permute-start(bf16[1088,128]{1,0:T(8,128)(2,1)} %maximum_bitcast_fusion.1), channel_id=1, source_target_pairs={{0,40},{8,32},{16,56},{24,48},{32,8},{40,0},{48,24},{56,16},{64,10... | collective-permute-start | bytes 835592 | tf_op jit(solution)/shard_map/ppermute | solution.py:125
  14.6 26.4 %collective-permute-start.1 = (bf16[1088,128]{1,0:T(8,128)(2,1)}, bf16[1088,128]{1,0:T(8,128)(2,1)}, u32[]{:S(2)}, u32[]{:S(2)}) collective-permute-start(bf16[1088,128]{1,0:T(8,128)(2,1)} %maximum_bitcast_fusion.1), channel_id=1, source_target_pairs={{0,16},{8,24},{16,0},{24,8},{32,48},{40,56},{48,32},{56,40},{64,80... | collective-permute-start | bytes 835592 | tf_op jit(solution)/shard_map/ppermute | solution.py:125
  15.9 16.7 %collective-permute-start = (bf16[1088,128]{1,0:T(8,128)(2,1)}, bf16[1088,128]{1,0:T(8,128)(2,1)}, u32[]{:S(2)}, u32[]{:S(2)}) collective-permute-start(bf16[1088,128]{1,0:T(8,128)(2,1)} %maximum_bitcast_fusion.1), channel_id=1, source_target_pairs={{0,8},{8,0},{16,24},{24,16},{32,40},{40,32},{48,56},{56,48},{64,72... | collective-permute-start | bytes 835592 | tf_op jit(solution)/shard_map/ppermute | solution.py:125
  30.2 2.3 %copy-start.4 = (bf16[1088,128]{1,0:T(8,128)(2,1)S(1)}, bf16[1088,128]{1,0:T(8,128)(2,1)}, u32[]{:S(2)}) copy-start(bf16[1088,128]{1,0:T(8,128)(2,1)} %maximum_bitcast_fusion.1) | copy-start | bytes 835588
  32.5 20.3 %collective-permute-start.2 = (bf16[1088,128]{1,0:T(8,128)(2,1)S(1)}, bf16[1088,128]{1,0:T(8,128)(2,1)S(1)}, u32[]{:S(2)}, u32[]{:S(2)}) collective-permute-start(bf16[1088,128]{1,0:T(8,128)(2,1)S(1)} %copy-done.4), channel_id=1, source_target_pairs={{0,24},{8,16},{16,8},{24,0},{32,56},{40,48},{48,40},{56,32},{64,88... | collective-permute-start | bytes 835592 | tf_op jit(solution)/shard_map/ppermute | solution.py:125
  41.0 12.9 %collective-permute-start.3 = (bf16[1088,128]{1,0:T(8,128)(2,1)S(1)}, bf16[1088,128]{1,0:T(8,128)(2,1)S(1)}, u32[]{:S(2)}, u32[]{:S(2)}) collective-permute-start(bf16[1088,128]{1,0:T(8,128)(2,1)S(1)} %copy-done.4), channel_id=1, source_target_pairs={{0,32},{8,40},{16,48},{24,56},{32,0},{40,8},{48,16},{56,24},{64,96... | collective-permute-start | bytes 835592 | tf_op jit(solution)/shard_map/ppermute | solution.py:125
  71.7 0.9 copy-start
  72.5 16.4 %copy-start.1 = (f32[1536,64]{1,0:T(8,128)S(1)}, f32[1536,64]{1,0:T(8,128)}, u32[]{:S(2)}) copy-start(f32[1536,64]{1,0:T(8,128)} %copy-done) | copy-start | bytes 1179652
  87.2 1.7 %copy-start.2 = (bf16[8,1536,128]{2,1,0:T(8,128)(2,1)}, bf16[8,1536,128]{2,1,0:T(8,128)(2,1)S(1)}, u32[]{:S(2)}) copy-start(bf16[8,1536,128]{2,1,0:T(8,128)(2,1)S(1)} %get-tuple-element.14) | copy-start | bytes 9437188
  116.8 4.0 %copy-start.3 = (bf16[8,1536,128]{2,1,0:T(8,128)(2,1)S(1)}, bf16[8,1536,128]{2,1,0:T(8,128)(2,1)}, u32[]{:S(2)}) copy-start(bf16[8,1536,128]{2,1,0:T(8,128)(2,1)} %copy-done.2) | copy-start | bytes 9437188
  116.8 4.7 %copy-start.5 = (bf16[8,1536,128]{2,1,0:T(8,128)(2,1)S(1)}, bf16[8,1536,128]{2,1,0:T(8,128)(2,1)}, u32[]{:S(2)}) copy-start(bf16[8,1536,128]{2,1,0:T(8,128)(2,1)} %get-tuple-element.16) | copy-start | bytes 9437188
Sparse Core Ops, SparseCore 0:
  9.2 54.4 all-gather.1

commit v16 on v14

--- a/solution.py
+++ b/solution.py
@@ -140,11 +140,12 @@
     fitted = all_sum(fitted, "land", land_count)
     fitted_high, fitted_low = split_pair(fitted)
     fitted_pair = jnp.concatenate([fitted_high, fitted_low], axis=1)
-    tile_high = jnp.concatenate([rest_high, first_high], axis=0)
-    tile_low = jnp.concatenate([rest_low, first_low], axis=0)
-    summed = jnp.einsum("qnl,nt->qlt", tile_high, fitted_pair, preferred_element_type=jnp.float32)
-    summed = summed + jnp.einsum("qnl,nt->qlt", tile_low, fitted_pair, preferred_element_type=jnp.float32)
-    summed = summed[:, :, :targets] + summed[:, :, targets:]
+    parts = []
+    for tile_high, tile_low in ((rest_high, rest_low), (first_high, first_low)):
+        part = jnp.einsum("qnl,nt->qlt", tile_high, fitted_pair, preferred_element_type=jnp.float32)
+        part = part + jnp.einsum("qnl,nt->qlt", tile_low, fitted_pair, preferred_element_type=jnp.float32)
+        parts.append(part[:, :, :targets] + part[:, :, targets:])
+    summed = jnp.concatenate(parts, axis=0)
     index = jnp.arange(dp_count, dtype=jnp.int32)
     order = index - near * (index >= pair_base + near).astype(jnp.int32)
     group = (index >= pair_base) & (index < pair_base + near)

time: 134 us -> 135 us (level)
    dot_general x1 -> x2, matrix products: 0.99 us -> 3.69 us  [on_device(): jnp.einsum('qnl,nt->qlt', tile_high, fitted_pair, preferred_element_type=...]
    dot_general x1 -> x2, matrix products: 3.53 us -> 1.16 us  [on_device(): jnp.einsum('qnl,nt->qlt', tile_low, fitted_pair, preferred_element_type=j...]
where the time goes in v16:
time: 135 us; the launch traced here: 134 us
  blocking collectives  32.4 us (24%)
  Pallas kernels  27.4 us (20%)
  waiting for transfers between devices  22.1 us (16%)
  local copies, waits for them, and re-layouts  19.6 us (15%)
  between operations  13.7 us (10%)
  other arithmetic  7.57 us (6%)
  starting transfers between devices  6.95 us (5%)
  matrix products  4.85 us (4%)
    all_to_all x2, blocking collectives, sum_over(): pieces = lax.all_to_all(pieces, axis, 0, 0, tiled=False)  32.4 us
    pallas_call x2, Pallas kernels, forward(): pl.pallas_call(forward_kernel, grid_spec=grid_spec, out_shape=[jax.ShapeD...  27.4 us
    all_gather x1, waiting for transfers between devices, on_device(): land_rows = lax.all_gather(own_rows, 'dp', axis=0, tiled=True)  12.6 us
    unnamed x28, local copies, waits for them, and re-layouts  10.7 us
    all_to_all x1, waiting for transfers between devices, all_sum(): return lax.all_to_all(spread, axis, 0, 0, tiled=False).reshape(values.shape)  8.61 us
    all_to_all x1, starting transfers between devices, all_sum(): return lax.all_to_all(spread, axis, 0, 0, tiled=False).reshape(values.shape)  3.76 us
    dot_general x2, matrix products, on_device(): jnp.einsum('qnl,nt->qlt', tile_high, fitted_pair, preferred_element_type=...  3.69 us
    ppermute x3, starting transfers between devices, on_device(): lax.ppermute(own_rows, 'dp', [(i, i ^ t) for i in range(dp_count)])  3.19 us
  transfers between devices with their start and end apart: 5, of which 3 were waited for; matrix products, arithmetic and copies ran while one was open for 11% of the time, Pallas kernels for 6%

profile of v16, /device:TPU:1, one launch (start us, length us, event | category | flops | bytes accessed | tf_op | source)
XLA Modules:
  0.0 134.5 jit_solution(8764599529224830563)
XLA Ops:
  6.5 1.1 copy.43
  7.7 1.4 %maximum_bitcast_fusion.1 = bf16[1088,128]{1,0:T(8,128)(2,1)} fusion(bf16[128,64]{0,1:T(8,128)(2,1)} %param.9, bf16[128,1024]{0,1:T(8,128)(2,1)S(1)} %copy.43), kind=kLoop, calls=%fused_computation.14 | loop fusion | flops 557056 | bytes 557056 | tf_op jit(solution)/shard_map/transpose | solution.py:120
  9.1 1.5 %collective-permute-start = (bf16[1088,128]{1,0:T(8,128)(2,1)}, bf16[1088,128]{1,0:T(8,128)(2,1)}, u32[]{:S(2)}, u32[]{:S(2)}) collective-permute-start(bf16[1088,128]{1,0:T(8,128)(2,1)} %maximum_bitcast_fusion.1), channel_id=1, source_target_pairs={{0,8},{8,0},{16,24},{24,16},{32,40},{40,32},{48,56},{56,48},{64,72... | collective-permute-start | bytes 835592 | tf_op jit(solution)/shard_map/ppermute | solution.py:125
  10.6 1.4 %collective-permute-start.1 = (bf16[1088,128]{1,0:T(8,128)(2,1)}, bf16[1088,128]{1,0:T(8,128)(2,1)}, u32[]{:S(2)}, u32[]{:S(2)}) collective-permute-start(bf16[1088,128]{1,0:T(8,128)(2,1)} %maximum_bitcast_fusion.1), channel_id=1, source_target_pairs={{0,16},{8,24},{16,0},{24,8},{32,48},{40,56},{48,32},{56,40},{64,80... | collective-permute-start | bytes 835592 | tf_op jit(solution)/shard_map/ppermute | solution.py:125
  12.3 0.8 reshape.287
  13.9 0.8 compare_reduce_fusion.1
  14.8 1.5 %compare_reduce_fusion = (pred[12,12,8]{1,2,0:T(8,128)(4,1)}, s32[12,12,8]{1,2,0:T(8,128)S(1)}) fusion(s32[12,8]{1,0:T(8,128)S(1)} %gather_fusion, s32[12,8]{0,1:T(8,128)} %param.6), kind=kLoop, calls=%fused_computation.9 | loop fusion | flops 65664 | bytes 6528 | tf_op jit(solution)/shard_map/match_table/reduce | solution.py:27
  16.5 2.7 %copy.54 = bf16[192,8,8,128]{3,2,1,0:T(8,128)(2,1)S(1)} copy(bf16[192,8,8,128]{3,1,2,0:T(8,128)(2,1)} %bitcast.37) | data formatting | bytes 6291456
  19.2 0.9 copy.56
  20.1 1.0 copy-done.9
  21.1 0.7 multiply_reduce_fusion
  21.8 1.2 mul.22.dn_ref
  23.7 0.8 compare_reduce_fusion.2
  24.7 2.1 %pad.4 = bf16[12,9,128,128]{3,2,1,0:T(8,128)(2,1)} pad(bf16[12,8,128,128]{3,2,1,0:T(8,128)(2,1)S(1)} %bitcast.38, bf16[]{:T(256)} %constant.35.clone.1), padding=0_0x0_1x0_0x0_0 | pad | bytes 6684674 | tf_op jit(solution)/shard_map/jit(_pad)/pad | solution.py:131
  26.8 0.9 collective-permute-done.2
  27.7 1.2 pad_maximum_fusion.land_ref
  28.9 8.6 %shard_map.56 = (bf16[4,1536,128]{2,1,0:T(8,128)(2,1)S(1)}, bf16[4,1536,128]{2,1,0:T(8,128)(2,1)S(1)}, f32[1536,64]{1,0:T(8,128)S(1)}) custom-call(s32[384]{0:T(512)S(1)} %reshape.292.slot_ref, s32[4]{0:T(128)S(1)} %iota.45.block_ref, bf16[108,128,128]{2,1,0:T(8,128)(2,1)} %bitcast.35, f32[1536,1]{1,0:T(8,128)S(1)} %copy-done.1, ...), custom_call_target="tpu_custom_call" | custom-call | tf_op jit(solution)/shard_map/pallas_call | solution.py:83
  37.6 1.1 copy-done.3
  38.7 1.1 copy-done.5
  39.8 0.9 copy-done.7
  40.7 12.6 %all-gather.2.cloned.1.call-done.land_ref = bf16[17408,128]{1,0:T(8,128)(2,1)} async-done(((bf16[1088,128]{1,0:T(8,128)(2,1)}), bf16[17408,128]{1,0:T(8,128)(2,1)}) %all-gather.2.cloned.1.call-update) | async-done | bytes 4456464 | tf_op jit(solution)/shard_map/all_gather | solution.py:121
  53.3 1.1 copy-done.2
  54.4 18.8 %shard_map.55 = (bf16[12,1536,128]{2,1,0:T(8,128)(2,1)}, bf16[12,1536,128]{2,1,0:T(8,128)(2,1)}, f32[1536,64]{1,0:T(8,128)S(1)}) custom-call(s32[1152]{0:T(1024)S(1)} %reshape.289.slot_ref, s32[12]{0:T(128)S(1)} %fusion.1.block_ref, bf16[108,128,128]{2,1,0:T(8,128)(2,1)S(1)} %bitcast.36, f32[1536,1]{1,0:T(8,128)S(1)} %copy-done.2, ...), custom_call_target="tpu_custom_call" | custom-call | tf_op jit(solution)/shard_map/pallas_call | solution.py:83
  73.7 16.3 %all_to_all.15 = f32[8,192,64]{1,2,0:T(8,128)S(1)} all-to-all(f32[8,192,64]{1,2,0:T(8,128)S(1)} %copy.48), channel_id=1, replica_groups=mesh['dp'=16,'land'=8] {'land'}, dimensions={0} | all-to-all | bytes 786432 | tf_op jit(solution)/shard_map/all_to_all | solution.py:98
  90.0 0.8 broadcast_in_dim.12
  90.8 3.8 %all-to-all-start.1 = ((f32[8,192,64]{1,2,0:T(8,128)}), f32[8,192,64]{1,2,0:T(8,128)S(1)}, u32[]{:S(2)}, u32[]{:S(2)}) async-start(f32[8,192,64]{1,2,0:T(8,128)} %broadcast_in_dim.12), calls=%async_computation.1 | async-start | bytes 1048576 | tf_op jit(solution)/shard_map/all_to_all | solution.py:105
  94.6 8.6 %all-to-all-done.1 = f32[8,192,64]{1,2,0:T(8,128)S(1)} async-done(((f32[8,192,64]{1,2,0:T(8,128)}), f32[8,192,64]{1,2,0:T(8,128)S(1)}, u32[]{:S(2)}, u32[]{:S(2)}) %all-to-all-start.1) | async-done | bytes 393248 | tf_op jit(solution)/shard_map/all_to_all | solution.py:105
  103.8 3.3 %fusion.6 = f32[12,128,128]{1,2,0:T(8,128)S(1)} fusion(bf16[12,1536,128]{2,1,0:T(8,128)(2,1)} %get-tuple-element.14, bf16[1536,64]{0,1:T(8,128)(2,1)S(1)} %subtract_convert_fusion, bf16[1536,64]{0,1:T(8,128)(2,1)S(1)} %convert_element_type.17), kind=kOutput, calls=%fused_computation.39 | convolution fusion | flops 604766208 | bytes 5898240 | tf_op jit(solution)/shard_map/qnl,nt->qlt/dot_general | solution.py:145
  107.5 0.8 convolution_add_fusion
  110.3 0.6 gather_fusion.2
  110.9 16.1 %all_to_all.16 = f32[16,128,64]{1,2,0:T(8,128)S(1)} all-to-all(f32[16,128,64]{1,2,0:T(8,128)S(1)} %gather_fusion.2), channel_id=1, replica_groups=mesh['dp'=16,'land'=8] {'dp'}, dimensions={0} | all-to-all | bytes 1048576 | tf_op jit(solution)/shard_map/all_to_all | solution.py:98
  127.0 0.6 broadcast_multiply_fusion
  (59 shorter events, 5.8 us)
Async XLA Ops:
  6.5 46.8 %all-gather.2.cloned.1.call-start = ((), (), s32[]{:S(2)}) async-start(), calls=%async_computation.3 | async-start | bytes 4734976 | tf_op jit(solution)/shard_map/all_gather | solution.py:121
  9.1 17.7 %collective-permute-start = (bf16[1088,128]{1,0:T(8,128)(2,1)}, bf16[1088,128]{1,0:T(8,128)(2,1)}, u32[]{:S(2)}, u32[]{:S(2)}) collective-permute-start(bf16[1088,128]{1,0:T(8,128)(2,1)} %maximum_bitcast_fusion.1), channel_id=1, source_target_pairs={{0,8},{8,0},{16,24},{24,16},{32,40},{40,32},{48,56},{56,48},{64,72... | collective-permute-start | bytes 835592 | tf_op jit(solution)/shard_map/ppermute | solution.py:125
  10.6 16.2 %collective-permute-start.1 = (bf16[1088,128]{1,0:T(8,128)(2,1)}, bf16[1088,128]{1,0:T(8,128)(2,1)}, u32[]{:S(2)}, u32[]{:S(2)}) collective-permute-start(bf16[1088,128]{1,0:T(8,128)(2,1)} %maximum_bitcast_fusion.1), channel_id=1, source_target_pairs={{0,16},{8,24},{16,0},{24,8},{32,48},{40,56},{48,32},{56,40},{64,80... | collective-permute-start | bytes 835592 | tf_op jit(solution)/shard_map/ppermute | solution.py:125
  12.0 15.7 %collective-permute-start.2 = (bf16[1088,128]{1,0:T(8,128)(2,1)}, bf16[1088,128]{1,0:T(8,128)(2,1)}, u32[]{:S(2)}, u32[]{:S(2)}) collective-permute-start(bf16[1088,128]{1,0:T(8,128)(2,1)} %maximum_bitcast_fusion.1), channel_id=1, source_target_pairs={{0,24},{8,16},{16,8},{24,0},{32,56},{40,48},{48,40},{56,32},{64,88... | collective-permute-start | bytes 835592 | tf_op jit(solution)/shard_map/ppermute | solution.py:125
  19.2 1.9 %copy-start.9 = (bf16[1536,1024]{1,0:T(8,128)(2,1)S(1)}, bf16[1536,1024]{1,0:T(8,128)(2,1)}, u32[]{:S(2)}) copy-start(bf16[1536,1024]{1,0:T(8,128)(2,1)} %param.5) | copy-start | bytes 9437188
  21.1 2.5 %copy-start.12 = (s32[12,8]{0,1:T(8,128)S(1)}, s32[12,8]{0,1:T(8,128)}, u32[]{:S(2)}) copy-start(s32[12,8]{0,1:T(8,128)} %param.6) | copy-start | bytes 1156
  24.7 3.0 %copy-start.11 = (bf16[1088,128]{1,0:T(8,128)(2,1)S(1)}, bf16[1088,128]{1,0:T(8,128)(2,1)}, u32[]{:S(2)}) copy-start(bf16[1088,128]{1,0:T(8,128)(2,1)} %maximum_bitcast_fusion.1) | copy-start | bytes 835588
  26.8 2.1 %copy-start.1 = (f32[1536,1]{1,0:T(8,128)S(1)}, f32[1536,1]{1,0:T(8,128)}, u32[]{:S(2)}) copy-start(f32[1536,1]{1,0:T(8,128)} %mul.22.dn_ref) | copy-start | bytes 18436
  28.9 24.4 %copy-start = (bf16[12,9,128,128]{3,2,1,0:T(8,128)(2,1)S(1)}, bf16[12,9,128,128]{3,2,1,0:T(8,128)(2,1)}, u32[]{:S(2)}) copy-start(bf16[12,9,128,128]{3,2,1,0:T(8,128)(2,1)} %pad.4) | copy-start | bytes 10616836
  37.5 1.1 copy-start.3
  38.7 1.1 copy-start.5
  39.8 0.9 copy-start.7
  53.3 1.1 copy-start.2
  54.4 18.8 %copy-start.8 = (f32[1536,64]{1,0:T(8,128)S(1)}, f32[1536,64]{1,0:T(8,128)}, u32[]{:S(2)}) copy-start(f32[1536,64]{1,0:T(8,128)} %copy-done.7) | copy-start | bytes 1179652
  90.8 12.4 %all-to-all-start.1 = ((f32[8,192,64]{1,2,0:T(8,128)}), f32[8,192,64]{1,2,0:T(8,128)S(1)}, u32[]{:S(2)}, u32[]{:S(2)}) async-start(f32[8,192,64]{1,2,0:T(8,128)} %broadcast_in_dim.12), calls=%async_computation.1 | async-start | bytes 1048576 | tf_op jit(solution)/shard_map/all_to_all | solution.py:105
  103.8 3.8 %copy-start.10 = (bf16[12,1536,128]{2,1,0:T(8,128)(2,1)S(1)}, bf16[12,1536,128]{2,1,0:T(8,128)(2,1)}, u32[]{:S(2)}) copy-start(bf16[12,1536,128]{2,1,0:T(8,128)(2,1)} %get-tuple-element.18) | copy-start | bytes 14155780
  107.5 1.4 %copy-start.6 = (bf16[4,1536,128]{2,1,0:T(8,128)(2,1)S(1)}, bf16[4,1536,128]{2,1,0:T(8,128)(2,1)}, u32[]{:S(2)}) copy-start(bf16[4,1536,128]{2,1,0:T(8,128)(2,1)} %copy-done.5) | copy-start | bytes 4718596
  108.3 1.5 %copy-start.4 = (bf16[4,1536,128]{2,1,0:T(8,128)(2,1)S(1)}, bf16[4,1536,128]{2,1,0:T(8,128)(2,1)}, u32[]{:S(2)}) copy-start(bf16[4,1536,128]{2,1,0:T(8,128)(2,1)} %copy-done.3) | copy-start | bytes 4718596
Sparse Core Ops, SparseCore 0:
  9.3 44.0 all-gather.1
